TPU v7x, 128 devices: a whole 4x4x4 slice. The times are simulated.
128 devices in a mesh: dp: 8 (over z, core), expert: 16 (over x, y).
Axes of the slice: x: 4, y: 4, z: 4, core: 2. Of those that a mesh axis runs over, the one named last changes fastest.
Arguments:
- residual_in: bfloat16 [8192, 2048], P(('dp', 'expert')), may hold values from -40 to 40
- attention_gain: float32 [2048], replicated, may hold values from 0.25 to 1.75
- query_weight: bfloat16 [2048, 2048], P(None, 'expert'), may hold values from -0.125 to 0.125
- key_weight: bfloat16 [2048, 2048], P(None, 'expert'), may hold values from -0.125 to 0.125
- value_weight: bfloat16 [2048, 2048], P(None, 'expert'), may hold values from -0.125 to 0.125
- output_weight: bfloat16 [2048, 2048], P('expert'), may hold values from -0.125 to 0.125
- prompt_keys: bfloat16 [24, 2048, 2048], P('dp', None, 'expert'), may hold values from -220 to 220
- prompt_values: bfloat16 [24, 2048, 2048], P('dp', None, 'expert'), may hold values from -12 to 12
- group_index: int32 [8, 32], P('dp'), may hold values from 0 to 2, never falling along the last dimension, each value on 1 to 16 neighbouring positions
- prompt_length: int32 [24], P('dp'), may hold values from 1 to 2048, 24576 in all
- own_length: int32 [256], P('dp'), may hold values from 1 to 32
- expert_gain: float32 [2048], replicated, may hold values from 0.25 to 1.75
- expert_ids: int32 [8192, 8], P(('dp', 'expert')), may hold values from 0 to 63, all different within a row; in each aligned block of 64 rows (0 to 63, 64 to 127, ...) at most 12 rows name the same one
- expert_mix: float32 [8192, 8], P(('dp', 'expert')), may hold values from 0.02 to 0.3
- gate_weight: bfloat16 [128, 2048, 512], P(('dp', 'expert')), may hold values from -0.125 to 0.125
- up_weight: bfloat16 [128, 2048, 512], P(('dp', 'expert')), may hold values from -0.125 to 0.125
- down_weight: bfloat16 [128, 512, 2048], P(('dp', 'expert')), may hold values from -0.1875 to 0.1875
Outputs:
- attention_update: bfloat16 [8192, 2048], P(('dp', 'expert'))
- expert_update: bfloat16 [8192, 2048], P(('dp', 'expert'))
Inputs may be any that keep to these rules, and one draw needn't show every extreme that they name: `group_index`: each row holds the 32 requests of one index of dp; a group's requests are consecutive, every group has 1 to 16 requests and some group exactly 16. `prompt_length`: some prompt is exactly 2048 long. `expert_ids`: a token's 8 experts differ; among the 64 rows of one device no expert is named more than 12 times, a bound that some block reaches.
All inputs are finite; a program needn't handle non-finite values. No bound on the sum of `prompt_length` on one device may be relied on, other than what follows from the above.
Results may differ from a plain program's by a relative error of at most 0.025.
The roundings to bfloat16 on the way count: a program that leaves them out, or rounds other values in their place, can miss the bound.
Values may be sent and summed in bfloat16 or wider, within the bound.
No kernel may reach another device: no remote copies, remote signals or barrier semaphores. Data moves between devices by JAX's collectives and lax.ppermute only.
A program may use at most 128 MiB of HBM per device.

v0:
```python
import jax
import jax.numpy as jnp
from jax import lax
from jax.sharding import PartitionSpec as P

HD = 128
FF = 1024
TOP = 8
GSIZE = 16
SB = 32


epsilon = 1e-06


def rms_scale(values, gain):
    widened = values.astype(jnp.float32)
    spread = jnp.mean(widened * widened, axis=-1, keepdims=True)
    return (widened * lax.rsqrt(spread + epsilon) * gain).astype(jnp.bfloat16)


def expert_block(block, gate_weight, up_weight, down_weight):
    shape_kept = block.shape
    flat = block.reshape(-1, shape_kept[-1])
    gated = jnp.dot(flat, gate_weight[0], preferred_element_type=jnp.float32)
    lifted = jnp.dot(flat, up_weight[0], preferred_element_type=jnp.float32)
    hidden = (jax.nn.silu(gated) * lifted).astype(jnp.bfloat16)
    produced = jnp.dot(hidden, down_weight[0], preferred_element_type=jnp.float32).astype(
        jnp.bfloat16
    )
    return produced.reshape(shape_kept)


def per_device(
    residual_in,
    attention_gain,
    query_weight,
    key_weight,
    value_weight,
    output_weight,
    prompt_keys,
    prompt_values,
    group_index,
    prompt_length,
    own_length,
    expert_gain,
    expert_ids,
    expert_mix,
    gate_weight,
    up_weight,
    down_weight,
):
    tok_rows, width = residual_in.shape
    local_width = query_weight.shape[1]
    heads_here = local_width // HD
    requests = group_index.shape[1]
    longest = prompt_keys.shape[1]
    groups_here = prompt_keys.shape[0]
    normed = rms_scale(residual_in, attention_gain)
    piece = lax.all_gather(normed, "expert", axis=0, tiled=True)
    query_part = jnp.dot(piece, query_weight, preferred_element_type=jnp.float32).astype(
        jnp.bfloat16
    )
    key_part = jnp.dot(piece, key_weight, preferred_element_type=jnp.float32).astype(jnp.bfloat16)
    value_part = jnp.dot(piece, value_weight, preferred_element_type=jnp.float32).astype(
        jnp.bfloat16
    )
    projected = jnp.concatenate([query_part, key_part, value_part], axis=1)
    layout = (requests, SB, heads_here, HD)
    queries = projected[:, :local_width].reshape(layout)
    new_keys = projected[:, local_width : 2 * local_width].reshape(layout)
    new_values = projected[:, 2 * local_width :].reshape(layout)
    scale = HD ** (-0.5)
    positions = jnp.arange(SB, dtype=jnp.int32)
    own_scores = (
        jnp.einsum("rihd,rjhd->rhij", queries, new_keys, preferred_element_type=jnp.float32) * scale
    )
    own_scores = jnp.where(
        positions[None, None, None, :] < own_length[:, None, None, None], own_scores, -jnp.inf
    )
    member = group_index[0]
    prompt_positions = jnp.arange(longest, dtype=jnp.int32)

    def group_step(group, attended):
        first = jnp.sum((member < group).astype(jnp.int32))
        start = jnp.minimum(first, requests - GSIZE)
        window_queries = lax.dynamic_slice_in_dim(queries, start, GSIZE, 0)
        group_keys = lax.dynamic_index_in_dim(prompt_keys, group, 0, keepdims=False).reshape(
            longest, heads_here, HD
        )
        group_values = lax.dynamic_index_in_dim(prompt_values, group, 0, keepdims=False).reshape(
            longest, heads_here, HD
        )
        scores = (
            jnp.einsum(
                "rihd,jhd->rhij", window_queries, group_keys, preferred_element_type=jnp.float32
            )
            * scale
        )
        limit = lax.dynamic_index_in_dim(prompt_length, group, 0, keepdims=False)
        scores = jnp.where(prompt_positions < limit, scores, -jnp.inf)
        window_own = lax.dynamic_slice_in_dim(own_scores, start, GSIZE, 0)
        highest = jnp.maximum(jnp.max(scores, axis=-1), jnp.max(window_own, axis=-1))
        prompt_weights = jnp.exp(scores - highest[..., None]).astype(jnp.bfloat16)
        own_weights = jnp.exp(window_own - highest[..., None]).astype(jnp.bfloat16)
        window_values = lax.dynamic_slice_in_dim(new_values, start, GSIZE, 0)
        summed = jnp.einsum(
            "rhij,jhd->rihd", prompt_weights, group_values, preferred_element_type=jnp.float32
        )
        summed = summed + jnp.einsum(
            "rhij,rjhd->rihd", own_weights, window_values, preferred_element_type=jnp.float32
        )
        totals = jnp.sum(prompt_weights, axis=-1, dtype=jnp.float32) + jnp.sum(
            own_weights, axis=-1, dtype=jnp.float32
        )
        result = (summed / jnp.transpose(totals, (0, 2, 1))[..., None]).astype(jnp.bfloat16)
        inside = lax.dynamic_slice_in_dim(member, start, GSIZE, 0) == group
        current = lax.dynamic_slice_in_dim(attended, start, GSIZE, 0)
        merged = jnp.where(inside[:, None, None, None], result, current)
        return lax.dynamic_update_slice_in_dim(attended, merged, start, 0)

    attended = lax.fori_loop(0, groups_here, group_step, jnp.zeros(layout, jnp.bfloat16))
    flat_attended = attended.reshape(requests * SB, local_width)
    piece = flat_attended
    attention_update = lax.psum_scatter(
        jnp.dot(piece, output_weight, preferred_element_type=jnp.float32).astype(jnp.bfloat16),
        "expert",
        scatter_dimension=0,
        tiled=True,
    )
    expert_input = rms_scale(
        residual_in.astype(jnp.float32) + attention_update.astype(jnp.float32), expert_gain
    )
    data_groups = lax.axis_size("dp")
    expert_groups = lax.axis_size("expert")
    devices = data_groups * expert_groups
    hidden_split = FF // gate_weight.shape[2]
    experts = devices // hidden_split
    capacity = max(2, tok_rows * TOP * 3 // (2 * experts))
    chosen = expert_ids.reshape(-1)
    routes_here = chosen.shape[0]
    owners = jnp.arange(routes_here, dtype=jnp.int32) // TOP
    matches = (chosen[:, None] == jnp.arange(experts, dtype=jnp.int32)[None, :]).astype(jnp.int32)
    slots = jnp.sum((jnp.cumsum(matches, axis=0) - matches) * matches, axis=1)
    table = (
        jnp.full((experts * capacity,), tok_rows, jnp.int32)
        .at[chosen * capacity + slots]
        .set(owners)
    )
    padded = jnp.concatenate([expert_input, jnp.zeros((1, width), jnp.bfloat16)], axis=0)
    outgoing = jnp.broadcast_to(
        padded[table].reshape(experts, 1, capacity, width), (experts, hidden_split, capacity, width)
    )
    outgoing = outgoing.reshape(devices, capacity, width)
    returned = lax.all_to_all(
        expert_block(
            lax.all_to_all(outgoing, ("dp", "expert"), split_axis=0, concat_axis=0, tiled=True),
            gate_weight,
            up_weight,
            down_weight,
        ),
        ("dp", "expert"),
        split_axis=0,
        concat_axis=0,
        tiled=True,
    )
    pieces = returned.reshape(experts, hidden_split, capacity, width)[chosen, :, slots]
    blended = jnp.sum(pieces.astype(jnp.float32), axis=1) * expert_mix.reshape(-1)[:, None]
    expert_update = jnp.sum(blended.reshape(tok_rows, TOP, width), axis=1).astype(jnp.bfloat16)
    return (attention_update, expert_update)


def solution(mesh):
    in_specs = (
        P(("dp", "expert"), None),
        P(),
        P(None, "expert"),
        P(None, "expert"),
        P(None, "expert"),
        P("expert", None),
        P("dp", None, "expert"),
        P("dp", None, "expert"),
        P("dp", None),
        P("dp"),
        P("dp"),
        P(),
        P(("dp", "expert"), None),
        P(("dp", "expert"), None),
        P(("dp", "expert"), None, None),
        P(("dp", "expert"), None, None),
        P(("dp", "expert"), None, None),
    )
    out_specs = (P(("dp", "expert"), None), P(("dp", "expert"), None))
    return jax.shard_map(
        per_device, mesh=mesh, in_specs=in_specs, out_specs=out_specs, check_vma=False
    )
```

profile of v0, /device:TPU:1, one launch (start us, length us, event | category | flops | bytes accessed | tf_op | source)
XLA Modules:
  0.0 501.5 jit_solution(6749602268431022761)
XLA Ops:
  11.1 53.9 %all-gather.2.cloned.1.call-done = bf16[1024,2048]{1,0:T(8,128)(2,1)} async-done(((bf16[64,2048]{1,0:T(8,128)(2,1)}), bf16[1024,2048]{1,0:T(8,128)(2,1)}) %all-gather.2.cloned.1.call-update) | async-done | bytes 4194320 | tf_op jit(solution)/shard_map/all_gather | solution.py:60
  65.1 3.7 convolution_convert_fusion.4
  71.7 24.7 %while.14 = (s32[]{:T(128)}, bf16[32,32,1,128]{3,1,0,2:T(8,128)(2,1)S(1)}, s32[32]{0:T(128)S(1)}, bf16[3,2048,128]{2,1,0:T(8,128)(2,1)}, s32[3]{0:T(128)S(1)}, /...) while((s32[]{:T(128)}, ...), condition=%wide.region_7.8_spmd.clone, body=%wide.region_1.7_spmd.clone.sunk | while | flops 555074688 | bytes 15133611 | solution.py:122
  77.8 2.1 fusion.92
  82.4 1.9 bitcast_reduce_fusion.2
  86.0 2.1 fusion.92
  94.3 2.1 fusion.92
  96.3 4.2 convolution_convert_fusion.1
  102.6 2.4 scatter_custom_fusion
  105.1 72.2 %reduce-scatter.2.cloned.1.call-done = bf16[64,2048]{1,0:T(8,128)(2,1)} async-done(((bf16[1024,2048]{1,0:T(8,128)(2,1)}), bf16[64,2048]{1,0:T(8,128)(2,1)}) %reduce-scatter.2.cloned.1.call-update) | async-done | bytes 262160 | tf_op jit(solution)/shard_map/reduce_scatter | solution.py:125
  179.5 4.3 gather_fusion
  183.8 6.1 %broadcast_in_dim.83 = bf16[64,12,2048]{2,1,0:T(8,128)(2,1)} reshape(bf16[768,2048]{1,0:T(8,128)(2,1)} %gather_fusion) | data formatting | bytes 6291456 | tf_op jit(solution)/shard_map/broadcast_in_dim | solution.py:151
  189.9 6.8 %broadcast_in_dim.84 = bf16[64,2,12,2048]{3,2,1,0:T(8,128)(2,1)} broadcast(bf16[64,12,2048]{2,1,0:T(8,128)(2,1)} %broadcast_in_dim.83), dimensions={0,2,3} | broadcast | bytes 9437184 | tf_op jit(solution)/shard_map/broadcast_in_dim | solution.py:151
  196.6 107.1 %all_to_all.10 = bf16[128,12,2048]{2,1,0:T(8,128)(2,1)} all-to-all(bf16[128,12,2048]{2,1,0:T(8,128)(2,1)} %bitcast.168), channel_id=1, replica_groups=mesh['dp'=8,'expert'=16] {'dp','expert'}, dimensions={0} | all-to-all | bytes 12582912 | tf_op jit(solution)/shard_map/all_to_all | solution.py:157
  303.7 10.7 %reshape.281 = bf16[1536,2048]{1,0:T(8,128)(2,1)} reshape(bf16[128,12,2048]{2,1,0:T(8,128)(2,1)} %all_to_all.10) | data formatting | bytes 12582912 | tf_op jit(solution)/shard_map/reshape | solution.py:24
  314.4 8.5 %fusion.45 = f32[1536,512]{1,0:T(8,128)} fusion(bf16[1536,2048]{1,0:T(8,128)(2,1)} %reshape.281, bf16[1,2048,512]{2,1,0:T(8,128)(2,1)} %param.33), kind=kOutput, calls=%fused_computation.50 | convolution fusion | flops 3221225472 | bytes 11534336 | tf_op jit(solution)/shard_map/dot_general | solution.py:25
  322.9 11.7 %convolution_convert_fusion = bf16[1536,2048]{1,0:T(8,128)(2,1)} fusion(bf16[1,512,2048]{2,1,0:T(8,128)(2,1)S(1)} %copy-done, bf16[1536,2048]{1,0:T(8,128)(2,1)} %reshape.281, f32[1536,512]{1,0:T(8,128)} %fusion.45, bf16[1,2048,512]{2,1,0:T(8,128)(2,1)} %param.34), kind=kOutput, calls=%fused_computation.42 | convolution fusion | flops 6450315264 | bytes 19922944 | tf_op jit(solution)/shard_map/dot_general | solution.py:28
  334.7 10.6 %reshape.282 = bf16[128,12,2048]{2,1,0:T(8,128)(2,1)} reshape(bf16[1536,2048]{1,0:T(8,128)(2,1)} %convolution_convert_fusion) | data formatting | bytes 12582912 | tf_op jit(solution)/shard_map/reshape | solution.py:31
  345.3 5.2 %all-to-all-start.1 = ((bf16[128,12,2048]{2,1,0:T(8,128)(2,1)}), bf16[128,12,2048]{2,1,0:T(8,128)(2,1)}, u32[]{:S(2)}, u32[]{:S(2)}) async-start(bf16[128,12,2048]{2,1,0:T(8,128)(2,1)} %reshape.282), calls=%async_computation.2 | async-start | bytes 16777216 | tf_op jit(solution)/shard_map/all_to_all | solution.py:155
  350.6 100.1 %all-to-all-done.1 = bf16[128,12,2048]{2,1,0:T(8,128)(2,1)} async-done(((bf16[128,12,2048]{2,1,0:T(8,128)(2,1)}), bf16[128,12,2048]{2,1,0:T(8,128)(2,1)}, u32[]{:S(2)}, u32[]{:S(2)}) %all-to-all-start.1) | async-done | bytes 6291488 | tf_op jit(solution)/shard_map/all_to_all | solution.py:155
  450.7 13.0 %copy.37 = bf16[64,2,12,2048]{3,1,2,0:T(2,128)(2,1)} copy(bf16[64,2,12,2048]{3,2,1,0:T(8,128)(2,1)} %bitcast.14) | data formatting | bytes 12582912 | tf_op jit(solution)/shard_map/reshape | solution.py:167
  463.7 16.2 %gather_fusion.1 = bf16[512,2,2048]{2,1,0:T(2,128)(2,1)} fusion(bf16[64,2,12,2048]{3,1,2,0:T(2,128)(2,1)} %copy.37, s32[512]{0:T(512)S(1)} %bitcast.167), kind=kCustom, calls=%fused_computation.1 | custom fusion | bytes 8392704 | tf_op jit(solution)/shard_map/gather | solution.py:167
  479.9 12.6 %convert_reduce_fusion.2 = f32[512,2048]{1,0:T(8,128)S(1)} fusion(bf16[512,2,2048]{2,1,0:T(2,128)(2,1)} %gather_fusion.1), kind=kLoop, calls=%fused_computation.41 | loop fusion | flops 3145728 | bytes 8388608 | tf_op jit(solution)/shard_map/reduce_sum | solution.py:168
  492.6 2.1 fusion.41
  (83 shorter events, 25.6 us)
Async XLA Ops:
  7.2 315.8 %copy-start = (bf16[1,512,2048]{2,1,0:T(8,128)(2,1)S(1)}, bf16[1,512,2048]{2,1,0:T(8,128)(2,1)}, u32[]{:S(2)}) copy-start(bf16[1,512,2048]{2,1,0:T(8,128)(2,1)} %param.35) | copy-start | bytes 6291460
  7.2 61.6 %copy-start.7 = (bf16[2048,128]{1,0:T(8,128)(2,1)S(1)}, bf16[2048,128]{1,0:T(8,128)(2,1)}, u32[]{:S(2)}) copy-start(bf16[2048,128]{1,0:T(8,128)(2,1)} %param.22) | copy-start | bytes 1572868
  7.2 57.9 %all-gather.2.cloned.1.call-start = ((), (), s32[]{:S(2)}) async-start(), calls=%async_computation.3 | async-start | bytes 4456448 | tf_op jit(solution)/shard_map/all_gather | solution.py:60
  10.4 166.9 %reduce-scatter.2.cloned.1.call-start = ((), (), s32[]{:S(2)}) async-start(), calls=%async_computation.4 | async-start | bytes 4456448 | tf_op jit(solution)/shard_map/reduce_scatter | solution.py:125
  65.1 3.7 copy-start.6
  68.8 1.6 copy-start.8
  70.0 1.6 copy-start.2
  70.1 1.6 copy-start.9
  96.3 4.3 copy-start.4
  100.6 76.7 %copy-start.1 = (bf16[64,2048]{1,0:T(8,128)(2,1)S(1)}, bf16[64,2048]{1,0:T(8,128)(2,1)}, u32[]{:S(2)}) copy-start(bf16[64,2048]{1,0:T(8,128)(2,1)} %param.19) | copy-start | bytes 786436
  100.6 77.9 %copy-start.3 = (f32[2048]{0:T(1024)S(1)}, f32[2048]{0:T(1024)}, u32[]{:S(2)}) copy-start(f32[2048]{0:T(1024)} %param.30) | copy-start | bytes 24580
  345.3 5.2 %copy-start.5 = (f32[64,8]{0,1:T(8,128)S(1)}, f32[64,8]{0,1:T(8,128)}, u32[]{:S(2)}) copy-start(f32[64,8]{0,1:T(8,128)} %param.32) | copy-start | bytes 6148
  345.3 105.4 %all-to-all-start.1 = ((bf16[128,12,2048]{2,1,0:T(8,128)(2,1)}), bf16[128,12,2048]{2,1,0:T(8,128)(2,1)}, u32[]{:S(2)}, u32[]{:S(2)}) async-start(bf16[128,12,2048]{2,1,0:T(8,128)(2,1)} %reshape.282), calls=%async_computation.2 | async-start | bytes 16777216 | tf_op jit(solution)/shard_map/all_to_all | solution.py:155
Sparse Core Ops, SparseCore 0:
  10.7 54.2 all-gather.1
  100.7 76.5 reduce-scatter.1
where the time goes:
time: 505 us; the launch traced here: 502 us
  waiting for transfers between devices  226 us (45%)
  blocking collectives  107 us (21%)
  local copies, waits for them, and re-layouts  72.6 us (14%)
  matrix products  43.5 us (9%)
  other arithmetic  30.4 us (6%)
  between operations  14.3 us (3%)
  starting transfers between devices  5.29 us (1%)
    all_to_all x1, blocking collectives, per_device(): lax.all_to_all(outgoing, ('dp', 'expert'), split_axis=0, concat_axis=0, t...  107 us
    all_to_all x1, waiting for transfers between devices, per_device(): lax.all_to_all(expert_block(lax.all_to_all(outgoing, ('dp', 'expert'), sp...  100 us
    reduce_scatter x1, waiting for transfers between devices, per_device(): lax.psum_scatter(jnp.dot(piece, output_weight, preferred_element_type=jnp...  72.2 us
    all_gather x1, waiting for transfers between devices, per_device(): piece = lax.all_gather(normed, 'expert', axis=0, tiled=True)  53.9 us
    gather x1, local copies, waits for them, and re-layouts, per_device(): returned.reshape(experts, hidden_split, capacity, width)[chosen, :, slots]  16.2 us
    reshape x1, local copies, waits for them, and re-layouts, per_device(): returned.reshape(experts, hidden_split, capacity, width)[chosen, :, slots]  13 us
    broadcast_in_dim x2, local copies, waits for them, and re-layouts, per_device(): jnp.broadcast_to(padded[table].reshape(experts, 1, capacity, width), (exp...  12.8 us
    reduce_sum x1, other arithmetic, per_device(): jnp.sum(pieces.astype(jnp.float32), axis=1)  12.6 us
  transfers between devices with their start and end apart: 3, of which 3 were waited for; matrix products, arithmetic and copies ran while one was open for 1% of the time, Pallas kernels for 0%

commit v1 on v0

--- a/solution.py
+++ b/solution.py
@@ -122,17 +122,16 @@
     attended = lax.fori_loop(0, groups_here, group_step, jnp.zeros(layout, jnp.bfloat16))
     flat_attended = attended.reshape(requests * SB, local_width)
     piece = flat_attended
-    attention_update = lax.psum_scatter(
-        jnp.dot(piece, output_weight, preferred_element_type=jnp.float32).astype(jnp.bfloat16),
-        "expert",
-        scatter_dimension=0,
-        tiled=True,
+    expert_groups = lax.axis_size("expert")
+    projected_out = jnp.dot(piece, output_weight, preferred_element_type=jnp.float32).astype(jnp.bfloat16)
+    partials = lax.all_to_all(
+        projected_out.reshape(expert_groups, tok_rows, width), "expert", 0, 0, tiled=True
     )
+    attention_update = jnp.sum(partials.astype(jnp.float32), axis=0).astype(jnp.bfloat16)
     expert_input = rms_scale(
         residual_in.astype(jnp.float32) + attention_update.astype(jnp.float32), expert_gain
     )
     data_groups = lax.axis_size("dp")
-    expert_groups = lax.axis_size("expert")
     devices = data_groups * expert_groups
     hidden_split = FF // gate_weight.shape[2]
     experts = devices // hidden_split
@@ -147,26 +146,28 @@
         .at[chosen * capacity + slots]
         .set(owners)
     )
-    padded = jnp.concatenate([expert_input, jnp.zeros((1, width), jnp.bfloat16)], axis=0)
-    outgoing = jnp.broadcast_to(
-        padded[table].reshape(experts, 1, capacity, width), (experts, hidden_split, capacity, width)
+    lanes = 128
+    sub = width // lanes
+    tiles = expert_input.reshape(tok_rows, sub, lanes)
+    padded = jnp.concatenate([tiles, jnp.zeros((1, sub, lanes), jnp.bfloat16)], axis=0)
+    index = jnp.broadcast_to(
+        table.reshape(experts, 1, capacity), (experts, hidden_split, capacity)
+    ).reshape(-1)
+    outgoing = padded[index].reshape(devices, capacity * sub, lanes)
+    arrived = lax.all_to_all(outgoing, ("dp", "expert"), 0, 0, tiled=True)
+    produced = expert_block(
+        arrived.reshape(devices * capacity, width), gate_weight, up_weight, down_weight
     )
-    outgoing = outgoing.reshape(devices, capacity, width)
     returned = lax.all_to_all(
-        expert_block(
-            lax.all_to_all(outgoing, ("dp", "expert"), split_axis=0, concat_axis=0, tiled=True),
-            gate_weight,
-            up_weight,
-            down_weight,
-        ),
-        ("dp", "expert"),
-        split_axis=0,
-        concat_axis=0,
-        tiled=True,
+        produced.reshape(devices, capacity * sub, lanes), ("dp", "expert"), 0, 0, tiled=True
     )
-    pieces = returned.reshape(experts, hidden_split, capacity, width)[chosen, :, slots]
-    blended = jnp.sum(pieces.astype(jnp.float32), axis=1) * expert_mix.reshape(-1)[:, None]
-    expert_update = jnp.sum(blended.reshape(tok_rows, TOP, width), axis=1).astype(jnp.bfloat16)
+    pieces = returned.reshape(experts, hidden_split, capacity, sub, lanes)[chosen, :, slots]
+    blended = jnp.sum(pieces.astype(jnp.float32), axis=1) * expert_mix.reshape(-1)[:, None, None]
+    expert_update = (
+        jnp.sum(blended.reshape(tok_rows, TOP, sub, lanes), axis=1)
+        .reshape(tok_rows, width)
+        .astype(jnp.bfloat16)
+    )
     return (attention_update, expert_update)
 
 

time: 505 us -> 410 us (0.81)
  waiting for transfers between devices: 226 us -> 184 us
  local copies, waits for them, and re-layouts: 72.6 us -> 41.5 us
  blocking collectives: 107 us -> 90.9 us
  other arithmetic: 30.4 us -> 21.8 us
  starting transfers between devices: 5.29 us -> 10.8 us
    reduce_scatter x1 -> x0, waiting for transfers between devices: 72.2 us -> none  [per_device(): lax.psum_scatter(jnp.dot(piece, output_weight, preferred_element_type=jnp...]
    all_to_all x1 -> x2, waiting for transfers between devices: 100 us -> 130 us  [the longest x1 75.4 us: per_device(): lax.all_to_all(produced.reshape(devices, capacity * sub, lanes), ('dp', '...]
    all_to_all x1, blocking collectives: 107 us -> 90.9 us  [per_device(): arrived = lax.all_to_all(outgoing, ('dp', 'expert'), 0, 0, tiled=True)]
    reshape x3, local copies, waits for them, and re-layouts: 34.3 us -> 20.9 us  [the longest x1 10.5 us: per_device(): produced.reshape(devices, capacity * sub, lanes)]
    broadcast_in_dim x2, local copies, waits for them, and re-layouts: 12.8 us -> 0.12 us  [per_device(): jnp.broadcast_to(table.reshape(experts, 1, capacity), (experts, hidden_sp...]
    reduce_sum x1, other arithmetic: 12.6 us -> 4.15 us  [per_device(): jnp.sum(pieces.astype(jnp.float32), axis=1)]
    gather x2, local copies, waits for them, and re-layouts: 20.5 us -> 14.6 us  [the longest x1 8.93 us: per_device(): returned.reshape(experts, hidden_split, capacity, sub, lanes)]
    all_to_all x1 -> x2, starting transfers between devices: 5.21 us -> 10.8 us  [the longest x1 5.61 us: per_device(): lax.all_to_all(produced.reshape(devices, capacity * sub, lanes), ('dp', '...]
where the time goes in v1:
time: 410 us; the launch traced here: 408 us
  waiting for transfers between devices  184 us (45%)
  blocking collectives  90.9 us (22%)
  matrix products  43.6 us (11%)
  local copies, waits for them, and re-layouts  41.5 us (10%)
  other arithmetic  21.8 us (5%)
  between operations  14.3 us (3%)
  starting transfers between devices  10.8 us (3%)
    all_to_all x1, blocking collectives, per_device(): arrived = lax.all_to_all(outgoing, ('dp', 'expert'), 0, 0, tiled=True)  90.9 us
    all_to_all x1, waiting for transfers between devices, per_device(): lax.all_to_all(produced.reshape(devices, capacity * sub, lanes), ('dp', '...  75.4 us
    all_to_all x1, waiting for transfers between devices, per_device(): lax.all_to_all(projected_out.reshape(expert_groups, tok_rows, width), 'ex...  54.1 us
    all_gather x1, waiting for transfers between devices, per_device(): piece = lax.all_gather(normed, 'expert', axis=0, tiled=True)  54 us
    dot_general x1, matrix products, expert_block(): jnp.dot(hidden, down_weight[0], preferred_element_type=jnp.float32)  11.7 us
    reshape x1, local copies, waits for them, and re-layouts, per_device(): produced.reshape(devices, capacity * sub, lanes)  10.5 us
    reshape x1, local copies, waits for them, and re-layouts, per_device(): arrived.reshape(devices * capacity, width)  10.3 us
    gather x1, local copies, waits for them, and re-layouts, per_device(): returned.reshape(experts, hidden_split, capacity, sub, lanes)  8.93 us
  transfers between devices with their start and end apart: 3, of which 3 were waited for; matrix products, arithmetic and copies ran while one was open for 1% of the time, Pallas kernels for 0%

profile of v1, /device:TPU:1, one launch (start us, length us, event | category | flops | bytes accessed | tf_op | source)
XLA Modules:
  0.0 408.5 jit_solution(3782199950880802426)
XLA Ops:
  11.1 54.0 %all-gather.2.cloned.1.call-done = bf16[1024,2048]{1,0:T(8,128)(2,1)} async-done(((bf16[64,2048]{1,0:T(8,128)(2,1)}), bf16[1024,2048]{1,0:T(8,128)(2,1)}) %all-gather.2.cloned.1.call-update) | async-done | bytes 4194320 | tf_op jit(solution)/shard_map/all_gather | solution.py:60
  65.1 3.7 convolution_convert_fusion.4
  71.7 24.7 %while.14 = (s32[]{:T(128)}, bf16[32,32,1,128]{3,1,0,2:T(8,128)(2,1)S(1)}, s32[32]{0:T(128)S(1)}, bf16[3,2048,128]{2,1,0:T(8,128)(2,1)}, s32[3]{0:T(128)S(1)}, /...) while((s32[]{:T(128)}, ...), condition=%wide.region_7.8_spmd.clone, body=%wide.region_1.7_spmd.clone.sunk | while | flops 555074688 | bytes 15133611 | solution.py:122
  74.2 1.9 bitcast_reduce_fusion.2
  77.8 2.1 fusion.93
  82.4 1.9 bitcast_reduce_fusion.2
  86.0 2.1 fusion.93
  90.6 1.9 bitcast_reduce_fusion.2
  94.3 2.1 fusion.93
  96.3 4.3 %convolution_convert_fusion.1 = bf16[1024,2048]{1,0:T(8,128)(2,1)} fusion(bf16[1024,128]{1,0:T(8,128)(2,1)S(1)} %bitcast.178, bf16[128,2048]{1,0:T(8,128)(2,1)} %param.24), kind=kOutput, calls=%fused_computation.44 | convolution fusion | flops 538968064 | bytes 4980736 | tf_op jit(solution)/shard_map/dot_general | solution.py:126
  100.6 5.2 %all-to-all-start = ((bf16[16,64,2048]{2,1,0:T(8,128)(2,1)}), bf16[16,64,2048]{2,1,0:T(8,128)(2,1)}, u32[]{:S(2)}, u32[]{:S(2)}) async-start(bf16[16,64,2048]{2,1,0:T(8,128)(2,1)} %bitcast.174), calls=%async_computation | async-start | bytes 8388608 | tf_op jit(solution)/shard_map/all_to_all | solution.py:127
  107.8 2.4 scatter_custom_fusion
  110.6 54.1 %all-to-all-done = bf16[16,64,2048]{2,1,0:T(8,128)(2,1)} async-done(((bf16[16,64,2048]{2,1,0:T(8,128)(2,1)}), bf16[16,64,2048]{2,1,0:T(8,128)(2,1)}, u32[]{:S(2)}, u32[]{:S(2)}) %all-to-all-start) | async-done | bytes 4194336 | tf_op jit(solution)/shard_map/all_to_all | solution.py:127
  164.7 3.0 reduce_sum.97
  168.1 5.7 %gather_fusion = bf16[1536,16,128]{2,1,0:T(8,128)(2,1)} fusion(bf16[65,16,128]{2,1,0:T(8,128)(2,1)S(1)} %concatenate.6, s32[2048]{0:T(1024)S(1)} %pad_clamp_fusion), kind=kCustom, calls=%fused_computation | custom fusion | bytes 12589056 | tf_op jit(solution)/shard_map/gather | solution.py:156
  173.8 90.9 %all_to_all.15 = bf16[128,192,128]{2,1,0:T(8,128)(2,1)} all-to-all(bf16[128,192,128]{2,1,0:T(8,128)(2,1)} %bitcast.175), channel_id=1, replica_groups=mesh['dp'=8,'expert'=16] {'dp','expert'}, dimensions={0} | all-to-all | bytes 12582912 | tf_op jit(solution)/shard_map/all_to_all | solution.py:157
  264.7 10.3 %reshape.320 = bf16[1536,2048]{1,0:T(8,128)(2,1)} reshape(bf16[128,192,128]{2,1,0:T(8,128)(2,1)} %all_to_all.15) | data formatting | bytes 12582912 | tf_op jit(solution)/shard_map/reshape | solution.py:159
  275.0 8.5 %fusion.44 = f32[1536,512]{1,0:T(8,128)} fusion(bf16[1536,2048]{1,0:T(8,128)(2,1)} %reshape.320, bf16[1,2048,512]{2,1,0:T(8,128)(2,1)} %param.33), kind=kOutput, calls=%fused_computation.49 | convolution fusion | flops 3221225472 | bytes 11534336 | tf_op jit(solution)/shard_map/dot_general | solution.py:25
  283.6 11.7 %convolution_convert_fusion = bf16[1536,2048]{1,0:T(8,128)(2,1)} fusion(bf16[1,512,2048]{2,1,0:T(8,128)(2,1)S(1)} %copy-done, bf16[1536,2048]{1,0:T(8,128)(2,1)} %reshape.320, f32[1536,512]{1,0:T(8,128)} %fusion.44, bf16[1,2048,512]{2,1,0:T(8,128)(2,1)} %param.34), kind=kOutput, calls=%fused_computation.42 | convolution fusion | flops 6450315264 | bytes 19922944 | tf_op jit(solution)/shard_map/dot_general | solution.py:28
  295.3 10.5 %reshape.321 = bf16[128,192,128]{2,1,0:T(8,128)(2,1)} reshape(bf16[1536,2048]{1,0:T(8,128)(2,1)} %convolution_convert_fusion) | data formatting | bytes 12582912 | tf_op jit(solution)/shard_map/reshape | solution.py:162
  305.8 5.6 %all-to-all-start.2 = ((bf16[128,192,128]{2,1,0:T(8,128)(2,1)}), bf16[128,192,128]{2,1,0:T(8,128)(2,1)}, u32[]{:S(2)}, u32[]{:S(2)}) async-start(bf16[128,192,128]{2,1,0:T(8,128)(2,1)} %reshape.321), calls=%async_computation.2 | async-start | bytes 12582912 | tf_op jit(solution)/shard_map/all_to_all | solution.py:161
  311.5 75.4 %all-to-all-done.2 = bf16[128,192,128]{2,1,0:T(8,128)(2,1)} async-done(((bf16[128,192,128]{2,1,0:T(8,128)(2,1)}), bf16[128,192,128]{2,1,0:T(8,128)(2,1)}, u32[]{:S(2)}, u32[]{:S(2)}) %all-to-all-start.2) | async-done | bytes 6291488 | tf_op jit(solution)/shard_map/all_to_all | solution.py:161
  386.9 8.9 %gather_fusion.1 = bf16[512,2,16,128]{3,2,1,0:T(8,128)(2,1)} fusion(bf16[64,2,12,16,128]{4,3,2,1,0:T(8,128)(2,1)} %bitcast.15, s32[512]{0:T(512)S(1)} %bitcast.173), kind=kCustom, calls=%fused_computation.1 | custom fusion | bytes 8392704 | tf_op jit(solution)/shard_map/gather | solution.py:164
  395.8 4.1 %convert_reduce_fusion.2 = f32[512,16,128]{2,1,0:T(8,128)S(1)} fusion(bf16[512,2,16,128]{3,2,1,0:T(8,128)(2,1)} %gather_fusion.1), kind=kLoop, calls=%fused_computation.41 | loop fusion | flops 3145728 | bytes 8388608 | tf_op jit(solution)/shard_map/reduce_sum | solution.py:165
  (87 shorter events, 21.9 us)
Async XLA Ops:
  7.2 276.4 %copy-start = (bf16[1,512,2048]{2,1,0:T(8,128)(2,1)S(1)}, bf16[1,512,2048]{2,1,0:T(8,128)(2,1)}, u32[]{:S(2)}) copy-start(bf16[1,512,2048]{2,1,0:T(8,128)(2,1)} %param.35) | copy-start | bytes 6291460
  7.2 61.6 %copy-start.8 = (bf16[2048,128]{1,0:T(8,128)(2,1)S(1)}, bf16[2048,128]{1,0:T(8,128)(2,1)}, u32[]{:S(2)}) copy-start(bf16[2048,128]{1,0:T(8,128)(2,1)} %param.22) | copy-start | bytes 1572868
  7.2 57.9 %all-gather.2.cloned.1.call-start = ((), (), s32[]{:S(2)}) async-start(), calls=%async_computation.3 | async-start | bytes 4456448 | tf_op jit(solution)/shard_map/all_gather | solution.py:60
  65.1 3.7 copy-start.7
  68.8 1.6 copy-start.9
  70.0 1.6 copy-start.3
  70.1 1.6 copy-start.10
  100.6 5.2 %copy-start.5 = (s32[64,8]{0,1:T(8,128)S(1)}, s32[64,8]{0,1:T(8,128)}, u32[]{:S(2)}) copy-start(s32[64,8]{0,1:T(8,128)} %param.31) | copy-start | bytes 6148
  100.6 64.1 %all-to-all-start = ((bf16[16,64,2048]{2,1,0:T(8,128)(2,1)}), bf16[16,64,2048]{2,1,0:T(8,128)(2,1)}, u32[]{:S(2)}, u32[]{:S(2)}) async-start(bf16[16,64,2048]{2,1,0:T(8,128)(2,1)} %bitcast.174), calls=%async_computation | async-start | bytes 8388608 | tf_op jit(solution)/shard_map/all_to_all | solution.py:127
  105.8 61.9 %copy-start.1 = (bf16[64,2048]{1,0:T(8,128)(2,1)S(1)}, bf16[64,2048]{1,0:T(8,128)(2,1)}, u32[]{:S(2)}) copy-start(bf16[64,2048]{1,0:T(8,128)(2,1)} %param.19) | copy-start | bytes 786436
  105.8 62.1 %copy-start.4 = (f32[2048]{0:T(1024)S(1)}, f32[2048]{0:T(1024)}, u32[]{:S(2)}) copy-start(f32[2048]{0:T(1024)} %param.30) | copy-start | bytes 24580
  167.7 6.1 %copy-start.2 = (bf16[64,2048]{1,0:T(8,128)(2,1)}, bf16[64,2048]{1,0:T(8,128)(2,1)S(1)}, u32[]{:S(2)}) copy-start(bf16[64,2048]{1,0:T(8,128)(2,1)S(1)} %reduce_sum.97) | copy-start | bytes 786436
  305.8 5.6 %copy-start.6 = (f32[64,8]{0,1:T(8,128)S(1)}, f32[64,8]{0,1:T(8,128)}, u32[]{:S(2)}) copy-start(f32[64,8]{0,1:T(8,128)} %param.32) | copy-start | bytes 6148
  305.8 81.2 %all-to-all-start.2 = ((bf16[128,192,128]{2,1,0:T(8,128)(2,1)}), bf16[128,192,128]{2,1,0:T(8,128)(2,1)}, u32[]{:S(2)}, u32[]{:S(2)}) async-start(bf16[128,192,128]{2,1,0:T(8,128)(2,1)} %reshape.321), calls=%async_computation.2 | async-start | bytes 12582912 | tf_op jit(solution)/shard_map/all_to_all | solution.py:161
Sparse Core Ops, SparseCore 0:
  10.7 54.2 all-gather.1

commit v2 on v1

--- a/solution.py
+++ b/solution.py
@@ -20,15 +20,17 @@
 
 
 def expert_block(block, gate_weight, up_weight, down_weight):
-    shape_kept = block.shape
-    flat = block.reshape(-1, shape_kept[-1])
-    gated = jnp.dot(flat, gate_weight[0], preferred_element_type=jnp.float32)
-    lifted = jnp.dot(flat, up_weight[0], preferred_element_type=jnp.float32)
+    rows, sub, lanes = block.shape
+    gate = gate_weight[0].reshape(sub, lanes, -1)
+    up = up_weight[0].reshape(sub, lanes, -1)
+    down = down_weight[0].reshape(-1, sub, lanes)
+    contract = (((1, 2), (0, 1)), ((), ()))
+    gated = lax.dot_general(block, gate, contract, preferred_element_type=jnp.float32)
+    lifted = lax.dot_general(block, up, contract, preferred_element_type=jnp.float32)
     hidden = (jax.nn.silu(gated) * lifted).astype(jnp.bfloat16)
-    produced = jnp.dot(hidden, down_weight[0], preferred_element_type=jnp.float32).astype(
-        jnp.bfloat16
-    )
-    return produced.reshape(shape_kept)
+    return lax.dot_general(
+        hidden, down, (((1,), (0,)), ((), ())), preferred_element_type=jnp.float32
+    ).astype(jnp.bfloat16)
 
 
 def per_device(
@@ -156,7 +158,7 @@
     outgoing = padded[index].reshape(devices, capacity * sub, lanes)
     arrived = lax.all_to_all(outgoing, ("dp", "expert"), 0, 0, tiled=True)
     produced = expert_block(
-        arrived.reshape(devices * capacity, width), gate_weight, up_weight, down_weight
+        arrived.reshape(devices * capacity, sub, lanes), gate_weight, up_weight, down_weight
     )
     returned = lax.all_to_all(
         produced.reshape(devices, capacity * sub, lanes), ("dp", "expert"), 0, 0, tiled=True

time: 410 us -> 403 us (0.983)
  blocking collectives: 90.9 us -> 0 us
  waiting for transfers between devices: 184 us -> 255 us
  starting transfers between devices: 10.8 us -> 26.8 us
  matrix products: 43.6 us -> 38.9 us
    all_to_all x1 -> x0, blocking collectives: 90.9 us -> none  [per_device(): arrived = lax.all_to_all(outgoing, ('dp', 'expert'), 0, 0, tiled=True)]
    all_to_all x0 -> x1, waiting for transfers between devices: none -> 71.8 us  [per_device(): arrived = lax.all_to_all(outgoing, ('dp', 'expert'), 0, 0, tiled=True)]
    reshape x2 -> x0, local copies, waits for them, and re-layouts: 20.8 us -> none  [the longest x1 10.5 us: per_device(): produced.reshape(devices, capacity * sub, lanes)]
    convert_element_type x0 -> x1, local copies, waits for them, and re-layouts: none -> 18.3 us  [expert_block(): return lax.dot_general(hidden, down, (((1,), (0,)), ((), ())), preferred_...]
    all_to_all x0 -> x1, starting transfers between devices: none -> 16.3 us  [per_device(): arrived = lax.all_to_all(outgoing, ('dp', 'expert'), 0, 0, tiled=True)]
    dot_general x2 -> x3, matrix products: 20.3 us -> 15.6 us  [the longest x1 6.01 us: expert_block(): lax.dot_general(block, up, contract, preferred_element_type=jnp.float32)]
  transfers between devices with their start and end apart: 3 -> 4, of which waited for: 3 -> 4; matrix products, arithmetic and copies ran while one was open for 1% -> 2% of each run, Pallas kernels for 0% -> 0%
where the time goes in v2:
time: 403 us; the launch traced here: 402 us
  waiting for transfers between devices  255 us (63%)
  local copies, waits for them, and re-layouts  42.6 us (11%)
  matrix products  38.9 us (10%)
  starting transfers between devices  26.8 us (7%)
  other arithmetic  21.8 us (5%)
  between operations  14.4 us (4%)
    all_to_all x1, waiting for transfers between devices, per_device(): lax.all_to_all(produced.reshape(devices, capacity * sub, lanes), ('dp', '...  75.3 us
    all_to_all x1, waiting for transfers between devices, per_device(): arrived = lax.all_to_all(outgoing, ('dp', 'expert'), 0, 0, tiled=True)  71.8 us
    all_to_all x1, waiting for transfers between devices, per_device(): lax.all_to_all(projected_out.reshape(expert_groups, tok_rows, width), 'ex...  54.2 us
    all_gather x1, waiting for transfers between devices, per_device(): piece = lax.all_gather(normed, 'expert', axis=0, tiled=True)  54 us
    convert_element_type x1, local copies, waits for them, and re-layouts, expert_block(): return lax.dot_general(hidden, down, (((1,), (0,)), ((), ())), preferred_...  18.3 us
    all_to_all x1, starting transfers between devices, per_device(): arrived = lax.all_to_all(outgoing, ('dp', 'expert'), 0, 0, tiled=True)  16.3 us
    gather x1, local copies, waits for them, and re-layouts, per_device(): returned.reshape(experts, hidden_split, capacity, sub, lanes)  8.94 us
  transfers between devices with their start and end apart: 4, of which 4 were waited for; matrix products, arithmetic and copies ran while one was open for 2% of the time, Pallas kernels for 0%

profile of v2, /device:TPU:1, one launch (start us, length us, event | category | flops | bytes accessed | tf_op | source)
XLA Modules:
  0.0 401.9 jit_solution(474718073541000666)
XLA Ops:
  11.1 54.0 %all-gather.2.cloned.1.call-done = bf16[1024,2048]{1,0:T(8,128)(2,1)} async-done(((bf16[64,2048]{1,0:T(8,128)(2,1)}), bf16[1024,2048]{1,0:T(8,128)(2,1)}) %all-gather.2.cloned.1.call-update) | async-done | bytes 4194320 | tf_op jit(solution)/shard_map/all_gather | solution.py:62
  65.1 3.7 convolution_convert_fusion.4
  71.7 24.7 %while.14 = (s32[]{:T(128)}, bf16[32,32,1,128]{3,1,0,2:T(8,128)(2,1)S(1)}, s32[32]{0:T(128)S(1)}, bf16[3,2048,128]{2,1,0:T(8,128)(2,1)}, s32[3]{0:T(128)S(1)}, /...) while((s32[]{:T(128)}, ...), condition=%wide.region_7.8_spmd.clone, body=%wide.region_1.7_spmd.clone.sunk | while | flops 555074688 | bytes 15133611 | solution.py:124
  77.8 2.1 fusion.106
  82.4 1.9 bitcast_reduce_fusion.2
  86.0 2.1 fusion.106
  94.3 2.1 fusion.106
  96.3 4.3 %convolution_convert_fusion.1 = bf16[1024,2048]{1,0:T(8,128)(2,1)} fusion(bf16[1024,128]{1,0:T(8,128)(2,1)S(1)} %bitcast.191, bf16[128,2048]{1,0:T(8,128)(2,1)} %param.24), kind=kOutput, calls=%fused_computation.48 | convolution fusion | flops 538968064 | bytes 4980736 | tf_op jit(solution)/shard_map/dot_general | solution.py:128
  100.6 5.2 %all-to-all-start = ((bf16[16,64,2048]{2,1,0:T(8,128)(2,1)}), bf16[16,64,2048]{2,1,0:T(8,128)(2,1)}, u32[]{:S(2)}, u32[]{:S(2)}) async-start(bf16[16,64,2048]{2,1,0:T(8,128)(2,1)} %bitcast.184), calls=%async_computation | async-start | bytes 8388608 | tf_op jit(solution)/shard_map/all_to_all | solution.py:129
  107.8 2.4 scatter_custom_fusion
  110.6 54.2 %all-to-all-done = bf16[16,64,2048]{2,1,0:T(8,128)(2,1)} async-done(((bf16[16,64,2048]{2,1,0:T(8,128)(2,1)}), bf16[16,64,2048]{2,1,0:T(8,128)(2,1)}, u32[]{:S(2)}, u32[]{:S(2)}) %all-to-all-start) | async-done | bytes 4194336 | tf_op jit(solution)/shard_map/all_to_all | solution.py:129
  164.8 3.0 reduce_sum.97
  168.2 5.8 %gather_fusion = bf16[1536,16,128]{2,1,0:T(8,128)(2,1)} fusion(bf16[65,16,128]{2,1,0:T(8,128)(2,1)S(1)} %concatenate.6, s32[2048]{0:T(1024)S(1)} %pad_clamp_fusion), kind=kCustom, calls=%fused_computation | custom fusion | bytes 12589056 | tf_op jit(solution)/shard_map/gather | solution.py:158
  174.0 16.3 %all-to-all-start.1 = ((bf16[128,192,128]{2,1,0:T(8,128)(2,1)}), bf16[128,192,128]{2,1,0:T(8,128)(2,1)}, u32[]{:S(2)}, u32[]{:S(2)}) async-start(bf16[128,192,128]{2,1,0:T(8,128)(2,1)} %bitcast.186), calls=%async_computation.1 | async-start | bytes 12582912 | tf_op jit(solution)/shard_map/all_to_all | solution.py:159
  190.3 3.6 copy.40
  193.9 71.8 %all-to-all-done.1 = bf16[128,192,128]{2,1,0:T(8,128)(2,1)} async-done(((bf16[128,192,128]{2,1,0:T(8,128)(2,1)}), bf16[128,192,128]{2,1,0:T(8,128)(2,1)}, u32[]{:S(2)}, u32[]{:S(2)}) %all-to-all-start.1) | async-done | bytes 6291488 | tf_op jit(solution)/shard_map/all_to_all | solution.py:159
  265.7 5.6 %fusion.45 = f32[1536,512]{1,0:T(8,128)S(1)} fusion(bf16[16,128,512]{2,1,0:T(8,128)(2,1)S(1)} %bitcast.182, bf16[1536,16,128]{2,1,0:T(8,128)(2,1)} %bitcast.12), kind=kOutput, calls=%fused_computation.49 | convolution fusion | flops 3221225472 | bytes 11534336 | tf_op jit(solution)/shard_map/dot_general | solution.py:28
  271.4 6.0 %fusion.57 = bf16[1536,512,1]{1,0,2:T(8,128)(2,1)S(1)} fusion(bf16[16,128,512]{2,1,0:T(8,128)(2,1)S(1)} %bitcast.200, bf16[1536,16,128]{2,1,0:T(8,128)(2,1)} %bitcast.12, f32[1536,512]{1,0:T(8,128)S(1)} %fusion.45), kind=kOutput, calls=%fused_computation.53 | convolution fusion | flops 3225944064 | bytes 13107200 | tf_op jit(solution)/shard_map/dot_general | solution.py:29
  277.4 4.0 convolution_convert_fusion
  281.4 18.3 %copy.36 = bf16[1536,16,128]{2,1,0:T(8,128)(2,1)} copy(bf16[1536,16,128]{2,0,1:T(8,128)(2,1)S(1)} %convolution_convert_fusion) | data formatting | bytes 12582912 | tf_op jit(solution)/shard_map/convert_element_type | solution.py:33
  299.6 5.3 %all-to-all-start.2 = ((bf16[128,192,128]{2,1,0:T(8,128)(2,1)}), bf16[128,192,128]{2,1,0:T(8,128)(2,1)}, u32[]{:S(2)}, u32[]{:S(2)}) async-start(bf16[128,192,128]{2,1,0:T(8,128)(2,1)} %bitcast.185), calls=%async_computation.2 | async-start | bytes 12582912 | tf_op jit(solution)/shard_map/all_to_all | solution.py:163
  305.0 75.3 %all-to-all-done.2 = bf16[128,192,128]{2,1,0:T(8,128)(2,1)} async-done(((bf16[128,192,128]{2,1,0:T(8,128)(2,1)}), bf16[128,192,128]{2,1,0:T(8,128)(2,1)}, u32[]{:S(2)}, u32[]{:S(2)}) %all-to-all-start.2) | async-done | bytes 6291488 | tf_op jit(solution)/shard_map/all_to_all | solution.py:163
  380.3 8.9 %gather_fusion.1 = bf16[512,2,16,128]{3,2,1,0:T(8,128)(2,1)} fusion(bf16[64,2,12,16,128]{4,3,2,1,0:T(8,128)(2,1)} %bitcast.19, s32[512]{0:T(512)S(1)} %bitcast.183), kind=kCustom, calls=%fused_computation.1 | custom fusion | bytes 8392704 | tf_op jit(solution)/shard_map/gather | solution.py:166
  389.2 4.1 %convert_reduce_fusion.2 = f32[512,16,128]{2,1,0:T(8,128)S(1)} fusion(bf16[512,2,16,128]{3,2,1,0:T(8,128)(2,1)} %gather_fusion.1), kind=kLoop, calls=%fused_computation.41 | loop fusion | flops 3145728 | bytes 8388608 | tf_op jit(solution)/shard_map/reduce_sum | solution.py:167
  (93 shorter events, 25.6 us)
Async XLA Ops:
  7.2 258.5 %copy-start = (bf16[1,2048,512]{2,1,0:T(8,128)(2,1)S(1)}, bf16[1,2048,512]{2,1,0:T(8,128)(2,1)}, u32[]{:S(2)}) copy-start(bf16[1,2048,512]{2,1,0:T(8,128)(2,1)} %param.33) | copy-start | bytes 6291460
  7.2 61.6 %copy-start.10 = (bf16[2048,128]{1,0:T(8,128)(2,1)S(1)}, bf16[2048,128]{1,0:T(8,128)(2,1)}, u32[]{:S(2)}) copy-start(bf16[2048,128]{1,0:T(8,128)(2,1)} %param.22) | copy-start | bytes 1572868
  7.2 57.9 %all-gather.2.cloned.1.call-start = ((), (), s32[]{:S(2)}) async-start(), calls=%async_computation.3 | async-start | bytes 4456448 | tf_op jit(solution)/shard_map/all_gather | solution.py:62
  65.1 3.7 copy-start.8
  68.8 1.6 copy-start.11
  70.0 1.6 copy-start.4
  70.1 1.6 copy-start.12
  100.6 5.2 %copy-start.6 = (s32[64,8]{0,1:T(8,128)S(1)}, s32[64,8]{0,1:T(8,128)}, u32[]{:S(2)}) copy-start(s32[64,8]{0,1:T(8,128)} %param.31) | copy-start | bytes 6148
  100.6 64.2 %all-to-all-start = ((bf16[16,64,2048]{2,1,0:T(8,128)(2,1)}), bf16[16,64,2048]{2,1,0:T(8,128)(2,1)}, u32[]{:S(2)}, u32[]{:S(2)}) async-start(bf16[16,64,2048]{2,1,0:T(8,128)(2,1)} %bitcast.184), calls=%async_computation | async-start | bytes 8388608 | tf_op jit(solution)/shard_map/all_to_all | solution.py:129
  105.8 62.0 %copy-start.1 = (bf16[64,2048]{1,0:T(8,128)(2,1)S(1)}, bf16[64,2048]{1,0:T(8,128)(2,1)}, u32[]{:S(2)}) copy-start(bf16[64,2048]{1,0:T(8,128)(2,1)} %param.19) | copy-start | bytes 786436
  105.8 62.2 %copy-start.5 = (f32[2048]{0:T(1024)S(1)}, f32[2048]{0:T(1024)}, u32[]{:S(2)}) copy-start(f32[2048]{0:T(1024)} %param.30) | copy-start | bytes 24580
  167.7 6.2 %copy-start.2 = (bf16[64,2048]{1,0:T(8,128)(2,1)}, bf16[64,2048]{1,0:T(8,128)(2,1)S(1)}, u32[]{:S(2)}) copy-start(bf16[64,2048]{1,0:T(8,128)(2,1)S(1)} %reduce_sum.97) | copy-start | bytes 786436
  174.0 91.7 %all-to-all-start.1 = ((bf16[128,192,128]{2,1,0:T(8,128)(2,1)}), bf16[128,192,128]{2,1,0:T(8,128)(2,1)}, u32[]{:S(2)}, u32[]{:S(2)}) async-start(bf16[128,192,128]{2,1,0:T(8,128)(2,1)} %bitcast.186), calls=%async_computation.1 | async-start | bytes 12582912 | tf_op jit(solution)/shard_map/all_to_all | solution.py:159
  265.7 5.7 %copy-start.9 = (bf16[1,2048,512]{2,1,0:T(8,128)(2,1)S(1)}, bf16[1,2048,512]{2,1,0:T(8,128)(2,1)}, u32[]{:S(2)}) copy-start(bf16[1,2048,512]{2,1,0:T(8,128)(2,1)} %param.34) | copy-start | bytes 6291460
  271.3 6.0 %copy-start.3 = (bf16[64,8,16,128]{3,2,1,0:T(8,128)(2,1)S(1)}, bf16[64,8,16,128]{3,2,1,0:T(8,128)(2,1)}, u32[]{:S(2)}) copy-start(bf16[64,8,16,128]{3,2,1,0:T(8,128)(2,1)} %copy.40) | copy-start | bytes 6291460
  299.6 5.3 %copy-start.7 = (f32[64,8]{0,1:T(8,128)S(1)}, f32[64,8]{0,1:T(8,128)}, u32[]{:S(2)}) copy-start(f32[64,8]{0,1:T(8,128)} %param.32) | copy-start | bytes 6148
  299.6 80.7 %all-to-all-start.2 = ((bf16[128,192,128]{2,1,0:T(8,128)(2,1)}), bf16[128,192,128]{2,1,0:T(8,128)(2,1)}, u32[]{:S(2)}, u32[]{:S(2)}) async-start(bf16[128,192,128]{2,1,0:T(8,128)(2,1)} %bitcast.185), calls=%async_computation.2 | async-start | bytes 12582912 | tf_op jit(solution)/shard_map/all_to_all | solution.py:163
Sparse Core Ops, SparseCore 0:
  10.7 54.2 all-gather.1

commit v3 on v2

--- a/solution.py
+++ b/solution.py
@@ -23,14 +23,12 @@
     rows, sub, lanes = block.shape
     gate = gate_weight[0].reshape(sub, lanes, -1)
     up = up_weight[0].reshape(sub, lanes, -1)
-    down = down_weight[0].reshape(-1, sub, lanes)
     contract = (((1, 2), (0, 1)), ((), ()))
     gated = lax.dot_general(block, gate, contract, preferred_element_type=jnp.float32)
     lifted = lax.dot_general(block, up, contract, preferred_element_type=jnp.float32)
     hidden = (jax.nn.silu(gated) * lifted).astype(jnp.bfloat16)
-    return lax.dot_general(
-        hidden, down, (((1,), (0,)), ((), ())), preferred_element_type=jnp.float32
-    ).astype(jnp.bfloat16)
+    produced = jnp.dot(hidden, down_weight[0], preferred_element_type=jnp.float32)
+    return produced.astype(jnp.bfloat16).reshape(rows, sub, lanes)
 
 
 def per_device(
@@ -59,7 +57,9 @@
     longest = prompt_keys.shape[1]
     groups_here = prompt_keys.shape[0]
     normed = rms_scale(residual_in, attention_gain)
-    piece = lax.all_gather(normed, "expert", axis=0, tiled=True)
+    expert_groups = lax.axis_size("expert")
+    copies = jnp.broadcast_to(normed[None], (expert_groups, tok_rows, width))
+    piece = lax.all_to_all(copies, "expert", 0, 0, tiled=True).reshape(-1, width)
     query_part = jnp.dot(piece, query_weight, preferred_element_type=jnp.float32).astype(
         jnp.bfloat16
     )
@@ -124,7 +124,6 @@
     attended = lax.fori_loop(0, groups_here, group_step, jnp.zeros(layout, jnp.bfloat16))
     flat_attended = attended.reshape(requests * SB, local_width)
     piece = flat_attended
-    expert_groups = lax.axis_size("expert")
     projected_out = jnp.dot(piece, output_weight, preferred_element_type=jnp.float32).astype(jnp.bfloat16)
     partials = lax.all_to_all(
         projected_out.reshape(expert_groups, tok_rows, width), "expert", 0, 0, tiled=True

time: 403 us -> 397 us (0.985)
  blocking collectives: 0 us -> 87.1 us
  waiting for transfers between devices: 255 us -> 182 us
  between operations: 14.4 us -> 0.94 us
  local copies, waits for them, and re-layouts: 42.6 us -> 33.7 us
  matrix products: 38.9 us -> 44.6 us
    all_to_all x0 -> x1, blocking collectives: none -> 87.1 us  [per_device(): arrived = lax.all_to_all(outgoing, ('dp', 'expert'), 0, 0, tiled=True)]
    all_gather x1 -> x0, waiting for transfers between devices: 54 us -> none  [per_device(): piece = lax.all_gather(normed, 'expert', axis=0, tiled=True)]
    convert_element_type x1 -> x0, local copies, waits for them, and re-layouts: 18.3 us -> none  [expert_block(): return lax.dot_general(hidden, down, (((1,), (0,)), ((), ())), preferred_...]
    all_to_all x1, waiting for transfers between devices: 71.8 us -> 60.2 us  [per_device(): lax.all_to_all(copies, 'expert', 0, 0, tiled=True).reshape(-1, width)]
    another operation x1 -> x2, local copies, waits for them, and re-layouts: 0.01 us -> 10.5 us  [the longest x1 10.5 us: per_device(): produced.reshape(devices, capacity * sub, lanes)]
    all_to_all x1, starting transfers between devices: 16.3 us -> 7.76 us  [per_device(): lax.all_to_all(copies, 'expert', 0, 0, tiled=True).reshape(-1, width)]
    all_to_all x1, waiting for transfers between devices: 54.2 us -> 46.6 us  [per_device(): lax.all_to_all(projected_out.reshape(expert_groups, tok_rows, width), 'ex...]
    all_to_all x1, starting transfers between devices: 5.17 us -> 11.6 us  [per_device(): lax.all_to_all(projected_out.reshape(expert_groups, tok_rows, width), 'ex...]
  transfers between devices with their start and end apart: 4 -> 3, of which waited for: 4 -> 3; matrix products, arithmetic and copies ran while one was open for 2% -> 1% of each run, Pallas kernels for 0% -> 0%
where the time goes in v3:
time: 397 us; the launch traced here: 396 us
  waiting for transfers between devices  182 us (46%)
  blocking collectives  87.1 us (22%)
  matrix products  44.6 us (11%)
  local copies, waits for them, and re-layouts  33.7 us (8%)
  starting transfers between devices  25 us (6%)
  other arithmetic  20.4 us (5%)
    all_to_all x1, blocking collectives, per_device(): arrived = lax.all_to_all(outgoing, ('dp', 'expert'), 0, 0, tiled=True)  87.1 us
    all_to_all x1, waiting for transfers between devices, per_device(): lax.all_to_all(produced.reshape(devices, capacity * sub, lanes), ('dp', '...  75.4 us
    all_to_all x1, waiting for transfers between devices, per_device(): lax.all_to_all(copies, 'expert', 0, 0, tiled=True).reshape(-1, width)  60.2 us
    all_to_all x1, waiting for transfers between devices, per_device(): lax.all_to_all(projected_out.reshape(expert_groups, tok_rows, width), 'ex...  46.6 us
    dot_general x1, matrix products, expert_block(): jnp.dot(hidden, down_weight[0], preferred_element_type=jnp.float32)  11.9 us
    all_to_all x1, starting transfers between devices, per_device(): lax.all_to_all(projected_out.reshape(expert_groups, tok_rows, width), 'ex...  11.6 us
    another operation x1, local copies, waits for them, and re-layouts, per_device(): produced.reshape(devices, capacity * sub, lanes)  10.5 us
    gather x1, local copies, waits for them, and re-layouts, per_device(): returned.reshape(experts, hidden_split, capacity, sub, lanes)  8.93 us
  transfers between devices with their start and end apart: 3, of which 3 were waited for; matrix products, arithmetic and copies ran while one was open for 1% of the time, Pallas kernels for 0%

profile of v3, /device:TPU:1, one launch (start us, length us, event | category | flops | bytes accessed | tf_op | source)
XLA Modules:
  0.0 396.2 jit_solution(5263146750973873830)
XLA Ops:
  3.0 2.5 broadcast_in_dim.83
  5.5 7.8 %all-to-all-start = ((bf16[16,64,2048]{2,1,0:T(8,128)(2,1)}), bf16[16,64,2048]{2,1,0:T(8,128)(2,1)}, u32[]{:S(2)}, u32[]{:S(2)}) async-start(bf16[16,64,2048]{2,1,0:T(8,128)(2,1)} %broadcast_in_dim.83), calls=%async_computation | async-start | bytes 8388608 | tf_op jit(solution)/shard_map/all_to_all | solution.py:62
  13.4 60.2 %all-to-all-done = bf16[16,64,2048]{2,1,0:T(8,128)(2,1)} async-done(((bf16[16,64,2048]{2,1,0:T(8,128)(2,1)}), bf16[16,64,2048]{2,1,0:T(8,128)(2,1)}, u32[]{:S(2)}, u32[]{:S(2)}) %all-to-all-start) | async-done | bytes 4194336 | tf_op jit(solution)/shard_map/all_to_all | solution.py:62
  73.6 3.4 convolution_convert_fusion.4
  77.0 3.6 convolution_convert_fusion.3
  80.7 3.4 convolution_convert_fusion.2
  84.5 24.7 %while.14 = (s32[]{:T(128)}, bf16[32,32,1,128]{3,1,0,2:T(8,128)(2,1)S(1)}, s32[32]{0:T(128)S(1)}, bf16[3,2048,128]{2,1,0:T(8,128)(2,1)}, s32[3]{0:T(128)S(1)}, /...) while((s32[]{:T(128)}, ...), condition=%wide.region_7.8_spmd.clone, body=%wide.region_1.7_spmd.clone.sunk | while | flops 555074688 | bytes 15133611 | solution.py:124
  90.6 2.1 fusion.105
  98.8 2.1 fusion.105
  107.1 2.1 fusion.105
  109.1 4.3 %convolution_convert_fusion.1 = bf16[1024,2048]{1,0:T(8,128)(2,1)} fusion(bf16[1024,128]{1,0:T(8,128)(2,1)S(1)} %bitcast.187, bf16[128,2048]{1,0:T(8,128)(2,1)} %param.24), kind=kOutput, calls=%fused_computation.48 | convolution fusion | flops 538968064 | bytes 4980736 | tf_op jit(solution)/shard_map/dot_general | solution.py:127
  113.4 11.6 %all-to-all-start.1 = ((bf16[16,64,2048]{2,1,0:T(8,128)(2,1)}), bf16[16,64,2048]{2,1,0:T(8,128)(2,1)}, u32[]{:S(2)}, u32[]{:S(2)}) async-start(bf16[16,64,2048]{2,1,0:T(8,128)(2,1)} %bitcast.181), calls=%async_computation.1 | async-start | bytes 8388608 | tf_op jit(solution)/shard_map/all_to_all | solution.py:128
  127.0 2.4 scatter_custom_fusion
  129.8 46.6 %all-to-all-done.1 = bf16[16,64,2048]{2,1,0:T(8,128)(2,1)} async-done(((bf16[16,64,2048]{2,1,0:T(8,128)(2,1)}), bf16[16,64,2048]{2,1,0:T(8,128)(2,1)}, u32[]{:S(2)}, u32[]{:S(2)}) %all-to-all-start.1) | async-done | bytes 4194336 | tf_op jit(solution)/shard_map/all_to_all | solution.py:128
  176.4 3.0 reduce_sum.97
  179.9 5.7 %gather_fusion = bf16[1536,16,128]{2,1,0:T(8,128)(2,1)} fusion(bf16[65,16,128]{2,1,0:T(8,128)(2,1)S(1)} %concatenate.6, s32[2048]{0:T(1024)S(1)} %pad_clamp_fusion), kind=kCustom, calls=%fused_computation | custom fusion | bytes 12589056 | tf_op jit(solution)/shard_map/gather | solution.py:157
  185.6 87.1 %all_to_all.20 = bf16[128,192,128]{2,1,0:T(8,128)(2,1)S(1)} all-to-all(bf16[128,192,128]{2,1,0:T(8,128)(2,1)} %bitcast.182), channel_id=1, replica_groups=mesh['dp'=8,'expert'=16] {'dp','expert'}, dimensions={0} | all-to-all | bytes 12582912 | tf_op jit(solution)/shard_map/all_to_all | solution.py:158
  272.7 5.1 %fusion.45 = f32[1536,512]{1,0:T(8,128)} fusion(bf16[16,128,512]{2,1,0:T(8,128)(2,1)S(1)} %bitcast.196, bf16[1536,16,128]{2,1,0:T(8,128)(2,1)S(1)} %bitcast.183), kind=kOutput, calls=%fused_computation.49 | convolution fusion | flops 3221225472 | bytes 11534336 | tf_op jit(solution)/shard_map/dot_general | solution.py:27
  277.9 11.9 %convolution_convert_fusion = bf16[1536,2048]{1,0:T(8,128)(2,1)} fusion(bf16[1,512,2048]{2,1,0:T(8,128)(2,1)} %param.35, bf16[16,128,512]{2,1,0:T(8,128)(2,1)S(1)} %bitcast.179, bf16[1536,16,128]{2,1,0:T(8,128)(2,1)} %bitcast.184, f32[1536,512]{1,0:T(8,128)} %fusion.45), kind=kOutput, calls=%fused_computation.42 | convolution fusion | flops 6450315264 | bytes 19922944 | tf_op jit(solution)/shard_map/dot_general | solution.py:30
  289.8 10.5 %reshape_reshape.3 = bf16[128,192,128]{2,1,0:T(8,128)(2,1)} reshape(bf16[1536,2048]{1,0:T(8,128)(2,1)} %convolution_convert_fusion) | data formatting | bytes 12582912 | tf_op jit(solution)/shard_map/reshape;reshape | solution.py:163
  300.2 5.6 %all-to-all-start.3 = ((bf16[128,192,128]{2,1,0:T(8,128)(2,1)}), bf16[128,192,128]{2,1,0:T(8,128)(2,1)}, u32[]{:S(2)}, u32[]{:S(2)}) async-start(bf16[128,192,128]{2,1,0:T(8,128)(2,1)} %reshape_reshape.3), calls=%async_computation.3 | async-start | bytes 12582912 | tf_op jit(solution)/shard_map/all_to_all | solution.py:162
  306.0 75.4 %all-to-all-done.3 = bf16[128,192,128]{2,1,0:T(8,128)(2,1)} async-done(((bf16[128,192,128]{2,1,0:T(8,128)(2,1)}), bf16[128,192,128]{2,1,0:T(8,128)(2,1)}, u32[]{:S(2)}, u32[]{:S(2)}) %all-to-all-start.3) | async-done | bytes 6291488 | tf_op jit(solution)/shard_map/all_to_all | solution.py:162
  381.4 8.9 %gather_fusion.1 = bf16[512,2,16,128]{3,2,1,0:T(8,128)(2,1)} fusion(bf16[64,2,12,16,128]{4,3,2,1,0:T(8,128)(2,1)} %bitcast.19, s32[512]{0:T(512)S(1)} %bitcast.180), kind=kCustom, calls=%fused_computation.1 | custom fusion | bytes 8392704 | tf_op jit(solution)/shard_map/gather | solution.py:165
  390.4 4.1 %convert_reduce_fusion.2 = f32[512,16,128]{2,1,0:T(8,128)S(1)} fusion(bf16[512,2,16,128]{3,2,1,0:T(8,128)(2,1)} %gather_fusion.1), kind=kLoop, calls=%fused_computation.41 | loop fusion | flops 3145728 | bytes 8388608 | tf_op jit(solution)/shard_map/reduce_sum | solution.py:166
  (90 shorter events, 23.5 us)
Async XLA Ops:
  0.6 277.2 %copy-start = (bf16[1,2048,512]{2,1,0:T(8,128)(2,1)S(1)}, bf16[1,2048,512]{2,1,0:T(8,128)(2,1)}, u32[]{:S(2)}) copy-start(bf16[1,2048,512]{2,1,0:T(8,128)(2,1)} %param.34) | copy-start | bytes 6291460
  5.5 7.8 %copy-start.8 = (s32[32]{0:T(128)S(1)}, s32[32]{0:T(128)}, u32[]{:S(2)}) copy-start(s32[32]{0:T(128)} %param.29) | copy-start | bytes 388
  5.5 68.1 %copy-start.10 = (bf16[2048,128]{1,0:T(8,128)(2,1)S(1)}, bf16[2048,128]{1,0:T(8,128)(2,1)}, u32[]{:S(2)}) copy-start(bf16[2048,128]{1,0:T(8,128)(2,1)} %param.21) | copy-start | bytes 1572868
  5.5 68.1 %all-to-all-start = ((bf16[16,64,2048]{2,1,0:T(8,128)(2,1)}), bf16[16,64,2048]{2,1,0:T(8,128)(2,1)}, u32[]{:S(2)}, u32[]{:S(2)}) async-start(bf16[16,64,2048]{2,1,0:T(8,128)(2,1)} %broadcast_in_dim.83), calls=%async_computation | async-start | bytes 8388608 | tf_op jit(solution)/shard_map/all_to_all | solution.py:62
  77.0 3.6 copy-start.11
  80.7 3.8 copy-start.4
  80.7 3.8 copy-start.12
  113.4 11.6 %copy-start.6 = (s32[64,8]{0,1:T(8,128)S(1)}, s32[64,8]{0,1:T(8,128)}, u32[]{:S(2)}) copy-start(s32[64,8]{0,1:T(8,128)} %param.31) | copy-start | bytes 6148
  113.4 63.0 %all-to-all-start.1 = ((bf16[16,64,2048]{2,1,0:T(8,128)(2,1)}), bf16[16,64,2048]{2,1,0:T(8,128)(2,1)}, u32[]{:S(2)}, u32[]{:S(2)}) async-start(bf16[16,64,2048]{2,1,0:T(8,128)(2,1)} %bitcast.181), calls=%async_computation.1 | async-start | bytes 8388608 | tf_op jit(solution)/shard_map/all_to_all | solution.py:128
  125.0 54.4 %copy-start.2 = (bf16[64,2048]{1,0:T(8,128)(2,1)S(1)}, bf16[64,2048]{1,0:T(8,128)(2,1)}, u32[]{:S(2)}) copy-start(bf16[64,2048]{1,0:T(8,128)(2,1)} %param.19) | copy-start | bytes 786436
  125.0 54.6 %copy-start.5 = (f32[2048]{0:T(1024)S(1)}, f32[2048]{0:T(1024)}, u32[]{:S(2)}) copy-start(f32[2048]{0:T(1024)} %param.30) | copy-start | bytes 24580
  179.4 6.1 %copy-start.3 = (bf16[64,2048]{1,0:T(8,128)(2,1)}, bf16[64,2048]{1,0:T(8,128)(2,1)S(1)}, u32[]{:S(2)}) copy-start(bf16[64,2048]{1,0:T(8,128)(2,1)S(1)} %reduce_sum.97) | copy-start | bytes 786436
  185.6 87.1 %copy-start.9 = (bf16[1,2048,512]{2,1,0:T(8,128)(2,1)S(1)}, bf16[1,2048,512]{2,1,0:T(8,128)(2,1)}, u32[]{:S(2)}) copy-start(bf16[1,2048,512]{2,1,0:T(8,128)(2,1)} %param.33) | copy-start | bytes 6291460
  272.7 5.2 %copy-start.1 = (bf16[128,192,128]{2,1,0:T(8,128)(2,1)}, bf16[128,192,128]{2,1,0:T(8,128)(2,1)S(1)}, u32[]{:S(2)}) copy-start(bf16[128,192,128]{2,1,0:T(8,128)(2,1)S(1)} %all_to_all.20) | copy-start | bytes 18874372
  300.2 5.7 %copy-start.7 = (f32[64,8]{0,1:T(8,128)S(1)}, f32[64,8]{0,1:T(8,128)}, u32[]{:S(2)}) copy-start(f32[64,8]{0,1:T(8,128)} %param.32) | copy-start | bytes 6148
  300.2 81.2 %all-to-all-start.3 = ((bf16[128,192,128]{2,1,0:T(8,128)(2,1)}), bf16[128,192,128]{2,1,0:T(8,128)(2,1)}, u32[]{:S(2)}, u32[]{:S(2)}) async-start(bf16[128,192,128]{2,1,0:T(8,128)(2,1)} %reshape_reshape.3), calls=%async_computation.3 | async-start | bytes 12582912 | tf_op jit(solution)/shard_map/all_to_all | solution.py:162

commit v4 on v3

--- a/solution.py
+++ b/solution.py
@@ -1,3 +1,5 @@
+import math
+
 import jax
 import jax.numpy as jnp
 from jax import lax
@@ -29,6 +31,33 @@
     hidden = (jax.nn.silu(gated) * lifted).astype(jnp.bfloat16)
     produced = jnp.dot(hidden, down_weight[0], preferred_element_type=jnp.float32)
     return produced.astype(jnp.bfloat16).reshape(rows, sub, lanes)
+
+
+def ring_shift(block, side, along_x, step):
+    pairs = []
+    for source in range(side * side):
+        row, column = divmod(source, side)
+        if along_x:
+            target = ((row + step) % side) * side + column
+        else:
+            target = row * side + (column + step) % side
+        pairs.append((source, target))
+    return lax.ppermute(block, "expert", pairs)
+
+
+def ring_gather(block, side, along_x):
+    assert side == 4
+    from_left = ring_shift(block, side, along_x, 1)
+    from_right = ring_shift(block, side, along_x, -1)
+    cut = block.shape[-2] // 2
+    far = jnp.concatenate(
+        [
+            ring_shift(from_left[..., :cut, :], side, along_x, 1),
+            ring_shift(from_right[..., cut:, :], side, along_x, -1),
+        ],
+        axis=-2,
+    )
+    return jnp.stack([block, from_right, far, from_left])
 
 
 def per_device(
@@ -58,16 +87,23 @@
     groups_here = prompt_keys.shape[0]
     normed = rms_scale(residual_in, attention_gain)
     expert_groups = lax.axis_size("expert")
-    copies = jnp.broadcast_to(normed[None], (expert_groups, tok_rows, width))
-    piece = lax.all_to_all(copies, "expert", 0, 0, tiled=True).reshape(-1, width)
-    query_part = jnp.dot(piece, query_weight, preferred_element_type=jnp.float32).astype(
-        jnp.bfloat16
-    )
-    key_part = jnp.dot(piece, key_weight, preferred_element_type=jnp.float32).astype(jnp.bfloat16)
-    value_part = jnp.dot(piece, value_weight, preferred_element_type=jnp.float32).astype(
-        jnp.bfloat16
-    )
-    projected = jnp.concatenate([query_part, key_part, value_part], axis=1)
+    side = math.isqrt(expert_groups)
+    half = tok_rows // 2
+    first = ring_gather(normed[:half], side, True)
+    second = ring_gather(normed[half:], side, False)
+    first = ring_gather(first, side, False)
+    second = ring_gather(second, side, True)
+    joined = jnp.concatenate([query_weight, key_weight, value_weight], axis=1)
+    first = jnp.dot(first.reshape(-1, width), joined, preferred_element_type=jnp.float32)
+    second = jnp.dot(second.reshape(-1, width), joined, preferred_element_type=jnp.float32)
+    first = jnp.swapaxes(first.astype(jnp.bfloat16).reshape(side, side, half, -1), 0, 1)
+    second = second.astype(jnp.bfloat16).reshape(side, side, half, -1)
+    relative = jnp.concatenate([first, second], axis=2)
+    place = lax.axis_index("expert")
+    offsets = jnp.arange(side, dtype=jnp.int32)
+    across = (offsets - place // side) % side
+    down = (offsets - place % side) % side
+    projected = relative[across][:, down].reshape(expert_groups * tok_rows, -1)
     layout = (requests, SB, heads_here, HD)
     queries = projected[:, :local_width].reshape(layout)
     new_keys = projected[:, local_width : 2 * local_width].reshape(layout)

time: 397 us -> 365 us (0.919)
  waiting for transfers between devices: 182 us -> 125 us
  local copies, waits for them, and re-layouts: 33.7 us -> 46.1 us
  starting transfers between devices: 25 us -> 33.4 us
  matrix products: 44.6 us -> 39.5 us
  other arithmetic: 20.4 us -> 25.2 us
  blocking collectives: 87.1 us -> 91.3 us
    all_to_all x1 -> x0, waiting for transfers between devices: 60.2 us -> none  [per_device(): lax.all_to_all(copies, 'expert', 0, 0, tiled=True).reshape(-1, width)]
    ppermute x0 -> x16, starting transfers between devices: none -> 23.1 us  [ring_shift(): return lax.ppermute(block, 'expert', pairs)]
    all_to_all x1 -> x0, starting transfers between devices: 7.76 us -> none  [per_device(): lax.all_to_all(copies, 'expert', 0, 0, tiled=True).reshape(-1, width)]
    all_to_all x1, starting transfers between devices: 11.6 us -> 4.66 us  [per_device(): lax.all_to_all(projected_out.reshape(expert_groups, tok_rows, width), 'ex...]
    ppermute x0 -> x16, waiting for transfers between devices: none -> 6.46 us  [ring_shift(): return lax.ppermute(block, 'expert', pairs)]
    unnamed x30 -> x36, local copies, waits for them, and re-layouts: 1.05 us -> 6.43 us
    dot_general x3 -> x2, matrix products: 10.5 us -> 5.33 us  [the longest x1 2.67 us: per_device(): jnp.dot(second.reshape(-1, width), joined, preferred_element_type=jnp.flo...]
    gather x0 -> x3, local copies, waits for them, and re-layouts: none -> 4.6 us  [per_device(): projected = relative[across][:, down].reshape(expert_groups * tok_rows, -1)]
  transfers between devices with their start and end apart: 3 -> 18, of which waited for: 3 -> 3; matrix products, arithmetic and copies ran while one was open for 1% -> 5% of each run, Pallas kernels for 0% -> 0%
where the time goes in v4:
time: 365 us; the launch traced here: 364 us
  waiting for transfers between devices  125 us (34%)
  blocking collectives  91.3 us (25%)
  local copies, waits for them, and re-layouts  46.1 us (13%)
  matrix products  39.5 us (11%)
  starting transfers between devices  33.4 us (9%)
  other arithmetic  25.2 us (7%)
    all_to_all x1, blocking collectives, per_device(): arrived = lax.all_to_all(outgoing, ('dp', 'expert'), 0, 0, tiled=True)  91.3 us
    all_to_all x1, waiting for transfers between devices, per_device(): lax.all_to_all(produced.reshape(devices, capacity * sub, lanes), ('dp', '...  75.4 us
    all_to_all x1, waiting for transfers between devices, per_device(): lax.all_to_all(projected_out.reshape(expert_groups, tok_rows, width), 'ex...  43.2 us
    ppermute x16, starting transfers between devices, ring_shift(): return lax.ppermute(block, 'expert', pairs)  23.1 us
    dot_general x1, matrix products, expert_block(): jnp.dot(hidden, down_weight[0], preferred_element_type=jnp.float32)  11.9 us
    another operation x1, local copies, waits for them, and re-layouts, per_device(): produced.reshape(devices, capacity * sub, lanes)  10.5 us
    gather x1, local copies, waits for them, and re-layouts, per_device(): returned.reshape(experts, hidden_split, capacity, sub, lanes)  8.94 us
  transfers between devices with their start and end apart: 18, of which 3 were waited for; matrix products, arithmetic and copies ran while one was open for 5% of the time, Pallas kernels for 0%

profile of v4, /device:TPU:1, one launch (start us, length us, event | category | flops | bytes accessed | tf_op | source)
XLA Modules:
  0.0 364.0 jit_solution(17521140683824307795)
XLA Ops:
  13.4 2.7 collective-permute-start.11
  16.3 2.7 collective-permute-start.3
  19.2 2.7 collective-permute-start.12
  22.8 2.7 collective-permute-start.4
  25.5 6.4 %collective-permute-done.13 = bf16[4,32,2048]{2,1,0:T(8,128)(2,1)S(1)} collective-permute-done((bf16[4,32,2048]{2,1,0:T(8,128)(2,1)S(1)}, bf16[4,32,2048]{2,1,0:T(8,128)(2,1)S(1)}, u32[]{:S(2)}, u32[]{:S(2)}) %collective-permute-start.13) | collective-permute-done | bytes 524320 | tf_op jit(solution)/shard_map/ppermute | solution.py:45
  34.4 2.7 collective-permute-start.15
  41.1 2.9 collective-permute-start.7
  45.4 2.7 convolution_convert_fusion.2
  49.6 2.7 convolution_convert_fusion.3
  58.4 24.7 %while.14 = (s32[]{:T(128)}, bf16[32,32,1,128]{3,1,0,2:T(8,128)(2,1)S(1)}, s32[32]{0:T(128)S(1)}, bf16[3,2048,128]{2,1,0:T(8,128)(2,1)}, s32[3]{0:T(128)S(1)}, /...) while((s32[]{:T(128)}, ...), condition=%wide.region_7.8_spmd.clone, body=%wide.region_1.7_spmd.clone.sunk | while | flops 555074688 | bytes 15133611 | solution.py:160
  83.0 4.3 %convolution_convert_fusion.1 = bf16[1024,2048]{1,0:T(8,128)(2,1)} fusion(bf16[1024,128]{1,0:T(8,128)(2,1)S(1)} %bitcast.225, bf16[128,2048]{1,0:T(8,128)(2,1)} %param.24), kind=kOutput, calls=%fused_computation.50 | convolution fusion | flops 538968064 | bytes 4980736 | tf_op jit(solution)/shard_map/dot_general | solution.py:163
  87.3 4.7 %all-to-all-start = ((bf16[16,64,2048]{2,1,0:T(8,128)(2,1)}), bf16[16,64,2048]{2,1,0:T(8,128)(2,1)}, u32[]{:S(2)}, u32[]{:S(2)}) async-start(bf16[16,64,2048]{2,1,0:T(8,128)(2,1)} %bitcast.214), calls=%async_computation | async-start | bytes 8388608 | tf_op jit(solution)/shard_map/all_to_all | solution.py:164
  94.0 2.4 scatter_custom_fusion
  96.8 43.2 %all-to-all-done = bf16[16,64,2048]{2,1,0:T(8,128)(2,1)} async-done(((bf16[16,64,2048]{2,1,0:T(8,128)(2,1)}), bf16[16,64,2048]{2,1,0:T(8,128)(2,1)}, u32[]{:S(2)}, u32[]{:S(2)}) %all-to-all-start) | async-done | bytes 4194336 | tf_op jit(solution)/shard_map/all_to_all | solution.py:164
  140.0 3.0 reduce_sum.97
  143.5 5.7 %gather_fusion.2 = bf16[1536,16,128]{2,1,0:T(8,128)(2,1)} fusion(bf16[65,16,128]{2,1,0:T(8,128)(2,1)S(1)} %concatenate.30, s32[2048]{0:T(1024)S(1)} %pad_clamp_fusion), kind=kCustom, calls=%fused_computation.2 | custom fusion | bytes 12589056 | tf_op jit(solution)/shard_map/gather | solution.py:193
  149.2 91.3 %all_to_all.15 = bf16[128,192,128]{2,1,0:T(8,128)(2,1)S(1)} all-to-all(bf16[128,192,128]{2,1,0:T(8,128)(2,1)} %bitcast.215), channel_id=1, replica_groups=mesh['dp'=8,'expert'=16] {'dp','expert'}, dimensions={0} | all-to-all | bytes 12582912 | tf_op jit(solution)/shard_map/all_to_all | solution.py:194
  240.5 5.1 %fusion.45 = f32[1536,512]{1,0:T(8,128)} fusion(bf16[16,128,512]{2,1,0:T(8,128)(2,1)S(1)} %bitcast.241, bf16[1536,16,128]{2,1,0:T(8,128)(2,1)S(1)} %bitcast.216), kind=kOutput, calls=%fused_computation.51 | convolution fusion | flops 3221225472 | bytes 11534336 | tf_op jit(solution)/shard_map/dot_general | solution.py:29
  245.7 11.9 %convolution_convert_fusion = bf16[1536,2048]{1,0:T(8,128)(2,1)} fusion(bf16[1,512,2048]{2,1,0:T(8,128)(2,1)} %param.35, bf16[16,128,512]{2,1,0:T(8,128)(2,1)S(1)} %bitcast.212, bf16[1536,16,128]{2,1,0:T(8,128)(2,1)} %bitcast.217, f32[1536,512]{1,0:T(8,128)} %fusion.45), kind=kOutput, calls=%fused_computation.44 | convolution fusion | flops 6450315264 | bytes 19922944 | tf_op jit(solution)/shard_map/dot_general | solution.py:32
  257.6 10.5 %reshape_reshape.3 = bf16[128,192,128]{2,1,0:T(8,128)(2,1)} reshape(bf16[1536,2048]{1,0:T(8,128)(2,1)} %convolution_convert_fusion) | data formatting | bytes 12582912 | tf_op jit(solution)/shard_map/reshape;reshape | solution.py:199
  268.0 5.7 %all-to-all-start.2 = ((bf16[128,192,128]{2,1,0:T(8,128)(2,1)}), bf16[128,192,128]{2,1,0:T(8,128)(2,1)}, u32[]{:S(2)}, u32[]{:S(2)}) async-start(bf16[128,192,128]{2,1,0:T(8,128)(2,1)} %reshape_reshape.3), calls=%async_computation.2 | async-start | bytes 12582912 | tf_op jit(solution)/shard_map/all_to_all | solution.py:198
  273.8 75.4 %all-to-all-done.2 = bf16[128,192,128]{2,1,0:T(8,128)(2,1)} async-done(((bf16[128,192,128]{2,1,0:T(8,128)(2,1)}), bf16[128,192,128]{2,1,0:T(8,128)(2,1)}, u32[]{:S(2)}, u32[]{:S(2)}) %all-to-all-start.2) | async-done | bytes 6291488 | tf_op jit(solution)/shard_map/all_to_all | solution.py:198
  349.3 8.9 %gather_fusion.3 = bf16[512,2,16,128]{3,2,1,0:T(8,128)(2,1)} fusion(bf16[64,2,12,16,128]{4,3,2,1,0:T(8,128)(2,1)} %bitcast.43, s32[512]{0:T(512)S(1)} %bitcast.213), kind=kCustom, calls=%fused_computation.3 | custom fusion | bytes 8392704 | tf_op jit(solution)/shard_map/gather | solution.py:201
  358.2 4.1 %convert_reduce_fusion.2 = f32[512,16,128]{2,1,0:T(8,128)S(1)} fusion(bf16[512,2,16,128]{3,2,1,0:T(8,128)(2,1)} %gather_fusion.3), kind=kLoop, calls=%fused_computation.43 | loop fusion | flops 3145728 | bytes 8388608 | tf_op jit(solution)/shard_map/reduce_sum | solution.py:202
  (150 shorter events, 56.3 us)
Async XLA Ops:
  0.6 245.0 %copy-start = (bf16[1,2048,512]{2,1,0:T(8,128)(2,1)S(1)}, bf16[1,2048,512]{2,1,0:T(8,128)(2,1)}, u32[]{:S(2)}) copy-start(bf16[1,2048,512]{2,1,0:T(8,128)(2,1)} %param.34) | copy-start | bytes 6291460
  3.1 10.2 %collective-permute-start.9 = (bf16[32,2048]{1,0:T(8,128)(2,1)S(1)}, bf16[32,2048]{1,0:T(8,128)(2,1)S(1)}, u32[]{:S(2)}, u32[]{:S(2)}) collective-permute-start(bf16[32,2048]{1,0:T(8,128)(2,1)S(1)} %get-tuple-element.221), channel_id=1, source_target_pairs={{0,1},{1,2},{2,3},{3,0},{4,5},{5,6},{6,7},{7,4},{8,9},{9,10},{10,1... | collective-permute-start | bytes 393224 | tf_op jit(solution)/shard_map/ppermute | solution.py:45
  5.2 8.1 %collective-permute-start.8 = (bf16[32,2048]{1,0:T(8,128)(2,1)S(1)}, bf16[32,2048]{1,0:T(8,128)(2,1)S(1)}, u32[]{:S(2)}, u32[]{:S(2)}) collective-permute-start(bf16[32,2048]{1,0:T(8,128)(2,1)S(1)} %get-tuple-element.221), channel_id=1, source_target_pairs={{0,3},{1,0},{2,1},{3,2},{4,7},{5,4},{6,5},{7,6},{8,11},{9,8},{10,9... | collective-permute-start | bytes 393224 | tf_op jit(solution)/shard_map/ppermute | solution.py:45
  6.8 18.7 %copy-start.12 = (s32[32]{0:T(128)S(1)}, s32[32]{0:T(128)}, u32[]{:S(2)}) copy-start(s32[32]{0:T(128)} %param.29) | copy-start | bytes 388
  6.8 9.4 %collective-permute-start.1 = (bf16[32,2048]{1,0:T(8,128)(2,1)S(1)}, bf16[32,2048]{1,0:T(8,128)(2,1)S(1)}, u32[]{:S(2)}, u32[]{:S(2)}) collective-permute-start(bf16[32,2048]{1,0:T(8,128)(2,1)S(1)} %get-tuple-element.222), channel_id=1, source_target_pairs={{0,4},{1,5},{2,6},{3,7},{4,8},{5,9},{6,10},{7,11},{8,12},{9,13},{1... | collective-permute-start | bytes 393224 | tf_op jit(solution)/shard_map/ppermute | solution.py:45
  8.0 8.3 %collective-permute-start = (bf16[32,2048]{1,0:T(8,128)(2,1)S(1)}, bf16[32,2048]{1,0:T(8,128)(2,1)S(1)}, u32[]{:S(2)}, u32[]{:S(2)}) collective-permute-start(bf16[32,2048]{1,0:T(8,128)(2,1)S(1)} %get-tuple-element.222), channel_id=1, source_target_pairs={{0,12},{1,13},{2,14},{3,15},{4,0},{5,1},{6,2},{7,3},{8,4},{9,5},{1... | collective-permute-start | bytes 393224 | tf_op jit(solution)/shard_map/ppermute | solution.py:45
  13.3 5.7 %collective-permute-start.10 = (bf16[16,2048]{1,0:T(8,128)(2,1)S(1)}, bf16[16,2048]{1,0:T(8,128)(2,1)S(1)}, u32[]{:S(2)}, u32[]{:S(2)}) collective-permute-start(bf16[16,2048]{1,0:T(8,128)(2,1)S(1)} %slice.74), channel_id=1, source_target_pairs={{0,1},{1,2},{2,3},{3,0},{4,5},{5,6},{6,7},{7,4},{8,9},{9,10},{10,1... | collective-permute-start | bytes 196616 | tf_op jit(solution)/shard_map/ppermute | solution.py:45
  13.4 5.6 %collective-permute-start.11 = (bf16[16,2048]{1,0:T(8,128)(2,1)S(1)}, bf16[16,2048]{1,0:T(8,128)(2,1)S(1)}, u32[]{:S(2)}, u32[]{:S(2)}) collective-permute-start(bf16[16,2048]{1,0:T(8,128)(2,1)S(1)} %slice.75), channel_id=1, source_target_pairs={{0,3},{1,0},{2,1},{3,2},{4,7},{5,4},{6,5},{7,6},{8,11},{9,8},{10,9... | collective-permute-start | bytes 196616 | tf_op jit(solution)/shard_map/ppermute | solution.py:45
  16.2 5.7 %collective-permute-start.2 = (bf16[16,2048]{1,0:T(8,128)(2,1)S(1)}, bf16[16,2048]{1,0:T(8,128)(2,1)S(1)}, u32[]{:S(2)}, u32[]{:S(2)}) collective-permute-start(bf16[16,2048]{1,0:T(8,128)(2,1)S(1)} %slice.69), channel_id=1, source_target_pairs={{0,4},{1,5},{2,6},{3,7},{4,8},{5,9},{6,10},{7,11},{8,12},{9,13},{1... | collective-permute-start | bytes 196616 | tf_op jit(solution)/shard_map/ppermute | solution.py:45
  16.3 5.6 %collective-permute-start.3 = (bf16[16,2048]{1,0:T(8,128)(2,1)S(1)}, bf16[16,2048]{1,0:T(8,128)(2,1)S(1)}, u32[]{:S(2)}, u32[]{:S(2)}) collective-permute-start(bf16[16,2048]{1,0:T(8,128)(2,1)S(1)} %slice.70), channel_id=1, source_target_pairs={{0,12},{1,13},{2,14},{3,15},{4,0},{5,1},{6,2},{7,3},{8,4},{9,5},{1... | collective-permute-start | bytes 196616 | tf_op jit(solution)/shard_map/ppermute | solution.py:45
  19.1 12.8 %collective-permute-start.13 = (bf16[4,32,2048]{2,1,0:T(8,128)(2,1)S(1)}, bf16[4,32,2048]{2,1,0:T(8,128)(2,1)S(1)}, u32[]{:S(2)}, u32[]{:S(2)}) collective-permute-start(bf16[4,32,2048]{2,1,0:T(8,128)(2,1)S(1)} %get-tuple-element.218), channel_id=1, source_target_pairs={{0,4},{1,5},{2,6},{3,7},{4,8},{5,9},{6,10},{7,11},{8,12},{9,13},{1... | collective-permute-start | bytes 1572872 | tf_op jit(solution)/shard_map/ppermute | solution.py:45
  19.2 13.7 %collective-permute-start.12 = (bf16[4,32,2048]{2,1,0:T(8,128)(2,1)S(1)}, bf16[4,32,2048]{2,1,0:T(8,128)(2,1)S(1)}, u32[]{:S(2)}, u32[]{:S(2)}) collective-permute-start(bf16[4,32,2048]{2,1,0:T(8,128)(2,1)S(1)} %get-tuple-element.218), channel_id=1, source_target_pairs={{0,12},{1,13},{2,14},{3,15},{4,0},{5,1},{6,2},{7,3},{8,4},{9,5},{1... | collective-permute-start | bytes 1572872 | tf_op jit(solution)/shard_map/ppermute | solution.py:45
  22.8 16.3 %collective-permute-start.5 = (bf16[4,32,2048]{2,1,0:T(8,128)(2,1)}, bf16[4,32,2048]{2,1,0:T(8,128)(2,1)}, u32[]{:S(2)}, u32[]{:S(2)}) collective-permute-start(bf16[4,32,2048]{2,1,0:T(8,128)(2,1)} %get-tuple-element.216), channel_id=1, source_target_pairs={{0,1},{1,2},{2,3},{3,0},{4,5},{5,6},{6,7},{7,4},{8,9},{9,10},{10,1... | collective-permute-start | bytes 1572872 | tf_op jit(solution)/shard_map/ppermute | solution.py:45
  22.8 17.3 %collective-permute-start.4 = (bf16[4,32,2048]{2,1,0:T(8,128)(2,1)}, bf16[4,32,2048]{2,1,0:T(8,128)(2,1)}, u32[]{:S(2)}, u32[]{:S(2)}) collective-permute-start(bf16[4,32,2048]{2,1,0:T(8,128)(2,1)} %get-tuple-element.216), channel_id=1, source_target_pairs={{0,3},{1,0},{2,1},{3,2},{4,7},{5,4},{6,5},{7,6},{8,11},{9,8},{10,9... | collective-permute-start | bytes 1572872 | tf_op jit(solution)/shard_map/ppermute | solution.py:45
  32.8 11.3 %collective-permute-start.14 = (bf16[4,16,2048]{2,1,0:T(8,128)(2,1)S(1)}, bf16[4,16,2048]{2,1,0:T(8,128)(2,1)}, u32[]{:S(2)}, u32[]{:S(2)}) collective-permute-start(bf16[4,16,2048]{2,1,0:T(8,128)(2,1)S(1)} %slice.76), channel_id=1, source_target_pairs={{0,4},{1,5},{2,6},{3,7},{4,8},{5,9},{6,10},{7,11},{8,12},{9,13},{1... | collective-permute-start | bytes 786440 | tf_op jit(solution)/shard_map/ppermute | solution.py:45
  34.4 9.6 %collective-permute-start.15 = (bf16[4,16,2048]{2,1,0:T(8,128)(2,1)}, bf16[4,16,2048]{2,1,0:T(8,128)(2,1)}, u32[]{:S(2)}, u32[]{:S(2)}) collective-permute-start(bf16[4,16,2048]{2,1,0:T(8,128)(2,1)} %slice.77), channel_id=1, source_target_pairs={{0,12},{1,13},{2,14},{3,15},{4,0},{5,1},{6,2},{7,3},{8,4},{9,5},{1... | collective-permute-start | bytes 786440 | tf_op jit(solution)/shard_map/ppermute | solution.py:45
  37.0 8.0 %copy-start.7 = (bf16[4,32,2048]{2,1,0:T(8,128)(2,1)S(1)}, bf16[4,32,2048]{2,1,0:T(8,128)(2,1)}, u32[]{:S(2)}) copy-start(bf16[4,32,2048]{2,1,0:T(8,128)(2,1)} %copy-done.6) | copy-start | bytes 1572868
  40.0 8.0 %collective-permute-start.6 = (bf16[4,16,2048]{2,1,0:T(8,128)(2,1)S(1)}, bf16[4,16,2048]{2,1,0:T(8,128)(2,1)S(1)}, u32[]{:S(2)}, u32[]{:S(2)}) collective-permute-start(bf16[4,16,2048]{2,1,0:T(8,128)(2,1)S(1)} %slice.71), channel_id=1, source_target_pairs={{0,1},{1,2},{2,3},{3,0},{4,5},{5,6},{6,7},{7,4},{8,9},{9,10},{10,1... | collective-permute-start | bytes 786440 | tf_op jit(solution)/shard_map/ppermute | solution.py:45
  41.1 7.0 %collective-permute-start.7 = (bf16[4,16,2048]{2,1,0:T(8,128)(2,1)S(1)}, bf16[4,16,2048]{2,1,0:T(8,128)(2,1)S(1)}, u32[]{:S(2)}, u32[]{:S(2)}) collective-permute-start(bf16[4,16,2048]{2,1,0:T(8,128)(2,1)S(1)} %slice.72), channel_id=1, source_target_pairs={{0,3},{1,0},{2,1},{3,2},{4,7},{5,4},{6,5},{7,6},{8,11},{9,8},{10,9... | collective-permute-start | bytes 786440 | tf_op jit(solution)/shard_map/ppermute | solution.py:45
  87.3 52.7 %all-to-all-start = ((bf16[16,64,2048]{2,1,0:T(8,128)(2,1)}), bf16[16,64,2048]{2,1,0:T(8,128)(2,1)}, u32[]{:S(2)}, u32[]{:S(2)}) async-start(bf16[16,64,2048]{2,1,0:T(8,128)(2,1)} %bitcast.214), calls=%async_computation | async-start | bytes 8388608 | tf_op jit(solution)/shard_map/all_to_all | solution.py:164
  92.0 51.0 %copy-start.2 = (bf16[64,2048]{1,0:T(8,128)(2,1)S(1)}, bf16[64,2048]{1,0:T(8,128)(2,1)}, u32[]{:S(2)}) copy-start(bf16[64,2048]{1,0:T(8,128)(2,1)} %param.19) | copy-start | bytes 786436
  92.0 51.2 %copy-start.9 = (f32[2048]{0:T(1024)S(1)}, f32[2048]{0:T(1024)}, u32[]{:S(2)}) copy-start(f32[2048]{0:T(1024)} %param.30) | copy-start | bytes 24580
  149.2 91.3 %copy-start.13 = (bf16[1,2048,512]{2,1,0:T(8,128)(2,1)S(1)}, bf16[1,2048,512]{2,1,0:T(8,128)(2,1)}, u32[]{:S(2)}) copy-start(bf16[1,2048,512]{2,1,0:T(8,128)(2,1)} %param.33) | copy-start | bytes 6291460
  268.0 81.2 %all-to-all-start.2 = ((bf16[128,192,128]{2,1,0:T(8,128)(2,1)}), bf16[128,192,128]{2,1,0:T(8,128)(2,1)}, u32[]{:S(2)}, u32[]{:S(2)}) async-start(bf16[128,192,128]{2,1,0:T(8,128)(2,1)} %reshape_reshape.3), calls=%async_computation.2 | async-start | bytes 12582912 | tf_op jit(solution)/shard_map/all_to_all | solution.py:198
  (9 other events, 37.8 us)

commit v5 on v4

--- a/solution.py
+++ b/solution.py
@@ -58,6 +58,19 @@
         axis=-2,
     )
     return jnp.stack([block, from_right, far, from_left])
+
+
+def ring_reduce(relative, side, along_x):
+    assert side == 4
+    cut = relative.shape[-2] // 2
+    far = relative[2].astype(jnp.bfloat16)
+    came_left = ring_shift(far[..., :cut, :], side, along_x, 1).astype(jnp.float32)
+    came_right = ring_shift(far[..., cut:, :], side, along_x, -1).astype(jnp.float32)
+    rightward = jnp.concatenate([relative[1][..., :cut, :] + came_left, relative[1][..., cut:, :]], axis=-2)
+    leftward = jnp.concatenate([relative[3][..., :cut, :], relative[3][..., cut:, :] + came_right], axis=-2)
+    from_left = ring_shift(rightward.astype(jnp.bfloat16), side, along_x, 1)
+    from_right = ring_shift(leftward.astype(jnp.bfloat16), side, along_x, -1)
+    return relative[0] + from_left.astype(jnp.float32) + from_right.astype(jnp.float32)
 
 
 def per_device(
@@ -158,13 +171,19 @@
         return lax.dynamic_update_slice_in_dim(attended, merged, start, 0)
 
     attended = lax.fori_loop(0, groups_here, group_step, jnp.zeros(layout, jnp.bfloat16))
-    flat_attended = attended.reshape(requests * SB, local_width)
-    piece = flat_attended
-    projected_out = jnp.dot(piece, output_weight, preferred_element_type=jnp.float32).astype(jnp.bfloat16)
-    partials = lax.all_to_all(
-        projected_out.reshape(expert_groups, tok_rows, width), "expert", 0, 0, tiled=True
-    )
-    attention_update = jnp.sum(partials.astype(jnp.float32), axis=0).astype(jnp.bfloat16)
+    owners = attended.reshape(side, side, tok_rows, local_width)
+    ahead_x = (offsets + place // side) % side
+    ahead_y = (offsets + place % side) % side
+    owners = owners[ahead_x][:, ahead_y]
+    first = owners[:, :, :half].reshape(-1, local_width)
+    second = jnp.swapaxes(owners[:, :, half:], 0, 1).reshape(-1, local_width)
+    first = jnp.dot(first, output_weight, preferred_element_type=jnp.float32)
+    second = jnp.dot(second, output_weight, preferred_element_type=jnp.float32)
+    first = ring_reduce(first.reshape(side, side, half, width), side, True)
+    second = ring_reduce(second.reshape(side, side, half, width), side, False)
+    first = ring_reduce(first, side, False)
+    second = ring_reduce(second, side, True)
+    attention_update = jnp.concatenate([first, second], axis=0).astype(jnp.bfloat16)
     expert_input = rms_scale(
         residual_in.astype(jnp.float32) + attention_update.astype(jnp.float32), expert_gain
     )

time: 365 us -> 353 us (0.967)
  waiting for transfers between devices: 125 us -> 89.1 us
  starting transfers between devices: 33.4 us -> 53 us
  matrix products: 39.5 us -> 34.8 us
  blocking collectives: 91.3 us -> 95.4 us
    all_to_all x1 -> x0, waiting for transfers between devices: 43.2 us -> none  [per_device(): lax.all_to_all(projected_out.reshape(expert_groups, tok_rows, width), 'ex...]
    ppermute x16 -> x32, starting transfers between devices: 23.1 us -> 47.1 us  [ring_shift(): return lax.ppermute(block, 'expert', pairs)]
    ppermute x16 -> x32, waiting for transfers between devices: 6.46 us -> 13.7 us  [ring_shift(): return lax.ppermute(block, 'expert', pairs)]
    all_to_all x1 -> x0, starting transfers between devices: 4.66 us -> none  [per_device(): lax.all_to_all(projected_out.reshape(expert_groups, tok_rows, width), 'ex...]
    all_to_all x1, blocking collectives: 91.3 us -> 95.4 us  [per_device(): arrived = lax.all_to_all(outgoing, ('dp', 'expert'), 0, 0, tiled=True)]
  transfers between devices with their start and end apart: 18 -> 33, of which waited for: 3 -> 9; matrix products, arithmetic and copies ran while one was open for 5% -> 6% of each run, Pallas kernels for 0% -> 0%
where the time goes in v5:
time: 353 us; the launch traced here: 352 us
  blocking collectives  95.4 us (27%)
  waiting for transfers between devices  89.1 us (25%)
  starting transfers between devices  53 us (15%)
  local copies, waits for them, and re-layouts  49.6 us (14%)
  matrix products  34.8 us (10%)
  other arithmetic  26.2 us (7%)
    all_to_all x1, blocking collectives, per_device(): arrived = lax.all_to_all(outgoing, ('dp', 'expert'), 0, 0, tiled=True)  95.4 us
    all_to_all x1, waiting for transfers between devices, per_device(): lax.all_to_all(produced.reshape(devices, capacity * sub, lanes), ('dp', '...  75.4 us
    ppermute x32, starting transfers between devices, ring_shift(): return lax.ppermute(block, 'expert', pairs)  47.1 us
    ppermute x32, waiting for transfers between devices, ring_shift(): return lax.ppermute(block, 'expert', pairs)  13.7 us
    dot_general x1, matrix products, expert_block(): jnp.dot(hidden, down_weight[0], preferred_element_type=jnp.float32)  11.9 us
    another operation x1, local copies, waits for them, and re-layouts, per_device(): produced.reshape(devices, capacity * sub, lanes)  10.5 us
    gather x1, local copies, waits for them, and re-layouts, per_device(): returned.reshape(experts, hidden_split, capacity, sub, lanes)  9.01 us
  transfers between devices with their start and end apart: 33, of which 9 were waited for; matrix products, arithmetic and copies ran while one was open for 6% of the time, Pallas kernels for 0%

profile of v5, /device:TPU:1, one launch (start us, length us, event | category | flops | bytes accessed | tf_op | source)
XLA Modules:
  0.0 351.6 jit_solution(3088730257637515952)
XLA Ops:
  24.5 2.7 collective-permute-start.3
  28.3 2.7 collective-permute-start.12
  31.9 2.7 collective-permute-start.4
  35.3 5.1 %collective-permute-done.13 = bf16[4,32,2048]{2,1,0:T(8,128)(2,1)S(1)} collective-permute-done((bf16[4,32,2048]{2,1,0:T(8,128)(2,1)S(1)}, bf16[4,32,2048]{2,1,0:T(8,128)(2,1)S(1)}, u32[]{:S(2)}, u32[]{:S(2)}) %collective-permute-start.13) | collective-permute-done | bytes 524320 | tf_op jit(solution)/shard_map/ppermute | solution.py:45
  42.8 2.7 collective-permute-start.15
  49.6 2.9 collective-permute-start.7
  62.8 24.7 %while.14 = (s32[]{:T(128)}, bf16[32,32,1,128]{3,1,0,2:T(8,128)(2,1)S(1)}, s32[32]{0:T(128)S(1)}, bf16[3,2048,128]{2,1,0:T(8,128)(2,1)}, s32[3]{0:T(128)S(1)}, /...) while((s32[]{:T(128)}, ...), condition=%wide.region_7.8_spmd.clone, body=%wide.region_1.7_spmd.clone.sunk | while | flops 555074688 | bytes 15133611 | solution.py:173
  93.0 2.7 collective-permute-start.18
  95.9 3.2 collective-permute-start.26
  99.7 2.7 collective-permute-start.19
  103.3 2.9 collective-permute-start.27
  106.3 4.6 %collective-permute-done.17 = bf16[4,32,2048]{2,1,0:T(8,128)(2,1)S(1)} collective-permute-done((bf16[4,32,2048]{2,1,0:T(8,128)(2,1)S(1)}, bf16[4,32,2048]{2,1,0:T(8,128)(2,1)S(1)}, u32[]{:S(2)}, u32[]{:S(2)}) %collective-permute-start.17) | collective-permute-done | bytes 524320 | tf_op jit(solution)/shard_map/ppermute | solution.py:45
  111.3 3.5 collective-permute-start.22
  115.2 2.7 collective-permute-start.30
  121.3 2.7 collective-permute-start.31
  126.8 5.8 %gather_fusion.4 = bf16[1536,16,128]{2,1,0:T(8,128)(2,1)} fusion(bf16[65,16,128]{2,1,0:T(8,128)(2,1)S(1)} %concatenate.75, s32[2048]{0:T(1024)S(1)} %pad_clamp_fusion), kind=kCustom, calls=%fused_computation.4 | custom fusion | bytes 12589056 | tf_op jit(solution)/shard_map/gather | solution.py:212
  132.6 95.4 %all_to_all.10 = bf16[128,192,128]{2,1,0:T(8,128)(2,1)S(1)} all-to-all(bf16[128,192,128]{2,1,0:T(8,128)(2,1)} %bitcast.288), channel_id=1, replica_groups=mesh['dp'=8,'expert'=16] {'dp','expert'}, dimensions={0} | all-to-all | bytes 12582912 | tf_op jit(solution)/shard_map/all_to_all | solution.py:213
  228.0 5.1 %fusion.45 = f32[1536,512]{1,0:T(8,128)} fusion(bf16[16,128,512]{2,1,0:T(8,128)(2,1)S(1)} %bitcast.328, bf16[1536,16,128]{2,1,0:T(8,128)(2,1)S(1)} %bitcast.289), kind=kOutput, calls=%fused_computation.52 | convolution fusion | flops 3221225472 | bytes 11534336 | tf_op jit(solution)/shard_map/dot_general | solution.py:29
  233.1 11.9 %convolution_convert_fusion = bf16[1536,2048]{1,0:T(8,128)(2,1)} fusion(bf16[1,512,2048]{2,1,0:T(8,128)(2,1)} %param.35, bf16[16,128,512]{2,1,0:T(8,128)(2,1)S(1)} %bitcast.286, bf16[1536,16,128]{2,1,0:T(8,128)(2,1)} %bitcast.290, f32[1536,512]{1,0:T(8,128)} %fusion.45), kind=kOutput, calls=%fused_computation.46 | convolution fusion | flops 6450315264 | bytes 19922944 | tf_op jit(solution)/shard_map/dot_general | solution.py:32
  245.0 10.5 %reshape_reshape.3 = bf16[128,192,128]{2,1,0:T(8,128)(2,1)} reshape(bf16[1536,2048]{1,0:T(8,128)(2,1)} %convolution_convert_fusion) | data formatting | bytes 12582912 | tf_op jit(solution)/shard_map/reshape;reshape | solution.py:218
  255.5 5.9 %all-to-all-start.1 = ((bf16[128,192,128]{2,1,0:T(8,128)(2,1)}), bf16[128,192,128]{2,1,0:T(8,128)(2,1)}, u32[]{:S(2)}, u32[]{:S(2)}) async-start(bf16[128,192,128]{2,1,0:T(8,128)(2,1)} %reshape_reshape.3), calls=%async_computation.1 | async-start | bytes 12582912 | tf_op jit(solution)/shard_map/all_to_all | solution.py:217
  261.5 75.4 %all-to-all-done.1 = bf16[128,192,128]{2,1,0:T(8,128)(2,1)} async-done(((bf16[128,192,128]{2,1,0:T(8,128)(2,1)}), bf16[128,192,128]{2,1,0:T(8,128)(2,1)}, u32[]{:S(2)}, u32[]{:S(2)}) %all-to-all-start.1) | async-done | bytes 6291488 | tf_op jit(solution)/shard_map/all_to_all | solution.py:217
  337.0 9.0 %gather_fusion.5 = bf16[512,2,16,128]{3,2,1,0:T(8,128)(2,1)} fusion(bf16[64,2,12,16,128]{4,3,2,1,0:T(8,128)(2,1)} %bitcast.70, s32[512]{0:T(512)S(1)} %bitcast.287), kind=kCustom, calls=%fused_computation.5 | custom fusion | bytes 8392704 | tf_op jit(solution)/shard_map/gather | solution.py:220
  346.0 4.0 %convert_reduce_fusion.2 = f32[512,16,128]{2,1,0:T(8,128)S(1)} fusion(bf16[512,2,16,128]{3,2,1,0:T(8,128)(2,1)} %gather_fusion.5), kind=kLoop, calls=%fused_computation.45 | loop fusion | flops 3145728 | bytes 8388608 | tf_op jit(solution)/shard_map/reduce_sum | solution.py:221
  (219 shorter events, 81.2 us)
Async XLA Ops:
  3.8 16.9 %collective-permute-start.9 = (bf16[32,2048]{1,0:T(8,128)(2,1)}, bf16[32,2048]{1,0:T(8,128)(2,1)S(1)}, u32[]{:S(2)}, u32[]{:S(2)}) collective-permute-start(bf16[32,2048]{1,0:T(8,128)(2,1)} %get-tuple-element.251), channel_id=1, source_target_pairs={{0,1},{1,2},{2,3},{3,0},{4,5},{5,6},{6,7},{7,4},{8,9},{9,10},{10,1... | collective-permute-start | bytes 393224 | tf_op jit(solution)/shard_map/ppermute | solution.py:45
  5.9 15.0 %collective-permute-start.8 = (bf16[32,2048]{1,0:T(8,128)(2,1)}, bf16[32,2048]{1,0:T(8,128)(2,1)}, u32[]{:S(2)}, u32[]{:S(2)}) collective-permute-start(bf16[32,2048]{1,0:T(8,128)(2,1)} %get-tuple-element.251), channel_id=1, source_target_pairs={{0,3},{1,0},{2,1},{3,2},{4,7},{5,4},{6,5},{7,6},{8,11},{9,8},{10,9... | collective-permute-start | bytes 393224 | tf_op jit(solution)/shard_map/ppermute | solution.py:45
  7.3 17.0 %collective-permute-start.1 = (bf16[32,2048]{1,0:T(8,128)(2,1)}, bf16[32,2048]{1,0:T(8,128)(2,1)S(1)}, u32[]{:S(2)}, u32[]{:S(2)}) collective-permute-start(bf16[32,2048]{1,0:T(8,128)(2,1)} %get-tuple-element.252), channel_id=1, source_target_pairs={{0,4},{1,5},{2,6},{3,7},{4,8},{5,9},{6,10},{7,11},{8,12},{9,13},{1... | collective-permute-start | bytes 393224 | tf_op jit(solution)/shard_map/ppermute | solution.py:45
  8.5 15.9 %collective-permute-start = (bf16[32,2048]{1,0:T(8,128)(2,1)}, bf16[32,2048]{1,0:T(8,128)(2,1)S(1)}, u32[]{:S(2)}, u32[]{:S(2)}) collective-permute-start(bf16[32,2048]{1,0:T(8,128)(2,1)} %get-tuple-element.252), channel_id=1, source_target_pairs={{0,12},{1,13},{2,14},{3,15},{4,0},{5,1},{6,2},{7,3},{8,4},{9,5},{1... | collective-permute-start | bytes 393224 | tf_op jit(solution)/shard_map/ppermute | solution.py:45
  24.4 6.6 %collective-permute-start.2 = (bf16[16,2048]{1,0:T(8,128)(2,1)S(1)}, bf16[16,2048]{1,0:T(8,128)(2,1)S(1)}, u32[]{:S(2)}, u32[]{:S(2)}) collective-permute-start(bf16[16,2048]{1,0:T(8,128)(2,1)S(1)} %slice.311), channel_id=1, source_target_pairs={{0,4},{1,5},{2,6},{3,7},{4,8},{5,9},{6,10},{7,11},{8,12},{9,13},{1... | collective-permute-start | bytes 196616 | tf_op jit(solution)/shard_map/ppermute | solution.py:45
  24.5 6.5 %collective-permute-start.3 = (bf16[16,2048]{1,0:T(8,128)(2,1)S(1)}, bf16[16,2048]{1,0:T(8,128)(2,1)S(1)}, u32[]{:S(2)}, u32[]{:S(2)}) collective-permute-start(bf16[16,2048]{1,0:T(8,128)(2,1)S(1)} %slice.312), channel_id=1, source_target_pairs={{0,12},{1,13},{2,14},{3,15},{4,0},{5,1},{6,2},{7,3},{8,4},{9,5},{1... | collective-permute-start | bytes 196616 | tf_op jit(solution)/shard_map/ppermute | solution.py:45
  28.2 12.1 %collective-permute-start.13 = (bf16[4,32,2048]{2,1,0:T(8,128)(2,1)S(1)}, bf16[4,32,2048]{2,1,0:T(8,128)(2,1)S(1)}, u32[]{:S(2)}, u32[]{:S(2)}) collective-permute-start(bf16[4,32,2048]{2,1,0:T(8,128)(2,1)S(1)} %get-tuple-element.246), channel_id=1, source_target_pairs={{0,4},{1,5},{2,6},{3,7},{4,8},{5,9},{6,10},{7,11},{8,12},{9,13},{1... | collective-permute-start | bytes 1572872 | tf_op jit(solution)/shard_map/ppermute | solution.py:45
  28.3 12.9 %collective-permute-start.12 = (bf16[4,32,2048]{2,1,0:T(8,128)(2,1)S(1)}, bf16[4,32,2048]{2,1,0:T(8,128)(2,1)S(1)}, u32[]{:S(2)}, u32[]{:S(2)}) collective-permute-start(bf16[4,32,2048]{2,1,0:T(8,128)(2,1)S(1)} %get-tuple-element.246), channel_id=1, source_target_pairs={{0,12},{1,13},{2,14},{3,15},{4,0},{5,1},{6,2},{7,3},{8,4},{9,5},{1... | collective-permute-start | bytes 1572872 | tf_op jit(solution)/shard_map/ppermute | solution.py:45
  31.9 15.6 %collective-permute-start.5 = (bf16[4,32,2048]{2,1,0:T(8,128)(2,1)}, bf16[4,32,2048]{2,1,0:T(8,128)(2,1)}, u32[]{:S(2)}, u32[]{:S(2)}) collective-permute-start(bf16[4,32,2048]{2,1,0:T(8,128)(2,1)} %get-tuple-element.244), channel_id=1, source_target_pairs={{0,1},{1,2},{2,3},{3,0},{4,5},{5,6},{6,7},{7,4},{8,9},{9,10},{10,1... | collective-permute-start | bytes 1572872 | tf_op jit(solution)/shard_map/ppermute | solution.py:45
  31.9 16.7 %collective-permute-start.4 = (bf16[4,32,2048]{2,1,0:T(8,128)(2,1)}, bf16[4,32,2048]{2,1,0:T(8,128)(2,1)}, u32[]{:S(2)}, u32[]{:S(2)}) collective-permute-start(bf16[4,32,2048]{2,1,0:T(8,128)(2,1)} %get-tuple-element.244), channel_id=1, source_target_pairs={{0,3},{1,0},{2,1},{3,2},{4,7},{5,4},{6,5},{7,6},{8,11},{9,8},{10,9... | collective-permute-start | bytes 1572872 | tf_op jit(solution)/shard_map/ppermute | solution.py:45
  41.2 11.3 %collective-permute-start.14 = (bf16[4,16,2048]{2,1,0:T(8,128)(2,1)S(1)}, bf16[4,16,2048]{2,1,0:T(8,128)(2,1)}, u32[]{:S(2)}, u32[]{:S(2)}) collective-permute-start(bf16[4,16,2048]{2,1,0:T(8,128)(2,1)S(1)} %slice.318), channel_id=1, source_target_pairs={{0,4},{1,5},{2,6},{3,7},{4,8},{5,9},{6,10},{7,11},{8,12},{9,13},{1... | collective-permute-start | bytes 786440 | tf_op jit(solution)/shard_map/ppermute | solution.py:45
  42.8 9.7 %collective-permute-start.15 = (bf16[4,16,2048]{2,1,0:T(8,128)(2,1)}, bf16[4,16,2048]{2,1,0:T(8,128)(2,1)}, u32[]{:S(2)}, u32[]{:S(2)}) collective-permute-start(bf16[4,16,2048]{2,1,0:T(8,128)(2,1)} %slice.319), channel_id=1, source_target_pairs={{0,12},{1,13},{2,14},{3,15},{4,0},{5,1},{6,2},{7,3},{8,4},{9,5},{1... | collective-permute-start | bytes 786440 | tf_op jit(solution)/shard_map/ppermute | solution.py:45
  48.5 6.6 %collective-permute-start.6 = (bf16[4,16,2048]{2,1,0:T(8,128)(2,1)S(1)}, bf16[4,16,2048]{2,1,0:T(8,128)(2,1)S(1)}, u32[]{:S(2)}, u32[]{:S(2)}) collective-permute-start(bf16[4,16,2048]{2,1,0:T(8,128)(2,1)S(1)} %slice.313), channel_id=1, source_target_pairs={{0,1},{1,2},{2,3},{3,0},{4,5},{5,6},{6,7},{7,4},{8,9},{9,10},{10,1... | collective-permute-start | bytes 786440 | tf_op jit(solution)/shard_map/ppermute | solution.py:45
  92.9 6.5 %collective-permute-start.16 = (bf16[4,16,2048]{2,1,0:T(8,128)(2,1)S(1)}, bf16[4,16,2048]{2,1,0:T(8,128)(2,1)S(1)}, u32[]{:S(2)}, u32[]{:S(2)}) collective-permute-start(bf16[4,16,2048]{2,1,0:T(8,128)(2,1)S(1)} %get-tuple-element.235), channel_id=1, source_target_pairs={{0,4},{1,5},{2,6},{3,7},{4,8},{5,9},{6,10},{7,11},{8,12},{9,13},{1... | collective-permute-start | bytes 786440 | tf_op jit(solution)/shard_map/ppermute | solution.py:45
  93.0 6.6 %collective-permute-start.18 = (bf16[4,16,2048]{2,1,0:T(8,128)(2,1)S(1)}, bf16[4,16,2048]{2,1,0:T(8,128)(2,1)S(1)}, u32[]{:S(2)}, u32[]{:S(2)}) collective-permute-start(bf16[4,16,2048]{2,1,0:T(8,128)(2,1)S(1)} %get-tuple-element.236), channel_id=1, source_target_pairs={{0,12},{1,13},{2,14},{3,15},{4,0},{5,1},{6,2},{7,3},{8,4},{9,5},{1... | collective-permute-start | bytes 786440 | tf_op jit(solution)/shard_map/ppermute | solution.py:45
  95.8 7.2 %collective-permute-start.24 = (bf16[4,16,2048]{2,1,0:T(8,128)(2,1)S(1)}, bf16[4,16,2048]{2,1,0:T(8,128)(2,1)S(1)}, u32[]{:S(2)}, u32[]{:S(2)}) collective-permute-start(bf16[4,16,2048]{2,1,0:T(8,128)(2,1)S(1)} %get-tuple-element.241), channel_id=1, source_target_pairs={{0,1},{1,2},{2,3},{3,0},{4,5},{5,6},{6,7},{7,4},{8,9},{9,10},{10,1... | collective-permute-start | bytes 786440 | tf_op jit(solution)/shard_map/ppermute | solution.py:45
  95.9 7.3 %collective-permute-start.26 = (bf16[4,16,2048]{2,1,0:T(8,128)(2,1)S(1)}, bf16[4,16,2048]{2,1,0:T(8,128)(2,1)S(1)}, u32[]{:S(2)}, u32[]{:S(2)}) collective-permute-start(bf16[4,16,2048]{2,1,0:T(8,128)(2,1)S(1)} %get-tuple-element.242), channel_id=1, source_target_pairs={{0,3},{1,0},{2,1},{3,2},{4,7},{5,4},{6,5},{7,6},{8,11},{9,8},{10,9... | collective-permute-start | bytes 786440 | tf_op jit(solution)/shard_map/ppermute | solution.py:45
  99.5 11.4 %collective-permute-start.17 = (bf16[4,32,2048]{2,1,0:T(8,128)(2,1)S(1)}, bf16[4,32,2048]{2,1,0:T(8,128)(2,1)S(1)}, u32[]{:S(2)}, u32[]{:S(2)}) collective-permute-start(bf16[4,32,2048]{2,1,0:T(8,128)(2,1)S(1)} %pad_maximum_fusion.5), channel_id=1, source_target_pairs={{0,4},{1,5},{2,6},{3,7},{4,8},{5,9},{6,10},{7,11},{8,12},{9,13},{1... | collective-permute-start | bytes 1572872 | tf_op jit(solution)/shard_map/ppermute | solution.py:45
  99.7 11.2 %collective-permute-start.19 = (bf16[4,32,2048]{2,1,0:T(8,128)(2,1)S(1)}, bf16[4,32,2048]{2,1,0:T(8,128)(2,1)S(1)}, u32[]{:S(2)}, u32[]{:S(2)}) collective-permute-start(bf16[4,32,2048]{2,1,0:T(8,128)(2,1)S(1)} %pad_maximum_fusion.6), channel_id=1, source_target_pairs={{0,12},{1,13},{2,14},{3,15},{4,0},{5,1},{6,2},{7,3},{8,4},{9,5},{1... | collective-permute-start | bytes 1572872 | tf_op jit(solution)/shard_map/ppermute | solution.py:45
  103.1 11.7 %collective-permute-start.25 = (bf16[4,32,2048]{2,1,0:T(8,128)(2,1)S(1)}, bf16[4,32,2048]{2,1,0:T(8,128)(2,1)S(1)}, u32[]{:S(2)}, u32[]{:S(2)}) collective-permute-start(bf16[4,32,2048]{2,1,0:T(8,128)(2,1)S(1)} %pad_maximum_fusion.7), channel_id=1, source_target_pairs={{0,1},{1,2},{2,3},{3,0},{4,5},{5,6},{6,7},{7,4},{8,9},{9,10},{10,1... | collective-permute-start | bytes 1572872 | tf_op jit(solution)/shard_map/ppermute | solution.py:45
  103.3 11.5 %collective-permute-start.27 = (bf16[4,32,2048]{2,1,0:T(8,128)(2,1)S(1)}, bf16[4,32,2048]{2,1,0:T(8,128)(2,1)S(1)}, u32[]{:S(2)}, u32[]{:S(2)}) collective-permute-start(bf16[4,32,2048]{2,1,0:T(8,128)(2,1)S(1)} %pad_maximum_fusion.8), channel_id=1, source_target_pairs={{0,3},{1,0},{2,1},{3,2},{4,7},{5,4},{6,5},{7,6},{8,11},{9,8},{10,9... | collective-permute-start | bytes 1572872 | tf_op jit(solution)/shard_map/ppermute | solution.py:45
  111.2 6.7 %collective-permute-start.20 = (bf16[16,2048]{1,0:T(8,128)(2,1)S(1)}, bf16[16,2048]{1,0:T(8,128)(2,1)S(1)}, u32[]{:S(2)}, u32[]{:S(2)}) collective-permute-start(bf16[16,2048]{1,0:T(8,128)(2,1)S(1)} %get-tuple-element.231), channel_id=1, source_target_pairs={{0,1},{1,2},{2,3},{3,0},{4,5},{5,6},{6,7},{7,4},{8,9},{9,10},{10,1... | collective-permute-start | bytes 196616 | tf_op jit(solution)/shard_map/ppermute | solution.py:45
  111.3 6.7 %collective-permute-start.22 = (bf16[16,2048]{1,0:T(8,128)(2,1)S(1)}, bf16[16,2048]{1,0:T(8,128)(2,1)S(1)}, u32[]{:S(2)}, u32[]{:S(2)}) collective-permute-start(bf16[16,2048]{1,0:T(8,128)(2,1)S(1)} %get-tuple-element.232), channel_id=1, source_target_pairs={{0,3},{1,0},{2,1},{3,2},{4,7},{5,4},{6,5},{7,6},{8,11},{9,8},{10,9... | collective-permute-start | bytes 196616 | tf_op jit(solution)/shard_map/ppermute | solution.py:45
  255.5 81.5 %all-to-all-start.1 = ((bf16[128,192,128]{2,1,0:T(8,128)(2,1)}), bf16[128,192,128]{2,1,0:T(8,128)(2,1)}, u32[]{:S(2)}, u32[]{:S(2)}) async-start(bf16[128,192,128]{2,1,0:T(8,128)(2,1)} %reshape_reshape.3), calls=%async_computation.1 | async-start | bytes 12582912 | tf_op jit(solution)/shard_map/all_to_all | solution.py:217
  (25 other events, 467.8 us)

commit v6 on v5

--- a/solution.py
+++ b/solution.py
@@ -3,6 +3,8 @@
 import jax
 import jax.numpy as jnp
 from jax import lax
+from jax.experimental import pallas as pl
+from jax.experimental.pallas import tpu as pltpu
 from jax.sharding import PartitionSpec as P
 
 HD = 128
@@ -31,6 +33,41 @@
     hidden = (jax.nn.silu(gated) * lifted).astype(jnp.bfloat16)
     produced = jnp.dot(hidden, down_weight[0], preferred_element_type=jnp.float32)
     return produced.astype(jnp.bfloat16).reshape(rows, sub, lanes)
+
+
+def attend_kernel(limit_ref, q_ref, k_ref, v_ref, ok_ref, ov_ref, om_ref, o_ref):
+    scale = HD ** (-0.5)
+    q = q_ref[...]
+    batch, block, depth = q.shape
+    rows = batch * block
+    scores = lax.dot_general(
+        q.reshape(rows, depth), k_ref[...], (((1,), (1,)), ((), ())),
+        preferred_element_type=jnp.float32) * scale
+    column = lax.broadcasted_iota(jnp.int32, scores.shape, 1)
+    scores = jnp.where(column < limit_ref[0], scores, -jnp.inf)
+    own = jnp.einsum("rid,rjd->rij", q, ok_ref[...], preferred_element_type=jnp.float32) * scale
+    own = own + om_ref[...]
+    highest = jnp.maximum(
+        jnp.max(scores, axis=1, keepdims=True),
+        jnp.max(own, axis=2, keepdims=True).reshape(rows, 1))
+    weights = jnp.exp(scores - highest).astype(jnp.bfloat16)
+    own_weights = jnp.exp(own - highest.reshape(batch, block, 1)).astype(jnp.bfloat16)
+    summed = jnp.dot(weights, v_ref[...], preferred_element_type=jnp.float32)
+    summed = summed.reshape(batch, block, depth) + jnp.einsum(
+        "rij,rjd->rid", own_weights, ov_ref[...], preferred_element_type=jnp.float32)
+    totals = jnp.sum(weights.astype(jnp.float32), axis=1, keepdims=True).reshape(batch, block, 1)
+    totals = totals + jnp.sum(own_weights.astype(jnp.float32), axis=2, keepdims=True)
+    o_ref[...] = (summed / totals).astype(o_ref.dtype)
+
+
+def attend_window(limit, q, k, v, ok, ov, om):
+    vmem = pl.BlockSpec(memory_space=pltpu.VMEM)
+    return pl.pallas_call(
+        attend_kernel,
+        out_shape=jax.ShapeDtypeStruct(q.shape, jnp.bfloat16),
+        in_specs=[pl.BlockSpec(memory_space=pltpu.SMEM)] + [vmem] * 6,
+        out_specs=vmem,
+    )(limit, q, k, v, ok, ov, om)
 
 
 def ring_shift(block, side, along_x, step):
@@ -123,54 +160,37 @@
     new_values = projected[:, 2 * local_width :].reshape(layout)
     scale = HD ** (-0.5)
     positions = jnp.arange(SB, dtype=jnp.int32)
-    own_scores = (
-        jnp.einsum("rihd,rjhd->rhij", queries, new_keys, preferred_element_type=jnp.float32) * scale
-    )
-    own_scores = jnp.where(
-        positions[None, None, None, :] < own_length[:, None, None, None], own_scores, -jnp.inf
-    )
+    assert heads_here == 1
+    queries = queries.reshape(requests, SB, HD)
+    new_keys = new_keys.reshape(requests, SB, HD)
+    new_values = new_values.reshape(requests, SB, HD)
+    own_mask = jnp.where(positions[None, :] < own_length[:, None], 0.0, -jnp.inf)
+    own_mask = jnp.broadcast_to(own_mask[:, None, :], (requests, SB, SB)).astype(jnp.float32)
     member = group_index[0]
-    prompt_positions = jnp.arange(longest, dtype=jnp.int32)
 
     def group_step(group, attended):
         first = jnp.sum((member < group).astype(jnp.int32))
         start = jnp.minimum(first, requests - GSIZE)
-        window_queries = lax.dynamic_slice_in_dim(queries, start, GSIZE, 0)
-        group_keys = lax.dynamic_index_in_dim(prompt_keys, group, 0, keepdims=False).reshape(
-            longest, heads_here, HD
+        window = lambda values: lax.dynamic_slice_in_dim(values, start, GSIZE, 0)
+        group_keys = lax.dynamic_index_in_dim(prompt_keys, group, 0, keepdims=False)
+        group_values = lax.dynamic_index_in_dim(prompt_values, group, 0, keepdims=False)
+        limit = lax.dynamic_slice_in_dim(prompt_length, group, 1, 0)
+        result = attend_window(
+            limit,
+            window(queries),
+            group_keys,
+            group_values,
+            window(new_keys),
+            window(new_values),
+            window(own_mask),
         )
-        group_values = lax.dynamic_index_in_dim(prompt_values, group, 0, keepdims=False).reshape(
-            longest, heads_here, HD
-        )
-        scores = (
-            jnp.einsum(
-                "rihd,jhd->rhij", window_queries, group_keys, preferred_element_type=jnp.float32
-            )
-            * scale
-        )
-        limit = lax.dynamic_index_in_dim(prompt_length, group, 0, keepdims=False)
-        scores = jnp.where(prompt_positions < limit, scores, -jnp.inf)
-        window_own = lax.dynamic_slice_in_dim(own_scores, start, GSIZE, 0)
-        highest = jnp.maximum(jnp.max(scores, axis=-1), jnp.max(window_own, axis=-1))
-        prompt_weights = jnp.exp(scores - highest[..., None]).astype(jnp.bfloat16)
-        own_weights = jnp.exp(window_own - highest[..., None]).astype(jnp.bfloat16)
-        window_values = lax.dynamic_slice_in_dim(new_values, start, GSIZE, 0)
-        summed = jnp.einsum(
-            "rhij,jhd->rihd", prompt_weights, group_values, preferred_element_type=jnp.float32
-        )
-        summed = summed + jnp.einsum(
-            "rhij,rjhd->rihd", own_weights, window_values, preferred_element_type=jnp.float32
-        )
-        totals = jnp.sum(prompt_weights, axis=-1, dtype=jnp.float32) + jnp.sum(
-            own_weights, axis=-1, dtype=jnp.float32
-        )
-        result = (summed / jnp.transpose(totals, (0, 2, 1))[..., None]).astype(jnp.bfloat16)
-        inside = lax.dynamic_slice_in_dim(member, start, GSIZE, 0) == group
-        current = lax.dynamic_slice_in_dim(attended, start, GSIZE, 0)
-        merged = jnp.where(inside[:, None, None, None], result, current)
+        inside = window(member) == group
+        merged = jnp.where(inside[:, None, None], result, window(attended))
         return lax.dynamic_update_slice_in_dim(attended, merged, start, 0)
 
-    attended = lax.fori_loop(0, groups_here, group_step, jnp.zeros(layout, jnp.bfloat16))
+    attended = lax.fori_loop(
+        0, groups_here, group_step, jnp.zeros((requests, SB, HD), jnp.bfloat16)
+    )
     owners = attended.reshape(side, side, tok_rows, local_width)
     ahead_x = (offsets + place // side) % side
     ahead_y = (offsets + place % side) % side

time: 353 us -> 368 us (1.042)
  local copies, waits for them, and re-layouts: 49.6 us -> 67.9 us
  Pallas kernels: 0 us -> 17.7 us
  matrix products: 34.8 us -> 20.9 us
  other arithmetic: 26.2 us -> 21.2 us
    pallas_call x0 -> x3, Pallas kernels: none -> 17.7 us  [attend_window(): pl.pallas_call(attend_kernel, out_shape=jax.ShapeDtypeStruct(q.shape, jnp...]
    dot_general x10 -> x0, matrix products: 12.9 us -> none  [the longest x3 6.2 us: group_step(): jnp.einsum('rhij,jhd->rihd', prompt_weights, group_values, preferred_elem...]
    dynamic_slice x3 -> x12, local copies, waits for them, and re-layouts: 1.77 us -> 10.9 us  [the longest x9 9 us: group_step(): window = lambda values: lax.dynamic_slice_in_dim(values, start, GSIZE, 0)]
    squeeze x0 -> x3, local copies, waits for them, and re-layouts: none -> 6.79 us  [group_step(): lax.dynamic_index_in_dim(prompt_values, group, 0, keepdims=False)]
  transfers between devices with their start and end apart: 33 -> 33, of which waited for: 9 -> 7; matrix products, arithmetic and copies ran while one was open for 6% -> 6% of each run, Pallas kernels for 0% -> 0%
where the time goes in v6:
time: 368 us; the launch traced here: 367 us
  blocking collectives  95.1 us (26%)
  waiting for transfers between devices  88.2 us (24%)
  local copies, waits for them, and re-layouts  67.9 us (18%)
  starting transfers between devices  52 us (14%)
  other arithmetic  21.2 us (6%)
  matrix products  20.9 us (6%)
  Pallas kernels  17.7 us (5%)
    all_to_all x1, blocking collectives, per_device(): arrived = lax.all_to_all(outgoing, ('dp', 'expert'), 0, 0, tiled=True)  95.1 us
    all_to_all x1, waiting for transfers between devices, per_device(): lax.all_to_all(produced.reshape(devices, capacity * sub, lanes), ('dp', '...  75.4 us
    ppermute x32, starting transfers between devices, ring_shift(): return lax.ppermute(block, 'expert', pairs)  46.3 us
    pallas_call x3, Pallas kernels, attend_window(): pl.pallas_call(attend_kernel, out_shape=jax.ShapeDtypeStruct(q.shape, jnp...  17.7 us
    ppermute x32, waiting for transfers between devices, ring_shift(): return lax.ppermute(block, 'expert', pairs)  12.7 us
    dot_general x1, matrix products, expert_block(): jnp.dot(hidden, down_weight[0], preferred_element_type=jnp.float32)  11.9 us
    another operation x1, local copies, waits for them, and re-layouts, per_device(): produced.reshape(devices, capacity * sub, lanes)  10.5 us
    dynamic_slice x9, local copies, waits for them, and re-layouts, group_step(): window = lambda values: lax.dynamic_slice_in_dim(values, start, GSIZE, 0)  9 us
  transfers between devices with their start and end apart: 33, of which 7 were waited for; matrix products, arithmetic and copies ran while one was open for 6% of the time, Pallas kernels for 0%

profile of v6, /device:TPU:1, one launch (start us, length us, event | category | flops | bytes accessed | tf_op | source)
XLA Modules:
  0.0 366.5 jit_solution(12888032517947455628)
XLA Ops:
  31.8 2.7 collective-permute-start.4
  34.6 4.6 %collective-permute-done.13 = bf16[4,32,2048]{2,1,0:T(8,128)(2,1)S(1)} collective-permute-done((bf16[4,32,2048]{2,1,0:T(8,128)(2,1)S(1)}, bf16[4,32,2048]{2,1,0:T(8,128)(2,1)S(1)}, u32[]{:S(2)}, u32[]{:S(2)}) %collective-permute-start.13) | collective-permute-done | bytes 524320 | tf_op jit(solution)/shard_map/ppermute | solution.py:82
  48.4 2.9 collective-permute-start.7
  62.4 42.7 %while.13 = (s32[]{:T(128)}, bf16[32,32,128]{2,1,0:T(8,128)(2,1)S(1)}, s32[32]{0:T(128)S(1)}, s32[3]{0:T(128)S(1)}, bf16[32,32,128]{2,1,0:T(8,128)(2,1)}, /*inde...) while((s32[]{:T(128)}, ...), condition=%wide.region_3.4_spmd, body=%wide.region_1.3_spmd.sunk | while | flops 65653 | bytes 3408819 | solution.py:191
  69.6 5.9 %eval_jaxpr.5 = bf16[16,32,128]{2,1,0:T(8,128)(2,1)} custom-call(s32[1]{0:T(128)} %dynamic_slice.65.limit_ref, bf16[16,32,128]{2,1,0:T(8,128)(2,1)} %constant_dynamic-slice_fusion.7.q_ref, bf16[2048,128]{1,0:T(8,128)(2,1)} %get-tuple-element.308.k_ref, bf16[2048,128]{1,0:T(8,128)(2,1)} %get-tuple-element.309.v_ref, ...), custom_call_target="tpu_custom_call" | custom-call | tf_op jit(solution)/shard_map/while/body/eval_jaxpr/pallas_call | solution.py:65
  83.9 5.9 %eval_jaxpr.5 = bf16[16,32,128]{2,1,0:T(8,128)(2,1)} custom-call(s32[1]{0:T(128)} %dynamic_slice.65.limit_ref, bf16[16,32,128]{2,1,0:T(8,128)(2,1)} %constant_dynamic-slice_fusion.7.q_ref, bf16[2048,128]{1,0:T(8,128)(2,1)} %get-tuple-element.308.k_ref, bf16[2048,128]{1,0:T(8,128)(2,1)} %get-tuple-element.309.v_ref, ...), custom_call_target="tpu_custom_call" | custom-call | tf_op jit(solution)/shard_map/while/body/eval_jaxpr/pallas_call | solution.py:65
  98.1 5.9 %eval_jaxpr.5 = bf16[16,32,128]{2,1,0:T(8,128)(2,1)} custom-call(s32[1]{0:T(128)} %dynamic_slice.65.limit_ref, bf16[16,32,128]{2,1,0:T(8,128)(2,1)} %constant_dynamic-slice_fusion.7.q_ref, bf16[2048,128]{1,0:T(8,128)(2,1)} %get-tuple-element.308.k_ref, bf16[2048,128]{1,0:T(8,128)(2,1)} %get-tuple-element.309.v_ref, ...), custom_call_target="tpu_custom_call" | custom-call | tf_op jit(solution)/shard_map/while/body/eval_jaxpr/pallas_call | solution.py:65
  108.8 2.7 collective-permute-start.18
  111.7 2.7 collective-permute-start.26
  115.5 2.7 collective-permute-start.19
  118.7 2.7 collective-permute-start.27
  121.4 4.9 %collective-permute-done.17 = bf16[4,32,2048]{2,1,0:T(8,128)(2,1)S(1)} collective-permute-done((bf16[4,32,2048]{2,1,0:T(8,128)(2,1)S(1)}, bf16[4,32,2048]{2,1,0:T(8,128)(2,1)S(1)}, u32[]{:S(2)}, u32[]{:S(2)}) %collective-permute-start.17) | collective-permute-done | bytes 524320 | tf_op jit(solution)/shard_map/ppermute | solution.py:82
  126.9 3.5 collective-permute-start.22
  130.8 2.8 collective-permute-start.30
  136.8 2.7 collective-permute-start.31
  142.3 5.8 %gather_fusion.4 = bf16[1536,16,128]{2,1,0:T(8,128)(2,1)} fusion(bf16[65,16,128]{2,1,0:T(8,128)(2,1)S(1)} %concatenate.75, s32[2048]{0:T(1024)S(1)} %pad_clamp_fusion), kind=kCustom, calls=%fused_computation.4 | custom fusion | bytes 12589056 | tf_op jit(solution)/shard_map/gather | solution.py:232
  148.1 95.1 %all_to_all.10 = bf16[128,192,128]{2,1,0:T(8,128)(2,1)S(1)} all-to-all(bf16[128,192,128]{2,1,0:T(8,128)(2,1)} %bitcast.181), channel_id=1, replica_groups=mesh['dp'=8,'expert'=16] {'dp','expert'}, dimensions={0} | all-to-all | bytes 12582912 | tf_op jit(solution)/shard_map/all_to_all | solution.py:233
  243.2 5.1 %fusion.5 = f32[1536,512]{1,0:T(8,128)} fusion(bf16[16,128,512]{2,1,0:T(8,128)(2,1)S(1)} %bitcast.217, bf16[1536,16,128]{2,1,0:T(8,128)(2,1)S(1)} %bitcast.182), kind=kOutput, calls=%fused_computation.24 | convolution fusion | flops 3221225472 | bytes 11534336 | tf_op jit(solution)/shard_map/dot_general | solution.py:31
  248.3 11.9 %convolution_convert_fusion = bf16[1536,2048]{1,0:T(8,128)(2,1)} fusion(bf16[1,512,2048]{2,1,0:T(8,128)(2,1)} %param.35, bf16[16,128,512]{2,1,0:T(8,128)(2,1)S(1)} %bitcast.179, bf16[1536,16,128]{2,1,0:T(8,128)(2,1)} %bitcast.183, f32[1536,512]{1,0:T(8,128)} %fusion.5), kind=kOutput, calls=%fused_computation.18 | convolution fusion | flops 6450315264 | bytes 19922944 | tf_op jit(solution)/shard_map/dot_general | solution.py:34
  260.2 10.5 %reshape_reshape.15 = bf16[128,192,128]{2,1,0:T(8,128)(2,1)} reshape(bf16[1536,2048]{1,0:T(8,128)(2,1)} %convolution_convert_fusion) | data formatting | bytes 12582912 | tf_op jit(solution)/shard_map/reshape;reshape | solution.py:238
  270.7 5.7 %all-to-all-start.1 = ((bf16[128,192,128]{2,1,0:T(8,128)(2,1)}), bf16[128,192,128]{2,1,0:T(8,128)(2,1)}, u32[]{:S(2)}, u32[]{:S(2)}) async-start(bf16[128,192,128]{2,1,0:T(8,128)(2,1)} %reshape_reshape.15), calls=%async_computation.1 | async-start | bytes 12582912 | tf_op jit(solution)/shard_map/all_to_all | solution.py:237
  276.5 75.4 %all-to-all-done.1 = bf16[128,192,128]{2,1,0:T(8,128)(2,1)} async-done(((bf16[128,192,128]{2,1,0:T(8,128)(2,1)}), bf16[128,192,128]{2,1,0:T(8,128)(2,1)}, u32[]{:S(2)}, u32[]{:S(2)}) %all-to-all-start.1) | async-done | bytes 6291488 | tf_op jit(solution)/shard_map/all_to_all | solution.py:237
  352.0 8.9 %gather_fusion.5 = bf16[512,2,16,128]{3,2,1,0:T(8,128)(2,1)} fusion(bf16[64,2,12,16,128]{4,3,2,1,0:T(8,128)(2,1)} %bitcast.70, s32[512]{0:T(512)S(1)} %bitcast.180), kind=kCustom, calls=%fused_computation.5 | custom fusion | bytes 8392704 | tf_op jit(solution)/shard_map/gather | solution.py:240
  360.9 4.0 %convert_reduce_fusion = f32[512,16,128]{2,1,0:T(8,128)S(1)} fusion(bf16[512,2,16,128]{3,2,1,0:T(8,128)(2,1)} %gather_fusion.5), kind=kLoop, calls=%fused_computation.17 | loop fusion | flops 3145728 | bytes 8388608 | tf_op jit(solution)/shard_map/reduce_sum | solution.py:241
  (214 shorter events, 87.8 us)
Async XLA Ops:
  3.8 13.6 %collective-permute-start.9 = (bf16[32,2048]{1,0:T(8,128)(2,1)}, bf16[32,2048]{1,0:T(8,128)(2,1)}, u32[]{:S(2)}, u32[]{:S(2)}) collective-permute-start(bf16[32,2048]{1,0:T(8,128)(2,1)} %get-tuple-element.235), channel_id=1, source_target_pairs={{0,1},{1,2},{2,3},{3,0},{4,5},{5,6},{6,7},{7,4},{8,9},{9,10},{10,1... | collective-permute-start | bytes 393224 | tf_op jit(solution)/shard_map/ppermute | solution.py:82
  5.9 12.3 %collective-permute-start.8 = (bf16[32,2048]{1,0:T(8,128)(2,1)}, bf16[32,2048]{1,0:T(8,128)(2,1)}, u32[]{:S(2)}, u32[]{:S(2)}) collective-permute-start(bf16[32,2048]{1,0:T(8,128)(2,1)} %get-tuple-element.235), channel_id=1, source_target_pairs={{0,3},{1,0},{2,1},{3,2},{4,7},{5,4},{6,5},{7,6},{8,11},{9,8},{10,9... | collective-permute-start | bytes 393224 | tf_op jit(solution)/shard_map/ppermute | solution.py:82
  7.3 14.4 %collective-permute-start.1 = (bf16[32,2048]{1,0:T(8,128)(2,1)}, bf16[32,2048]{1,0:T(8,128)(2,1)}, u32[]{:S(2)}, u32[]{:S(2)}) collective-permute-start(bf16[32,2048]{1,0:T(8,128)(2,1)} %get-tuple-element.236), channel_id=1, source_target_pairs={{0,4},{1,5},{2,6},{3,7},{4,8},{5,9},{6,10},{7,11},{8,12},{9,13},{1... | collective-permute-start | bytes 393224 | tf_op jit(solution)/shard_map/ppermute | solution.py:82
  8.6 14.1 %collective-permute-start = (bf16[32,2048]{1,0:T(8,128)(2,1)}, bf16[32,2048]{1,0:T(8,128)(2,1)}, u32[]{:S(2)}, u32[]{:S(2)}) collective-permute-start(bf16[32,2048]{1,0:T(8,128)(2,1)} %get-tuple-element.236), channel_id=1, source_target_pairs={{0,12},{1,13},{2,14},{3,15},{4,0},{5,1},{6,2},{7,3},{8,4},{9,5},{1... | collective-permute-start | bytes 393224 | tf_op jit(solution)/shard_map/ppermute | solution.py:82
  18.2 7.9 %collective-permute-start.10 = (bf16[16,2048]{1,0:T(8,128)(2,1)S(1)}, bf16[16,2048]{1,0:T(8,128)(2,1)S(1)}, u32[]{:S(2)}, u32[]{:S(2)}) collective-permute-start(bf16[16,2048]{1,0:T(8,128)(2,1)S(1)} %slice.316), channel_id=1, source_target_pairs={{0,1},{1,2},{2,3},{3,0},{4,5},{5,6},{6,7},{7,4},{8,9},{9,10},{10,1... | collective-permute-start | bytes 196616 | tf_op jit(solution)/shard_map/ppermute | solution.py:82
  19.1 7.0 %collective-permute-start.11 = (bf16[16,2048]{1,0:T(8,128)(2,1)S(1)}, bf16[16,2048]{1,0:T(8,128)(2,1)S(1)}, u32[]{:S(2)}, u32[]{:S(2)}) collective-permute-start(bf16[16,2048]{1,0:T(8,128)(2,1)S(1)} %slice.317), channel_id=1, source_target_pairs={{0,3},{1,0},{2,1},{3,2},{4,7},{5,4},{6,5},{7,6},{8,11},{9,8},{10,9... | collective-permute-start | bytes 196616 | tf_op jit(solution)/shard_map/ppermute | solution.py:82
  22.6 7.4 %collective-permute-start.2 = (bf16[16,2048]{1,0:T(8,128)(2,1)S(1)}, bf16[16,2048]{1,0:T(8,128)(2,1)S(1)}, u32[]{:S(2)}, u32[]{:S(2)}) collective-permute-start(bf16[16,2048]{1,0:T(8,128)(2,1)S(1)} %slice.311), channel_id=1, source_target_pairs={{0,4},{1,5},{2,6},{3,7},{4,8},{5,9},{6,10},{7,11},{8,12},{9,13},{1... | collective-permute-start | bytes 196616 | tf_op jit(solution)/shard_map/ppermute | solution.py:82
  27.2 12.0 %collective-permute-start.13 = (bf16[4,32,2048]{2,1,0:T(8,128)(2,1)S(1)}, bf16[4,32,2048]{2,1,0:T(8,128)(2,1)S(1)}, u32[]{:S(2)}, u32[]{:S(2)}) collective-permute-start(bf16[4,32,2048]{2,1,0:T(8,128)(2,1)S(1)} %get-tuple-element.230), channel_id=1, source_target_pairs={{0,4},{1,5},{2,6},{3,7},{4,8},{5,9},{6,10},{7,11},{8,12},{9,13},{1... | collective-permute-start | bytes 1572872 | tf_op jit(solution)/shard_map/ppermute | solution.py:82
  27.3 12.8 %collective-permute-start.12 = (bf16[4,32,2048]{2,1,0:T(8,128)(2,1)S(1)}, bf16[4,32,2048]{2,1,0:T(8,128)(2,1)S(1)}, u32[]{:S(2)}, u32[]{:S(2)}) collective-permute-start(bf16[4,32,2048]{2,1,0:T(8,128)(2,1)S(1)} %get-tuple-element.230), channel_id=1, source_target_pairs={{0,12},{1,13},{2,14},{3,15},{4,0},{5,1},{6,2},{7,3},{8,4},{9,5},{1... | collective-permute-start | bytes 1572872 | tf_op jit(solution)/shard_map/ppermute | solution.py:82
  31.8 14.5 %collective-permute-start.5 = (bf16[4,32,2048]{2,1,0:T(8,128)(2,1)}, bf16[4,32,2048]{2,1,0:T(8,128)(2,1)}, u32[]{:S(2)}, u32[]{:S(2)}) collective-permute-start(bf16[4,32,2048]{2,1,0:T(8,128)(2,1)} %get-tuple-element.228), channel_id=1, source_target_pairs={{0,1},{1,2},{2,3},{3,0},{4,5},{5,6},{6,7},{7,4},{8,9},{9,10},{10,1... | collective-permute-start | bytes 1572872 | tf_op jit(solution)/shard_map/ppermute | solution.py:82
  31.8 15.5 %collective-permute-start.4 = (bf16[4,32,2048]{2,1,0:T(8,128)(2,1)}, bf16[4,32,2048]{2,1,0:T(8,128)(2,1)}, u32[]{:S(2)}, u32[]{:S(2)}) collective-permute-start(bf16[4,32,2048]{2,1,0:T(8,128)(2,1)} %get-tuple-element.228), channel_id=1, source_target_pairs={{0,3},{1,0},{2,1},{3,2},{4,7},{5,4},{6,5},{7,6},{8,11},{9,8},{10,9... | collective-permute-start | bytes 1572872 | tf_op jit(solution)/shard_map/ppermute | solution.py:82
  40.0 11.2 %collective-permute-start.14 = (bf16[4,16,2048]{2,1,0:T(8,128)(2,1)S(1)}, bf16[4,16,2048]{2,1,0:T(8,128)(2,1)}, u32[]{:S(2)}, u32[]{:S(2)}) collective-permute-start(bf16[4,16,2048]{2,1,0:T(8,128)(2,1)S(1)} %slice.318), channel_id=1, source_target_pairs={{0,4},{1,5},{2,6},{3,7},{4,8},{5,9},{6,10},{7,11},{8,12},{9,13},{1... | collective-permute-start | bytes 786440 | tf_op jit(solution)/shard_map/ppermute | solution.py:82
  41.7 9.6 %collective-permute-start.15 = (bf16[4,16,2048]{2,1,0:T(8,128)(2,1)}, bf16[4,16,2048]{2,1,0:T(8,128)(2,1)}, u32[]{:S(2)}, u32[]{:S(2)}) collective-permute-start(bf16[4,16,2048]{2,1,0:T(8,128)(2,1)} %slice.319), channel_id=1, source_target_pairs={{0,12},{1,13},{2,14},{3,15},{4,0},{5,1},{6,2},{7,3},{8,4},{9,5},{1... | collective-permute-start | bytes 786440 | tf_op jit(solution)/shard_map/ppermute | solution.py:82
  47.3 7.7 %collective-permute-start.6 = (bf16[4,16,2048]{2,1,0:T(8,128)(2,1)S(1)}, bf16[4,16,2048]{2,1,0:T(8,128)(2,1)S(1)}, u32[]{:S(2)}, u32[]{:S(2)}) collective-permute-start(bf16[4,16,2048]{2,1,0:T(8,128)(2,1)S(1)} %slice.313), channel_id=1, source_target_pairs={{0,1},{1,2},{2,3},{3,0},{4,5},{5,6},{6,7},{7,4},{8,9},{9,10},{10,1... | collective-permute-start | bytes 786440 | tf_op jit(solution)/shard_map/ppermute | solution.py:82
  48.4 6.7 %collective-permute-start.7 = (bf16[4,16,2048]{2,1,0:T(8,128)(2,1)S(1)}, bf16[4,16,2048]{2,1,0:T(8,128)(2,1)S(1)}, u32[]{:S(2)}, u32[]{:S(2)}) collective-permute-start(bf16[4,16,2048]{2,1,0:T(8,128)(2,1)S(1)} %slice.314), channel_id=1, source_target_pairs={{0,3},{1,0},{2,1},{3,2},{4,7},{5,4},{6,5},{7,6},{8,11},{9,8},{10,9... | collective-permute-start | bytes 786440 | tf_op jit(solution)/shard_map/ppermute | solution.py:82
  111.6 6.8 %collective-permute-start.24 = (bf16[4,16,2048]{2,1,0:T(8,128)(2,1)S(1)}, bf16[4,16,2048]{2,1,0:T(8,128)(2,1)S(1)}, u32[]{:S(2)}, u32[]{:S(2)}) collective-permute-start(bf16[4,16,2048]{2,1,0:T(8,128)(2,1)S(1)} %get-tuple-element.225), channel_id=1, source_target_pairs={{0,1},{1,2},{2,3},{3,0},{4,5},{5,6},{6,7},{7,4},{8,9},{9,10},{10,1... | collective-permute-start | bytes 786440 | tf_op jit(solution)/shard_map/ppermute | solution.py:82
  111.7 6.9 %collective-permute-start.26 = (bf16[4,16,2048]{2,1,0:T(8,128)(2,1)S(1)}, bf16[4,16,2048]{2,1,0:T(8,128)(2,1)S(1)}, u32[]{:S(2)}, u32[]{:S(2)}) collective-permute-start(bf16[4,16,2048]{2,1,0:T(8,128)(2,1)S(1)} %get-tuple-element.226), channel_id=1, source_target_pairs={{0,3},{1,0},{2,1},{3,2},{4,7},{5,4},{6,5},{7,6},{8,11},{9,8},{10,9... | collective-permute-start | bytes 786440 | tf_op jit(solution)/shard_map/ppermute | solution.py:82
  115.3 11.1 %collective-permute-start.17 = (bf16[4,32,2048]{2,1,0:T(8,128)(2,1)S(1)}, bf16[4,32,2048]{2,1,0:T(8,128)(2,1)S(1)}, u32[]{:S(2)}, u32[]{:S(2)}) collective-permute-start(bf16[4,32,2048]{2,1,0:T(8,128)(2,1)S(1)} %pad_maximum_fusion.5), channel_id=1, source_target_pairs={{0,4},{1,5},{2,6},{3,7},{4,8},{5,9},{6,10},{7,11},{8,12},{9,13},{1... | collective-permute-start | bytes 1572872 | tf_op jit(solution)/shard_map/ppermute | solution.py:82
  115.5 10.9 %collective-permute-start.19 = (bf16[4,32,2048]{2,1,0:T(8,128)(2,1)S(1)}, bf16[4,32,2048]{2,1,0:T(8,128)(2,1)S(1)}, u32[]{:S(2)}, u32[]{:S(2)}) collective-permute-start(bf16[4,32,2048]{2,1,0:T(8,128)(2,1)S(1)} %pad_maximum_fusion.6), channel_id=1, source_target_pairs={{0,12},{1,13},{2,14},{3,15},{4,0},{5,1},{6,2},{7,3},{8,4},{9,5},{1... | collective-permute-start | bytes 1572872 | tf_op jit(solution)/shard_map/ppermute | solution.py:82
  118.5 11.9 %collective-permute-start.25 = (bf16[4,32,2048]{2,1,0:T(8,128)(2,1)S(1)}, bf16[4,32,2048]{2,1,0:T(8,128)(2,1)S(1)}, u32[]{:S(2)}, u32[]{:S(2)}) collective-permute-start(bf16[4,32,2048]{2,1,0:T(8,128)(2,1)S(1)} %pad_maximum_fusion.7), channel_id=1, source_target_pairs={{0,1},{1,2},{2,3},{3,0},{4,5},{5,6},{6,7},{7,4},{8,9},{9,10},{10,1... | collective-permute-start | bytes 1572872 | tf_op jit(solution)/shard_map/ppermute | solution.py:82
  118.7 11.7 %collective-permute-start.27 = (bf16[4,32,2048]{2,1,0:T(8,128)(2,1)S(1)}, bf16[4,32,2048]{2,1,0:T(8,128)(2,1)S(1)}, u32[]{:S(2)}, u32[]{:S(2)}) collective-permute-start(bf16[4,32,2048]{2,1,0:T(8,128)(2,1)S(1)} %pad_maximum_fusion.8), channel_id=1, source_target_pairs={{0,3},{1,0},{2,1},{3,2},{4,7},{5,4},{6,5},{7,6},{8,11},{9,8},{10,9... | collective-permute-start | bytes 1572872 | tf_op jit(solution)/shard_map/ppermute | solution.py:82
  126.6 7.0 %collective-permute-start.20 = (bf16[16,2048]{1,0:T(8,128)(2,1)S(1)}, bf16[16,2048]{1,0:T(8,128)(2,1)S(1)}, u32[]{:S(2)}, u32[]{:S(2)}) collective-permute-start(bf16[16,2048]{1,0:T(8,128)(2,1)S(1)} %get-tuple-element.215), channel_id=1, source_target_pairs={{0,1},{1,2},{2,3},{3,0},{4,5},{5,6},{6,7},{7,4},{8,9},{9,10},{10,1... | collective-permute-start | bytes 196616 | tf_op jit(solution)/shard_map/ppermute | solution.py:82
  126.9 6.7 %collective-permute-start.22 = (bf16[16,2048]{1,0:T(8,128)(2,1)S(1)}, bf16[16,2048]{1,0:T(8,128)(2,1)S(1)}, u32[]{:S(2)}, u32[]{:S(2)}) collective-permute-start(bf16[16,2048]{1,0:T(8,128)(2,1)S(1)} %get-tuple-element.216), channel_id=1, source_target_pairs={{0,3},{1,0},{2,1},{3,2},{4,7},{5,4},{6,5},{7,6},{8,11},{9,8},{10,9... | collective-permute-start | bytes 196616 | tf_op jit(solution)/shard_map/ppermute | solution.py:82
  270.7 81.2 %all-to-all-start.1 = ((bf16[128,192,128]{2,1,0:T(8,128)(2,1)}), bf16[128,192,128]{2,1,0:T(8,128)(2,1)}, u32[]{:S(2)}, u32[]{:S(2)}) async-start(bf16[128,192,128]{2,1,0:T(8,128)(2,1)} %reshape_reshape.15), calls=%async_computation.1 | async-start | bytes 12582912 | tf_op jit(solution)/shard_map/all_to_all | solution.py:237
  (27 other events, 497.6 us)

commit v7 on v5

--- a/solution.py
+++ b/solution.py
@@ -52,8 +52,8 @@
     cut = block.shape[-2] // 2
     far = jnp.concatenate(
         [
-            ring_shift(from_left[..., :cut, :], side, along_x, 1),
-            ring_shift(from_right[..., cut:, :], side, along_x, -1),
+            ring_shift(block[..., :cut, :], side, along_x, 2),
+            ring_shift(block[..., cut:, :], side, along_x, -2),
         ],
         axis=-2,
     )
@@ -63,14 +63,17 @@
 def ring_reduce(relative, side, along_x):
     assert side == 4
     cut = relative.shape[-2] // 2
-    far = relative[2].astype(jnp.bfloat16)
-    came_left = ring_shift(far[..., :cut, :], side, along_x, 1).astype(jnp.float32)
-    came_right = ring_shift(far[..., cut:, :], side, along_x, -1).astype(jnp.float32)
-    rightward = jnp.concatenate([relative[1][..., :cut, :] + came_left, relative[1][..., cut:, :]], axis=-2)
-    leftward = jnp.concatenate([relative[3][..., :cut, :], relative[3][..., cut:, :] + came_right], axis=-2)
-    from_left = ring_shift(rightward.astype(jnp.bfloat16), side, along_x, 1)
-    from_right = ring_shift(leftward.astype(jnp.bfloat16), side, along_x, -1)
-    return relative[0] + from_left.astype(jnp.float32) + from_right.astype(jnp.float32)
+    narrow = relative.astype(jnp.bfloat16)
+    from_left = ring_shift(narrow[1], side, along_x, 1).astype(jnp.float32)
+    from_right = ring_shift(narrow[3], side, along_x, -1).astype(jnp.float32)
+    far = jnp.concatenate(
+        [
+            ring_shift(narrow[2][..., :cut, :], side, along_x, 2),
+            ring_shift(narrow[2][..., cut:, :], side, along_x, -2),
+        ],
+        axis=-2,
+    ).astype(jnp.float32)
+    return relative[0] + from_left + from_right + far
 
 
 def per_device(

time: 353 us -> 383 us (1.085)
  waiting for transfers between devices: 89.1 us -> 125 us
  other arithmetic: 26.2 us -> 33.7 us
  blocking collectives: 95.4 us -> 89.5 us
  local copies, waits for them, and re-layouts: 49.6 us -> 45.3 us
    ppermute x32, waiting for transfers between devices: 13.7 us -> 49.8 us  [ring_shift(): return lax.ppermute(block, 'expert', pairs)]
    all_to_all x1, blocking collectives: 95.4 us -> 89.5 us  [per_device(): arrived = lax.all_to_all(outgoing, ('dp', 'expert'), 0, 0, tiled=True)]
  transfers between devices with their start and end apart: 33 -> 33, of which waited for: 9 -> 11; matrix products, arithmetic and copies ran while one was open for 6% -> 8% of each run, Pallas kernels for 0% -> 0%
where the time goes in v7:
time: 383 us; the launch traced here: 381 us
  waiting for transfers between devices  125 us (33%)
  blocking collectives  89.5 us (23%)
  starting transfers between devices  49.5 us (13%)
  local copies, waits for them, and re-layouts  45.3 us (12%)
  matrix products  34.8 us (9%)
  other arithmetic  33.7 us (9%)
    all_to_all x1, blocking collectives, per_device(): arrived = lax.all_to_all(outgoing, ('dp', 'expert'), 0, 0, tiled=True)  89.5 us
    all_to_all x1, waiting for transfers between devices, per_device(): lax.all_to_all(produced.reshape(devices, capacity * sub, lanes), ('dp', '...  75.4 us
    ppermute x32, waiting for transfers between devices, ring_shift(): return lax.ppermute(block, 'expert', pairs)  49.8 us
    ppermute x32, starting transfers between devices, ring_shift(): return lax.ppermute(block, 'expert', pairs)  43.8 us
    dot_general x1, matrix products, expert_block(): jnp.dot(hidden, down_weight[0], preferred_element_type=jnp.float32)  11.9 us
    another operation x1, local copies, waits for them, and re-layouts, per_device(): produced.reshape(devices, capacity * sub, lanes)  10.5 us
    gather x1, local copies, waits for them, and re-layouts, per_device(): returned.reshape(experts, hidden_split, capacity, sub, lanes)  8.97 us
    another operation x8, other arithmetic, ring_gather(): return jnp.stack([block, from_right, far, from_left])  8.46 us
  transfers between devices with their start and end apart: 33, of which 11 were waited for; matrix products, arithmetic and copies ran while one was open for 8% of the time, Pallas kernels for 0%

profile of v7, /device:TPU:1, one launch (start us, length us, event | category | flops | bytes accessed | tf_op | source)
XLA Modules:
  0.0 381.3 jit_solution(2765489635857979217)
XLA Ops:
  3.8 3.6 collective-permute-start.8
  11.0 2.7 collective-permute-start.1
  23.8 2.6 scatter_custom_fusion
  31.2 2.5 collective-permute-start
  47.1 9.8 %collective-permute-done.13 = bf16[4,16,2048]{2,1,0:T(8,128)(2,1)} collective-permute-done((bf16[4,16,2048]{2,1,0:T(8,128)(2,1)S(1)}, bf16[4,16,2048]{2,1,0:T(8,128)(2,1)}, u32[]{:S(2)}, u32[]{:S(2)}) %collective-permute-start.13) | collective-permute-done | bytes 262176 | tf_op jit(solution)/shard_map/ppermute | solution.py:45
  58.1 4.6 %collective-permute-done.14 = bf16[4,16,2048]{2,1,0:T(8,128)(2,1)} collective-permute-done((bf16[4,16,2048]{2,1,0:T(8,128)(2,1)}, bf16[4,16,2048]{2,1,0:T(8,128)(2,1)}, u32[]{:S(2)}, u32[]{:S(2)}) %collective-permute-start.14) | collective-permute-done | bytes 262176 | tf_op jit(solution)/shard_map/ppermute | solution.py:45
  70.4 6.1 %collective-permute-done.4 = bf16[4,32,2048]{2,1,0:T(8,128)(2,1)S(1)} collective-permute-done((bf16[4,32,2048]{2,1,0:T(8,128)(2,1)S(1)}, bf16[4,32,2048]{2,1,0:T(8,128)(2,1)S(1)}, u32[]{:S(2)}, u32[]{:S(2)}) %collective-permute-start.4) | collective-permute-done | bytes 524320 | tf_op jit(solution)/shard_map/ppermute | solution.py:45
  76.5 3.6 collective-permute-done.7
  86.0 24.7 %while.14 = (s32[]{:T(128)}, bf16[32,32,1,128]{3,1,0,2:T(8,128)(2,1)S(1)}, s32[32]{0:T(128)S(1)}, bf16[3,2048,128]{2,1,0:T(8,128)(2,1)}, s32[3]{0:T(128)S(1)}, /...) while((s32[]{:T(128)}, ...), condition=%wide.region_7.8_spmd.clone, body=%wide.region_1.7_spmd.clone.sunk | while | flops 555074688 | bytes 15133611 | solution.py:176
  117.1 2.7 collective-permute-start.17
  121.1 2.9 collective-permute-start.27
  126.9 13.8 %collective-permute-done.16 = bf16[4,32,2048]{2,1,0:T(8,128)(2,1)S(1)} collective-permute-done((bf16[4,32,2048]{2,1,0:T(8,128)(2,1)S(1)}, bf16[4,32,2048]{2,1,0:T(8,128)(2,1)S(1)}, u32[]{:S(2)}, u32[]{:S(2)}) %collective-permute-start.16) | collective-permute-done | bytes 524320 | tf_op jit(solution)/shard_map/ppermute | solution.py:45
  147.2 6.5 %collective-permute-done.25 = bf16[4,32,2048]{2,1,0:T(8,128)(2,1)S(1)} collective-permute-done((bf16[4,32,2048]{2,1,0:T(8,128)(2,1)S(1)}, bf16[4,32,2048]{2,1,0:T(8,128)(2,1)S(1)}, u32[]{:S(2)}, u32[]{:S(2)}) %collective-permute-start.25) | collective-permute-done | bytes 524320 | tf_op jit(solution)/shard_map/ppermute | solution.py:45
  154.1 2.7 collective-permute-start.29
  156.8 3.0 collective-permute-start.31
  162.8 5.7 %gather_fusion.4 = bf16[1536,16,128]{2,1,0:T(8,128)(2,1)} fusion(bf16[65,16,128]{2,1,0:T(8,128)(2,1)S(1)} %concatenate.51, s32[2048]{0:T(1024)S(1)} %pad_clamp_fusion), kind=kCustom, calls=%fused_computation.4 | custom fusion | bytes 12589056 | tf_op jit(solution)/shard_map/gather | solution.py:215
  168.5 89.5 %all_to_all.10 = bf16[128,192,128]{2,1,0:T(8,128)(2,1)S(1)} all-to-all(bf16[128,192,128]{2,1,0:T(8,128)(2,1)} %bitcast.268), channel_id=1, replica_groups=mesh['dp'=8,'expert'=16] {'dp','expert'}, dimensions={0} | all-to-all | bytes 12582912 | tf_op jit(solution)/shard_map/all_to_all | solution.py:216
  258.0 5.1 %fusion.45 = f32[1536,512]{1,0:T(8,128)} fusion(bf16[16,128,512]{2,1,0:T(8,128)(2,1)S(1)} %bitcast.303, bf16[1536,16,128]{2,1,0:T(8,128)(2,1)S(1)} %bitcast.269), kind=kOutput, calls=%fused_computation.52 | convolution fusion | flops 3221225472 | bytes 11534336 | tf_op jit(solution)/shard_map/dot_general | solution.py:29
  263.1 11.9 %convolution_convert_fusion = bf16[1536,2048]{1,0:T(8,128)(2,1)} fusion(bf16[1,512,2048]{2,1,0:T(8,128)(2,1)} %param.35, bf16[16,128,512]{2,1,0:T(8,128)(2,1)S(1)} %bitcast.266, bf16[1536,16,128]{2,1,0:T(8,128)(2,1)} %bitcast.270, f32[1536,512]{1,0:T(8,128)} %fusion.45), kind=kOutput, calls=%fused_computation.46 | convolution fusion | flops 6450315264 | bytes 19922944 | tf_op jit(solution)/shard_map/dot_general | solution.py:32
  275.0 10.5 %reshape_reshape.3 = bf16[128,192,128]{2,1,0:T(8,128)(2,1)} reshape(bf16[1536,2048]{1,0:T(8,128)(2,1)} %convolution_convert_fusion) | data formatting | bytes 12582912 | tf_op jit(solution)/shard_map/reshape;reshape | solution.py:221
  285.5 5.6 %all-to-all-start.1 = ((bf16[128,192,128]{2,1,0:T(8,128)(2,1)}), bf16[128,192,128]{2,1,0:T(8,128)(2,1)}, u32[]{:S(2)}, u32[]{:S(2)}) async-start(bf16[128,192,128]{2,1,0:T(8,128)(2,1)} %reshape_reshape.3), calls=%async_computation.1 | async-start | bytes 12582912 | tf_op jit(solution)/shard_map/all_to_all | solution.py:220
  291.3 75.4 %all-to-all-done.1 = bf16[128,192,128]{2,1,0:T(8,128)(2,1)} async-done(((bf16[128,192,128]{2,1,0:T(8,128)(2,1)}), bf16[128,192,128]{2,1,0:T(8,128)(2,1)}, u32[]{:S(2)}, u32[]{:S(2)}) %all-to-all-start.1) | async-done | bytes 6291488 | tf_op jit(solution)/shard_map/all_to_all | solution.py:220
  366.7 9.0 %gather_fusion.5 = bf16[512,2,16,128]{3,2,1,0:T(8,128)(2,1)} fusion(bf16[64,2,12,16,128]{4,3,2,1,0:T(8,128)(2,1)} %bitcast.66, s32[512]{0:T(512)S(1)} %bitcast.267), kind=kCustom, calls=%fused_computation.5 | custom fusion | bytes 8392704 | tf_op jit(solution)/shard_map/gather | solution.py:223
  375.7 4.0 %convert_reduce_fusion.2 = f32[512,16,128]{2,1,0:T(8,128)S(1)} fusion(bf16[512,2,16,128]{3,2,1,0:T(8,128)(2,1)} %gather_fusion.5), kind=kLoop, calls=%fused_computation.45 | loop fusion | flops 3145728 | bytes 8388608 | tf_op jit(solution)/shard_map/reduce_sum | solution.py:224
  (198 shorter events, 94.1 us)
Async XLA Ops:
  3.8 32.8 %collective-permute-start.8 = (bf16[32,2048]{1,0:T(8,128)(2,1)}, bf16[32,2048]{1,0:T(8,128)(2,1)}, u32[]{:S(2)}, u32[]{:S(2)}) collective-permute-start(bf16[32,2048]{1,0:T(8,128)(2,1)} %get-tuple-element.251), channel_id=1, source_target_pairs={{0,3},{1,0},{2,1},{3,2},{4,7},{5,4},{6,5},{7,6},{8,11},{9,8},{10,9... | collective-permute-start | bytes 393224 | tf_op jit(solution)/shard_map/ppermute | solution.py:45
  7.3 29.3 %collective-permute-start.11 = (bf16[32,2048]{1,0:T(8,128)(2,1)}, bf16[32,2048]{1,0:T(8,128)(2,1)}, u32[]{:S(2)}, u32[]{:S(2)}) collective-permute-start(bf16[32,2048]{1,0:T(8,128)(2,1)} %get-tuple-element.251), channel_id=1, source_target_pairs={{0,1},{1,2},{2,3},{3,0},{4,5},{5,6},{6,7},{7,4},{8,9},{9,10},{10,1... | collective-permute-start | bytes 393224 | tf_op jit(solution)/shard_map/ppermute | solution.py:45
  8.1 22.9 %collective-permute-start.10 = (bf16[16,2048]{1,0:T(8,128)(2,1)}, bf16[16,2048]{1,0:T(8,128)(2,1)}, u32[]{:S(2)}, u32[]{:S(2)}) collective-permute-start(bf16[16,2048]{1,0:T(8,128)(2,1)} %get-tuple-element.254), channel_id=1, source_target_pairs={{0,2},{1,3},{2,0},{3,1},{4,6},{5,7},{6,4},{7,5},{8,10},{9,11},{10,... | collective-permute-start | bytes 196616 | tf_op jit(solution)/shard_map/ppermute | solution.py:45
  9.7 21.5 %collective-permute-start.9 = (bf16[16,2048]{1,0:T(8,128)(2,1)}, bf16[16,2048]{1,0:T(8,128)(2,1)}, u32[]{:S(2)}, u32[]{:S(2)}) collective-permute-start(bf16[16,2048]{1,0:T(8,128)(2,1)} %get-tuple-element.255), channel_id=1, source_target_pairs={{0,2},{1,3},{2,0},{3,1},{4,6},{5,7},{6,4},{7,5},{8,10},{9,11},{10,... | collective-permute-start | bytes 196616 | tf_op jit(solution)/shard_map/ppermute | solution.py:45
  11.0 23.5 %collective-permute-start.1 = (bf16[16,2048]{1,0:T(8,128)(2,1)}, bf16[16,2048]{1,0:T(8,128)(2,1)}, u32[]{:S(2)}, u32[]{:S(2)}) collective-permute-start(bf16[16,2048]{1,0:T(8,128)(2,1)} %get-tuple-element.253), channel_id=1, source_target_pairs={{0,8},{1,9},{2,10},{3,11},{4,12},{5,13},{6,14},{7,15},{8,0},{9,1},... | collective-permute-start | bytes 196616 | tf_op jit(solution)/shard_map/ppermute | solution.py:45
  31.2 10.8 %collective-permute-start = (bf16[32,2048]{1,0:T(8,128)(2,1)}, bf16[32,2048]{1,0:T(8,128)(2,1)S(1)}, u32[]{:S(2)}, u32[]{:S(2)}) collective-permute-start(bf16[32,2048]{1,0:T(8,128)(2,1)} %get-tuple-element.252), channel_id=1, source_target_pairs={{0,12},{1,13},{2,14},{3,15},{4,0},{5,1},{6,2},{7,3},{8,4},{9,5},{1... | collective-permute-start | bytes 393224 | tf_op jit(solution)/shard_map/ppermute | solution.py:45
  39.2 28.2 %collective-permute-start.12 = (bf16[4,32,2048]{2,1,0:T(8,128)(2,1)S(1)}, bf16[4,32,2048]{2,1,0:T(8,128)(2,1)}, u32[]{:S(2)}, u32[]{:S(2)}) collective-permute-start(bf16[4,32,2048]{2,1,0:T(8,128)(2,1)S(1)} %get-tuple-element.244), channel_id=1, source_target_pairs={{0,12},{1,13},{2,14},{3,15},{4,0},{5,1},{6,2},{7,3},{8,4},{9,5},{1... | collective-permute-start | bytes 1572872 | tf_op jit(solution)/shard_map/ppermute | solution.py:45
  40.7 26.7 %collective-permute-start.15 = (bf16[4,32,2048]{2,1,0:T(8,128)(2,1)S(1)}, bf16[4,32,2048]{2,1,0:T(8,128)(2,1)}, u32[]{:S(2)}, u32[]{:S(2)}) collective-permute-start(bf16[4,32,2048]{2,1,0:T(8,128)(2,1)S(1)} %get-tuple-element.244), channel_id=1, source_target_pairs={{0,4},{1,5},{2,6},{3,7},{4,8},{5,9},{6,10},{7,11},{8,12},{9,13},{1... | collective-permute-start | bytes 1572872 | tf_op jit(solution)/shard_map/ppermute | solution.py:45
  40.7 16.2 %collective-permute-start.13 = (bf16[4,16,2048]{2,1,0:T(8,128)(2,1)S(1)}, bf16[4,16,2048]{2,1,0:T(8,128)(2,1)}, u32[]{:S(2)}, u32[]{:S(2)}) collective-permute-start(bf16[4,16,2048]{2,1,0:T(8,128)(2,1)S(1)} %get-tuple-element.245), channel_id=1, source_target_pairs={{0,8},{1,9},{2,10},{3,11},{4,12},{5,13},{6,14},{7,15},{8,0},{9,1},... | collective-permute-start | bytes 786440 | tf_op jit(solution)/shard_map/ppermute | solution.py:45
  41.9 20.8 %collective-permute-start.14 = (bf16[4,16,2048]{2,1,0:T(8,128)(2,1)}, bf16[4,16,2048]{2,1,0:T(8,128)(2,1)}, u32[]{:S(2)}, u32[]{:S(2)}) collective-permute-start(bf16[4,16,2048]{2,1,0:T(8,128)(2,1)} %get-tuple-element.246), channel_id=1, source_target_pairs={{0,8},{1,9},{2,10},{3,11},{4,12},{5,13},{6,14},{7,15},{8,0},{9,1},... | collective-permute-start | bytes 786440 | tf_op jit(solution)/shard_map/ppermute | solution.py:45
  45.4 20.7 %collective-permute-start.5 = (bf16[4,16,2048]{2,1,0:T(8,128)(2,1)}, bf16[4,16,2048]{2,1,0:T(8,128)(2,1)S(1)}, u32[]{:S(2)}, u32[]{:S(2)}) collective-permute-start(bf16[4,16,2048]{2,1,0:T(8,128)(2,1)} %get-tuple-element.241), channel_id=1, source_target_pairs={{0,2},{1,3},{2,0},{3,1},{4,6},{5,7},{6,4},{7,5},{8,10},{9,11},{10,... | collective-permute-start | bytes 786440 | tf_op jit(solution)/shard_map/ppermute | solution.py:45
  62.7 13.8 %collective-permute-start.4 = (bf16[4,32,2048]{2,1,0:T(8,128)(2,1)S(1)}, bf16[4,32,2048]{2,1,0:T(8,128)(2,1)S(1)}, u32[]{:S(2)}, u32[]{:S(2)}) collective-permute-start(bf16[4,32,2048]{2,1,0:T(8,128)(2,1)S(1)} %get-tuple-element.240), channel_id=1, source_target_pairs={{0,3},{1,0},{2,1},{3,2},{4,7},{5,4},{6,5},{7,6},{8,11},{9,8},{10,9... | collective-permute-start | bytes 1572872 | tf_op jit(solution)/shard_map/ppermute | solution.py:45
  66.2 13.9 %collective-permute-start.7 = (bf16[4,32,2048]{2,1,0:T(8,128)(2,1)S(1)}, bf16[4,32,2048]{2,1,0:T(8,128)(2,1)S(1)}, u32[]{:S(2)}, u32[]{:S(2)}) collective-permute-start(bf16[4,32,2048]{2,1,0:T(8,128)(2,1)S(1)} %get-tuple-element.240), channel_id=1, source_target_pairs={{0,1},{1,2},{2,3},{3,0},{4,5},{5,6},{6,7},{7,4},{8,9},{9,10},{10,1... | collective-permute-start | bytes 1572872 | tf_op jit(solution)/shard_map/ppermute | solution.py:45
  115.2 10.5 %collective-permute-start.19 = (bf16[4,16,2048]{2,1,0:T(8,128)(2,1)S(1)}, bf16[4,16,2048]{2,1,0:T(8,128)(2,1)S(1)}, u32[]{:S(2)}, u32[]{:S(2)}) collective-permute-start(bf16[4,16,2048]{2,1,0:T(8,128)(2,1)S(1)} %get-tuple-element.232), channel_id=1, source_target_pairs={{0,8},{1,9},{2,10},{3,11},{4,12},{5,13},{6,14},{7,15},{8,0},{9,1},... | collective-permute-start | bytes 786440 | tf_op jit(solution)/shard_map/ppermute | solution.py:45
  117.1 23.6 %collective-permute-start.16 = (bf16[4,32,2048]{2,1,0:T(8,128)(2,1)S(1)}, bf16[4,32,2048]{2,1,0:T(8,128)(2,1)S(1)}, u32[]{:S(2)}, u32[]{:S(2)}) collective-permute-start(bf16[4,32,2048]{2,1,0:T(8,128)(2,1)S(1)} %bitcast.292), channel_id=1, source_target_pairs={{0,4},{1,5},{2,6},{3,7},{4,8},{5,9},{6,10},{7,11},{8,12},{9,13},{1... | collective-permute-start | bytes 1572872 | tf_op jit(solution)/shard_map/ppermute | solution.py:45
  117.1 23.9 %collective-permute-start.17 = (bf16[4,32,2048]{2,1,0:T(8,128)(2,1)S(1)}, bf16[4,32,2048]{2,1,0:T(8,128)(2,1)S(1)}, u32[]{:S(2)}, u32[]{:S(2)}) collective-permute-start(bf16[4,32,2048]{2,1,0:T(8,128)(2,1)S(1)} %bitcast.291), channel_id=1, source_target_pairs={{0,12},{1,13},{2,14},{3,15},{4,0},{5,1},{6,2},{7,3},{8,4},{9,5},{1... | collective-permute-start | bytes 1572872 | tf_op jit(solution)/shard_map/ppermute | solution.py:45
  120.8 21.8 %collective-permute-start.26 = (bf16[4,16,2048]{2,1,0:T(8,128)(2,1)S(1)}, bf16[4,16,2048]{2,1,0:T(8,128)(2,1)S(1)}, u32[]{:S(2)}, u32[]{:S(2)}) collective-permute-start(bf16[4,16,2048]{2,1,0:T(8,128)(2,1)S(1)} %get-tuple-element.237), channel_id=1, source_target_pairs={{0,2},{1,3},{2,0},{3,1},{4,6},{5,7},{6,4},{7,5},{8,10},{9,11},{10,... | collective-permute-start | bytes 786440 | tf_op jit(solution)/shard_map/ppermute | solution.py:45
  121.1 23.1 %collective-permute-start.27 = (bf16[4,16,2048]{2,1,0:T(8,128)(2,1)S(1)}, bf16[4,16,2048]{2,1,0:T(8,128)(2,1)S(1)}, u32[]{:S(2)}, u32[]{:S(2)}) collective-permute-start(bf16[4,16,2048]{2,1,0:T(8,128)(2,1)S(1)} %get-tuple-element.238), channel_id=1, source_target_pairs={{0,2},{1,3},{2,0},{3,1},{4,6},{5,7},{6,4},{7,5},{8,10},{9,11},{10,... | collective-permute-start | bytes 786440 | tf_op jit(solution)/shard_map/ppermute | solution.py:45
  125.7 19.0 %collective-permute-start.24 = (bf16[4,32,2048]{2,1,0:T(8,128)(2,1)S(1)}, bf16[4,32,2048]{2,1,0:T(8,128)(2,1)S(1)}, u32[]{:S(2)}, u32[]{:S(2)}) collective-permute-start(bf16[4,32,2048]{2,1,0:T(8,128)(2,1)S(1)} %bitcast.290), channel_id=1, source_target_pairs={{0,1},{1,2},{2,3},{3,0},{4,5},{5,6},{6,7},{7,4},{8,9},{9,10},{10,1... | collective-permute-start | bytes 1572872 | tf_op jit(solution)/shard_map/ppermute | solution.py:45
  140.7 13.0 %collective-permute-start.25 = (bf16[4,32,2048]{2,1,0:T(8,128)(2,1)S(1)}, bf16[4,32,2048]{2,1,0:T(8,128)(2,1)S(1)}, u32[]{:S(2)}, u32[]{:S(2)}) collective-permute-start(bf16[4,32,2048]{2,1,0:T(8,128)(2,1)S(1)} %bitcast.289), channel_id=1, source_target_pairs={{0,3},{1,0},{2,1},{3,2},{4,7},{5,4},{6,5},{7,6},{8,11},{9,8},{10,9... | collective-permute-start | bytes 1572872 | tf_op jit(solution)/shard_map/ppermute | solution.py:45
  141.3 15.5 %collective-permute-start.20 = (bf16[32,2048]{1,0:T(8,128)(2,1)S(1)}, bf16[32,2048]{1,0:T(8,128)(2,1)S(1)}, u32[]{:S(2)}, u32[]{:S(2)}) collective-permute-start(bf16[32,2048]{1,0:T(8,128)(2,1)S(1)} %get-tuple-element.229), channel_id=1, source_target_pairs={{0,1},{1,2},{2,3},{3,0},{4,5},{5,6},{6,7},{7,4},{8,9},{9,10},{10,1... | collective-permute-start | bytes 393224 | tf_op jit(solution)/shard_map/ppermute | solution.py:45
  142.6 17.2 %collective-permute-start.21 = (bf16[32,2048]{1,0:T(8,128)(2,1)S(1)}, bf16[32,2048]{1,0:T(8,128)(2,1)S(1)}, u32[]{:S(2)}, u32[]{:S(2)}) collective-permute-start(bf16[32,2048]{1,0:T(8,128)(2,1)S(1)} %get-tuple-element.230), channel_id=1, source_target_pairs={{0,3},{1,0},{2,1},{3,2},{4,7},{5,4},{6,5},{7,6},{8,11},{9,8},{10,9... | collective-permute-start | bytes 393224 | tf_op jit(solution)/shard_map/ppermute | solution.py:45
  144.7 12.1 %collective-permute-start.23 = (bf16[16,2048]{1,0:T(8,128)(2,1)S(1)}, bf16[16,2048]{1,0:T(8,128)(2,1)S(1)}, u32[]{:S(2)}, u32[]{:S(2)}) collective-permute-start(bf16[16,2048]{1,0:T(8,128)(2,1)S(1)} %get-tuple-element.228), channel_id=1, source_target_pairs={{0,2},{1,3},{2,0},{3,1},{4,6},{5,7},{6,4},{7,5},{8,10},{9,11},{10,... | collective-permute-start | bytes 196616 | tf_op jit(solution)/shard_map/ppermute | solution.py:45
  285.5 81.2 %all-to-all-start.1 = ((bf16[128,192,128]{2,1,0:T(8,128)(2,1)}), bf16[128,192,128]{2,1,0:T(8,128)(2,1)}, u32[]{:S(2)}, u32[]{:S(2)}) async-start(bf16[128,192,128]{2,1,0:T(8,128)(2,1)} %reshape_reshape.3), calls=%async_computation.1 | async-start | bytes 12582912 | tf_op jit(solution)/shard_map/all_to_all | solution.py:220
  (25 other events, 587.7 us)

commit v8 on v5

--- a/solution.py
+++ b/solution.py
@@ -66,8 +66,9 @@
     far = relative[2].astype(jnp.bfloat16)
     came_left = ring_shift(far[..., :cut, :], side, along_x, 1).astype(jnp.float32)
     came_right = ring_shift(far[..., cut:, :], side, along_x, -1).astype(jnp.float32)
-    rightward = jnp.concatenate([relative[1][..., :cut, :] + came_left, relative[1][..., cut:, :]], axis=-2)
-    leftward = jnp.concatenate([relative[3][..., :cut, :], relative[3][..., cut:, :] + came_right], axis=-2)
+    spare = [(0, 0)] * (relative.ndim - 3)
+    rightward = relative[1] + jnp.pad(came_left, spare + [(0, cut), (0, 0)])
+    leftward = relative[3] + jnp.pad(came_right, spare + [(cut, 0), (0, 0)])
     from_left = ring_shift(rightward.astype(jnp.bfloat16), side, along_x, 1)
     from_right = ring_shift(leftward.astype(jnp.bfloat16), side, along_x, -1)
     return relative[0] + from_left.astype(jnp.float32) + from_right.astype(jnp.float32)
@@ -217,8 +218,12 @@
     returned = lax.all_to_all(
         produced.reshape(devices, capacity * sub, lanes), ("dp", "expert"), 0, 0, tiled=True
     )
-    pieces = returned.reshape(experts, hidden_split, capacity, sub, lanes)[chosen, :, slots]
-    blended = jnp.sum(pieces.astype(jnp.float32), axis=1) * expert_mix.reshape(-1)[:, None, None]
+    returned = returned.reshape(devices * capacity, sub, lanes)
+    spot = chosen * (hidden_split * capacity) + slots
+    blended = returned[spot].astype(jnp.float32)
+    for block in range(1, hidden_split):
+        blended = blended + returned[spot + block * capacity].astype(jnp.float32)
+    blended = blended * expert_mix.reshape(-1)[:, None, None]
     expert_update = (
         jnp.sum(blended.reshape(tok_rows, TOP, sub, lanes), axis=1)
         .reshape(tok_rows, width)

time: 353 us -> 355 us (level)
  local copies, waits for them, and re-layouts: 49.6 us -> 54.7 us
    reduce_sum x1 -> x0, other arithmetic: 4.02 us -> none  [per_device(): jnp.sum(pieces.astype(jnp.float32), axis=1)]
    gather x1 -> x2, local copies, waits for them, and re-layouts: 9.01 us -> 10.5 us  [the longest x1 5.24 us: per_device(): blended = blended + returned[spot + block * capacity].astype(jnp.float32)]
  transfers between devices with their start and end apart: 33 -> 33, of which waited for: 9 -> 7; matrix products, arithmetic and copies ran while one was open for 6% -> 8% of each run, Pallas kernels for 0% -> 0%
where the time goes in v8:
time: 355 us; the launch traced here: 353 us
  blocking collectives  95.3 us (27%)
  waiting for transfers between devices  88.6 us (25%)
  local copies, waits for them, and re-layouts  54.7 us (15%)
  starting transfers between devices  51.8 us (15%)
  matrix products  33.7 us (9%)
  other arithmetic  25.5 us (7%)
    all_to_all x1, blocking collectives, per_device(): arrived = lax.all_to_all(outgoing, ('dp', 'expert'), 0, 0, tiled=True)  95.3 us
    all_to_all x1, waiting for transfers between devices, per_device(): lax.all_to_all(produced.reshape(devices, capacity * sub, lanes), ('dp', '...  75.4 us
    ppermute x32, starting transfers between devices, ring_shift(): return lax.ppermute(block, 'expert', pairs)  46.1 us
    ppermute x32, waiting for transfers between devices, ring_shift(): return lax.ppermute(block, 'expert', pairs)  13.1 us
    dot_general x1, matrix products, expert_block(): jnp.dot(hidden, down_weight[0], preferred_element_type=jnp.float32)  11.9 us
    another operation x1, local copies, waits for them, and re-layouts, per_device(): produced.reshape(devices, capacity * sub, lanes)  10.5 us
  transfers between devices with their start and end apart: 33, of which 7 were waited for; matrix products, arithmetic and copies ran while one was open for 8% of the time, Pallas kernels for 0%

profile of v8, /device:TPU:1, one launch (start us, length us, event | category | flops | bytes accessed | tf_op | source)
XLA Modules:
  0.0 353.0 jit_solution(7052884397128212275)
XLA Ops:
  28.8 2.7 collective-permute-start.3
  32.6 2.7 collective-permute-start.12
  37.1 2.7 collective-permute-start.4
  39.8 4.7 %collective-permute-done.13 = bf16[4,32,2048]{2,1,0:T(8,128)(2,1)S(1)} collective-permute-done((bf16[4,32,2048]{2,1,0:T(8,128)(2,1)S(1)}, bf16[4,32,2048]{2,1,0:T(8,128)(2,1)S(1)}, u32[]{:S(2)}, u32[]{:S(2)}) %collective-permute-start.13) | collective-permute-done | bytes 524320 | tf_op jit(solution)/shard_map/ppermute | solution.py:45
  53.7 2.9 collective-permute-start.7
  67.6 24.6 %while.14 = (s32[]{:T(128)}, bf16[32,32,1,128]{3,1,0,2:T(8,128)(2,1)S(1)}, s32[32]{0:T(128)S(1)}, bf16[3,2048,128]{2,1,0:T(8,128)(2,1)}, s32[3]{0:T(128)S(1)}, /...) while((s32[]{:T(128)}, ...), condition=%wide.region_7.8_spmd.clone, body=%wide.region_1.7_spmd.clone.sunk | while | flops 555074688 | bytes 15133611 | solution.py:174
  96.0 2.7 collective-permute-start.18
  98.8 2.7 collective-permute-start.26
  102.7 2.7 collective-permute-start.19
  105.8 2.7 collective-permute-start.27
  108.5 5.1 %collective-permute-done.17 = bf16[4,32,2048]{2,1,0:T(8,128)(2,1)S(1)} collective-permute-done((bf16[4,32,2048]{2,1,0:T(8,128)(2,1)S(1)}, bf16[4,32,2048]{2,1,0:T(8,128)(2,1)S(1)}, u32[]{:S(2)}, u32[]{:S(2)}) %collective-permute-start.17) | collective-permute-done | bytes 524320 | tf_op jit(solution)/shard_map/ppermute | solution.py:45
  114.2 3.5 collective-permute-start.22
  118.0 2.7 collective-permute-start.30
  123.8 2.7 collective-permute-start.31
  129.3 5.8 %gather_fusion.4 = bf16[1536,16,128]{2,1,0:T(8,128)(2,1)} fusion(bf16[65,16,128]{2,1,0:T(8,128)(2,1)S(1)} %concatenate.32, s32[2048]{0:T(1024)S(1)} %pad_clamp_fusion), kind=kCustom, calls=%fused_computation.4 | custom fusion | bytes 12589056 | tf_op jit(solution)/shard_map/gather | solution.py:213
  135.1 95.3 %all_to_all.10 = bf16[128,192,128]{2,1,0:T(8,128)(2,1)S(1)} all-to-all(bf16[128,192,128]{2,1,0:T(8,128)(2,1)} %bitcast.280), channel_id=1, replica_groups=mesh['dp'=8,'expert'=16] {'dp','expert'}, dimensions={0} | all-to-all | bytes 12582912 | tf_op jit(solution)/shard_map/all_to_all | solution.py:214
  230.4 5.1 %fusion.45 = f32[1536,512]{1,0:T(8,128)} fusion(bf16[16,128,512]{2,1,0:T(8,128)(2,1)S(1)} %bitcast.316, bf16[1536,16,128]{2,1,0:T(8,128)(2,1)S(1)} %bitcast.281), kind=kOutput, calls=%fused_computation.53 | convolution fusion | flops 3221225472 | bytes 11534336 | tf_op jit(solution)/shard_map/dot_general | solution.py:29
  235.5 11.9 %convolution_convert_fusion = bf16[1536,2048]{1,0:T(8,128)(2,1)} fusion(bf16[1,512,2048]{2,1,0:T(8,128)(2,1)} %param.35, bf16[16,128,512]{2,1,0:T(8,128)(2,1)S(1)} %bitcast.279, bf16[1536,16,128]{2,1,0:T(8,128)(2,1)} %bitcast.282, f32[1536,512]{1,0:T(8,128)} %fusion.45), kind=kOutput, calls=%fused_computation.46 | convolution fusion | flops 6450315264 | bytes 19922944 | tf_op jit(solution)/shard_map/dot_general | solution.py:32
  247.4 10.5 %reshape_reshape.3 = bf16[128,192,128]{2,1,0:T(8,128)(2,1)} reshape(bf16[1536,2048]{1,0:T(8,128)(2,1)} %convolution_convert_fusion) | data formatting | bytes 12582912 | tf_op jit(solution)/shard_map/reshape;reshape | solution.py:219
  257.8 5.7 %all-to-all-start.1 = ((bf16[128,192,128]{2,1,0:T(8,128)(2,1)}), bf16[128,192,128]{2,1,0:T(8,128)(2,1)}, u32[]{:S(2)}, u32[]{:S(2)}) async-start(bf16[128,192,128]{2,1,0:T(8,128)(2,1)} %reshape_reshape.3), calls=%async_computation.1 | async-start | bytes 12582912 | tf_op jit(solution)/shard_map/all_to_all | solution.py:218
  263.6 75.4 %all-to-all-done.1 = bf16[128,192,128]{2,1,0:T(8,128)(2,1)} async-done(((bf16[128,192,128]{2,1,0:T(8,128)(2,1)}), bf16[128,192,128]{2,1,0:T(8,128)(2,1)}, u32[]{:S(2)}, u32[]{:S(2)}) %all-to-all-start.1) | async-done | bytes 6291488 | tf_op jit(solution)/shard_map/all_to_all | solution.py:218
  339.0 5.2 %gather_fusion.5 = bf16[512,16,128]{2,1,0:T(8,128)(2,1)} fusion(bf16[1536,16,128]{2,1,0:T(8,128)(2,1)} %bitcast.66, s32[1024]{0:T(1024)S(1)} %get-tuple-element.257), kind=kCustom, calls=%fused_computation.5 | custom fusion | bytes 4196352 | tf_op jit(solution)/shard_map/gather | solution.py:223
  344.3 5.2 %gather_fusion.6 = bf16[512,16,128]{2,1,0:T(8,128)(2,1)} fusion(bf16[1536,16,128]{2,1,0:T(8,128)(2,1)} %bitcast.66, s32[1024]{0:T(1024)S(1)} %get-tuple-element.256), kind=kCustom, calls=%fused_computation.6 | custom fusion | bytes 4196352 | tf_op jit(solution)/shard_map/gather | solution.py:225
  349.5 2.7 multiply_reduce_fusion
  (220 shorter events, 86.3 us)
Async XLA Ops:
  3.8 19.1 %collective-permute-start.9 = (bf16[32,2048]{1,0:T(8,128)(2,1)}, bf16[32,2048]{1,0:T(8,128)(2,1)}, u32[]{:S(2)}, u32[]{:S(2)}) collective-permute-start(bf16[32,2048]{1,0:T(8,128)(2,1)} %get-tuple-element.247), channel_id=1, source_target_pairs={{0,1},{1,2},{2,3},{3,0},{4,5},{5,6},{6,7},{7,4},{8,9},{9,10},{10,1... | collective-permute-start | bytes 393224 | tf_op jit(solution)/shard_map/ppermute | solution.py:45
  5.9 17.8 %collective-permute-start.8 = (bf16[32,2048]{1,0:T(8,128)(2,1)}, bf16[32,2048]{1,0:T(8,128)(2,1)}, u32[]{:S(2)}, u32[]{:S(2)}) collective-permute-start(bf16[32,2048]{1,0:T(8,128)(2,1)} %get-tuple-element.247), channel_id=1, source_target_pairs={{0,3},{1,0},{2,1},{3,2},{4,7},{5,4},{6,5},{7,6},{8,11},{9,8},{10,9... | collective-permute-start | bytes 393224 | tf_op jit(solution)/shard_map/ppermute | solution.py:45
  7.3 20.5 %collective-permute-start.1 = (bf16[32,2048]{1,0:T(8,128)(2,1)}, bf16[32,2048]{1,0:T(8,128)(2,1)S(1)}, u32[]{:S(2)}, u32[]{:S(2)}) collective-permute-start(bf16[32,2048]{1,0:T(8,128)(2,1)} %get-tuple-element.248), channel_id=1, source_target_pairs={{0,4},{1,5},{2,6},{3,7},{4,8},{5,9},{6,10},{7,11},{8,12},{9,13},{1... | collective-permute-start | bytes 393224 | tf_op jit(solution)/shard_map/ppermute | solution.py:45
  8.6 19.4 %collective-permute-start = (bf16[32,2048]{1,0:T(8,128)(2,1)}, bf16[32,2048]{1,0:T(8,128)(2,1)}, u32[]{:S(2)}, u32[]{:S(2)}) collective-permute-start(bf16[32,2048]{1,0:T(8,128)(2,1)} %get-tuple-element.248), channel_id=1, source_target_pairs={{0,12},{1,13},{2,14},{3,15},{4,0},{5,1},{6,2},{7,3},{8,4},{9,5},{1... | collective-permute-start | bytes 393224 | tf_op jit(solution)/shard_map/ppermute | solution.py:45
  23.7 7.7 %collective-permute-start.10 = (bf16[16,2048]{1,0:T(8,128)(2,1)S(1)}, bf16[16,2048]{1,0:T(8,128)(2,1)S(1)}, u32[]{:S(2)}, u32[]{:S(2)}) collective-permute-start(bf16[16,2048]{1,0:T(8,128)(2,1)S(1)} %slice.210), channel_id=1, source_target_pairs={{0,1},{1,2},{2,3},{3,0},{4,5},{5,6},{6,7},{7,4},{8,9},{9,10},{10,1... | collective-permute-start | bytes 196616 | tf_op jit(solution)/shard_map/ppermute | solution.py:45
  24.6 6.9 %collective-permute-start.11 = (bf16[16,2048]{1,0:T(8,128)(2,1)S(1)}, bf16[16,2048]{1,0:T(8,128)(2,1)S(1)}, u32[]{:S(2)}, u32[]{:S(2)}) collective-permute-start(bf16[16,2048]{1,0:T(8,128)(2,1)S(1)} %slice.211), channel_id=1, source_target_pairs={{0,3},{1,0},{2,1},{3,2},{4,7},{5,4},{6,5},{7,6},{8,11},{9,8},{10,9... | collective-permute-start | bytes 196616 | tf_op jit(solution)/shard_map/ppermute | solution.py:45
  27.8 7.4 %collective-permute-start.2 = (bf16[16,2048]{1,0:T(8,128)(2,1)S(1)}, bf16[16,2048]{1,0:T(8,128)(2,1)S(1)}, u32[]{:S(2)}, u32[]{:S(2)}) collective-permute-start(bf16[16,2048]{1,0:T(8,128)(2,1)S(1)} %slice.205), channel_id=1, source_target_pairs={{0,4},{1,5},{2,6},{3,7},{4,8},{5,9},{6,10},{7,11},{8,12},{9,13},{1... | collective-permute-start | bytes 196616 | tf_op jit(solution)/shard_map/ppermute | solution.py:45
  32.5 12.0 %collective-permute-start.13 = (bf16[4,32,2048]{2,1,0:T(8,128)(2,1)S(1)}, bf16[4,32,2048]{2,1,0:T(8,128)(2,1)S(1)}, u32[]{:S(2)}, u32[]{:S(2)}) collective-permute-start(bf16[4,32,2048]{2,1,0:T(8,128)(2,1)S(1)} %get-tuple-element.242), channel_id=1, source_target_pairs={{0,4},{1,5},{2,6},{3,7},{4,8},{5,9},{6,10},{7,11},{8,12},{9,13},{1... | collective-permute-start | bytes 1572872 | tf_op jit(solution)/shard_map/ppermute | solution.py:45
  32.6 12.8 %collective-permute-start.12 = (bf16[4,32,2048]{2,1,0:T(8,128)(2,1)S(1)}, bf16[4,32,2048]{2,1,0:T(8,128)(2,1)S(1)}, u32[]{:S(2)}, u32[]{:S(2)}) collective-permute-start(bf16[4,32,2048]{2,1,0:T(8,128)(2,1)S(1)} %get-tuple-element.242), channel_id=1, source_target_pairs={{0,12},{1,13},{2,14},{3,15},{4,0},{5,1},{6,2},{7,3},{8,4},{9,5},{1... | collective-permute-start | bytes 1572872 | tf_op jit(solution)/shard_map/ppermute | solution.py:45
  37.1 14.6 %collective-permute-start.5 = (bf16[4,32,2048]{2,1,0:T(8,128)(2,1)}, bf16[4,32,2048]{2,1,0:T(8,128)(2,1)}, u32[]{:S(2)}, u32[]{:S(2)}) collective-permute-start(bf16[4,32,2048]{2,1,0:T(8,128)(2,1)} %get-tuple-element.240), channel_id=1, source_target_pairs={{0,1},{1,2},{2,3},{3,0},{4,5},{5,6},{6,7},{7,4},{8,9},{9,10},{10,1... | collective-permute-start | bytes 1572872 | tf_op jit(solution)/shard_map/ppermute | solution.py:45
  37.1 15.6 %collective-permute-start.4 = (bf16[4,32,2048]{2,1,0:T(8,128)(2,1)}, bf16[4,32,2048]{2,1,0:T(8,128)(2,1)}, u32[]{:S(2)}, u32[]{:S(2)}) collective-permute-start(bf16[4,32,2048]{2,1,0:T(8,128)(2,1)} %get-tuple-element.240), channel_id=1, source_target_pairs={{0,3},{1,0},{2,1},{3,2},{4,7},{5,4},{6,5},{7,6},{8,11},{9,8},{10,9... | collective-permute-start | bytes 1572872 | tf_op jit(solution)/shard_map/ppermute | solution.py:45
  45.3 11.2 %collective-permute-start.14 = (bf16[4,16,2048]{2,1,0:T(8,128)(2,1)S(1)}, bf16[4,16,2048]{2,1,0:T(8,128)(2,1)}, u32[]{:S(2)}, u32[]{:S(2)}) collective-permute-start(bf16[4,16,2048]{2,1,0:T(8,128)(2,1)S(1)} %slice.212), channel_id=1, source_target_pairs={{0,4},{1,5},{2,6},{3,7},{4,8},{5,9},{6,10},{7,11},{8,12},{9,13},{1... | collective-permute-start | bytes 786440 | tf_op jit(solution)/shard_map/ppermute | solution.py:45
  47.0 9.6 %collective-permute-start.15 = (bf16[4,16,2048]{2,1,0:T(8,128)(2,1)}, bf16[4,16,2048]{2,1,0:T(8,128)(2,1)}, u32[]{:S(2)}, u32[]{:S(2)}) collective-permute-start(bf16[4,16,2048]{2,1,0:T(8,128)(2,1)} %slice.213), channel_id=1, source_target_pairs={{0,12},{1,13},{2,14},{3,15},{4,0},{5,1},{6,2},{7,3},{8,4},{9,5},{1... | collective-permute-start | bytes 786440 | tf_op jit(solution)/shard_map/ppermute | solution.py:45
  52.6 7.7 %collective-permute-start.6 = (bf16[4,16,2048]{2,1,0:T(8,128)(2,1)S(1)}, bf16[4,16,2048]{2,1,0:T(8,128)(2,1)S(1)}, u32[]{:S(2)}, u32[]{:S(2)}) collective-permute-start(bf16[4,16,2048]{2,1,0:T(8,128)(2,1)S(1)} %slice.207), channel_id=1, source_target_pairs={{0,1},{1,2},{2,3},{3,0},{4,5},{5,6},{6,7},{7,4},{8,9},{9,10},{10,1... | collective-permute-start | bytes 786440 | tf_op jit(solution)/shard_map/ppermute | solution.py:45
  53.7 6.7 %collective-permute-start.7 = (bf16[4,16,2048]{2,1,0:T(8,128)(2,1)S(1)}, bf16[4,16,2048]{2,1,0:T(8,128)(2,1)S(1)}, u32[]{:S(2)}, u32[]{:S(2)}) collective-permute-start(bf16[4,16,2048]{2,1,0:T(8,128)(2,1)S(1)} %slice.208), channel_id=1, source_target_pairs={{0,3},{1,0},{2,1},{3,2},{4,7},{5,4},{6,5},{7,6},{8,11},{9,8},{10,9... | collective-permute-start | bytes 786440 | tf_op jit(solution)/shard_map/ppermute | solution.py:45
  96.0 6.6 %collective-permute-start.18 = (bf16[4,16,2048]{2,1,0:T(8,128)(2,1)S(1)}, bf16[4,16,2048]{2,1,0:T(8,128)(2,1)S(1)}, u32[]{:S(2)}, u32[]{:S(2)}) collective-permute-start(bf16[4,16,2048]{2,1,0:T(8,128)(2,1)S(1)} %get-tuple-element.234), channel_id=1, source_target_pairs={{0,12},{1,13},{2,14},{3,15},{4,0},{5,1},{6,2},{7,3},{8,4},{9,5},{1... | collective-permute-start | bytes 786440 | tf_op jit(solution)/shard_map/ppermute | solution.py:45
  98.7 6.8 %collective-permute-start.24 = (bf16[4,16,2048]{2,1,0:T(8,128)(2,1)S(1)}, bf16[4,16,2048]{2,1,0:T(8,128)(2,1)S(1)}, u32[]{:S(2)}, u32[]{:S(2)}) collective-permute-start(bf16[4,16,2048]{2,1,0:T(8,128)(2,1)S(1)} %get-tuple-element.237), channel_id=1, source_target_pairs={{0,1},{1,2},{2,3},{3,0},{4,5},{5,6},{6,7},{7,4},{8,9},{9,10},{10,1... | collective-permute-start | bytes 786440 | tf_op jit(solution)/shard_map/ppermute | solution.py:45
  98.8 6.9 %collective-permute-start.26 = (bf16[4,16,2048]{2,1,0:T(8,128)(2,1)S(1)}, bf16[4,16,2048]{2,1,0:T(8,128)(2,1)S(1)}, u32[]{:S(2)}, u32[]{:S(2)}) collective-permute-start(bf16[4,16,2048]{2,1,0:T(8,128)(2,1)S(1)} %get-tuple-element.238), channel_id=1, source_target_pairs={{0,3},{1,0},{2,1},{3,2},{4,7},{5,4},{6,5},{7,6},{8,11},{9,8},{10,9... | collective-permute-start | bytes 786440 | tf_op jit(solution)/shard_map/ppermute | solution.py:45
  102.5 11.1 %collective-permute-start.17 = (bf16[4,32,2048]{2,1,0:T(8,128)(2,1)S(1)}, bf16[4,32,2048]{2,1,0:T(8,128)(2,1)S(1)}, u32[]{:S(2)}, u32[]{:S(2)}) collective-permute-start(bf16[4,32,2048]{2,1,0:T(8,128)(2,1)S(1)} %add_convert_fusion.3), channel_id=1, source_target_pairs={{0,4},{1,5},{2,6},{3,7},{4,8},{5,9},{6,10},{7,11},{8,12},{9,13},{1... | collective-permute-start | bytes 1572872 | tf_op jit(solution)/shard_map/ppermute | solution.py:45
  102.7 10.9 %collective-permute-start.19 = (bf16[4,32,2048]{2,1,0:T(8,128)(2,1)S(1)}, bf16[4,32,2048]{2,1,0:T(8,128)(2,1)S(1)}, u32[]{:S(2)}, u32[]{:S(2)}) collective-permute-start(bf16[4,32,2048]{2,1,0:T(8,128)(2,1)S(1)} %add_convert_fusion.2), channel_id=1, source_target_pairs={{0,12},{1,13},{2,14},{3,15},{4,0},{5,1},{6,2},{7,3},{8,4},{9,5},{1... | collective-permute-start | bytes 1572872 | tf_op jit(solution)/shard_map/ppermute | solution.py:45
  105.6 12.1 %collective-permute-start.25 = (bf16[4,32,2048]{2,1,0:T(8,128)(2,1)S(1)}, bf16[4,32,2048]{2,1,0:T(8,128)(2,1)S(1)}, u32[]{:S(2)}, u32[]{:S(2)}) collective-permute-start(bf16[4,32,2048]{2,1,0:T(8,128)(2,1)S(1)} %add_convert_fusion.1), channel_id=1, source_target_pairs={{0,1},{1,2},{2,3},{3,0},{4,5},{5,6},{6,7},{7,4},{8,9},{9,10},{10,1... | collective-permute-start | bytes 1572872 | tf_op jit(solution)/shard_map/ppermute | solution.py:45
  105.8 11.9 %collective-permute-start.27 = (bf16[4,32,2048]{2,1,0:T(8,128)(2,1)S(1)}, bf16[4,32,2048]{2,1,0:T(8,128)(2,1)S(1)}, u32[]{:S(2)}, u32[]{:S(2)}) collective-permute-start(bf16[4,32,2048]{2,1,0:T(8,128)(2,1)S(1)} %add_convert_fusion), channel_id=1, source_target_pairs={{0,3},{1,0},{2,1},{3,2},{4,7},{5,4},{6,5},{7,6},{8,11},{9,8},{10,9... | collective-permute-start | bytes 1572872 | tf_op jit(solution)/shard_map/ppermute | solution.py:45
  113.9 6.9 %collective-permute-start.20 = (bf16[16,2048]{1,0:T(8,128)(2,1)S(1)}, bf16[16,2048]{1,0:T(8,128)(2,1)S(1)}, u32[]{:S(2)}, u32[]{:S(2)}) collective-permute-start(bf16[16,2048]{1,0:T(8,128)(2,1)S(1)} %get-tuple-element.231), channel_id=1, source_target_pairs={{0,1},{1,2},{2,3},{3,0},{4,5},{5,6},{6,7},{7,4},{8,9},{9,10},{10,1... | collective-permute-start | bytes 196616 | tf_op jit(solution)/shard_map/ppermute | solution.py:45
  257.8 81.2 %all-to-all-start.1 = ((bf16[128,192,128]{2,1,0:T(8,128)(2,1)}), bf16[128,192,128]{2,1,0:T(8,128)(2,1)}, u32[]{:S(2)}, u32[]{:S(2)}) async-start(bf16[128,192,128]{2,1,0:T(8,128)(2,1)} %reshape_reshape.3), calls=%async_computation.1 | async-start | bytes 12582912 | tf_op jit(solution)/shard_map/all_to_all | solution.py:218
  (29 other events, 506.9 us)

commit v9 on v5

--- a/solution.py
+++ b/solution.py
@@ -143,11 +143,14 @@
             longest, heads_here, HD
         )
         scores = (
-            jnp.einsum(
-                "rihd,jhd->rhij", window_queries, group_keys, preferred_element_type=jnp.float32
-            )
+            jnp.dot(
+                window_queries.reshape(GSIZE * SB, local_width),
+                group_keys.reshape(longest, local_width).T,
+                preferred_element_type=jnp.float32,
+            ).reshape(GSIZE, SB, heads_here, longest)
             * scale
         )
+        scores = jnp.transpose(scores, (0, 2, 1, 3))
         limit = lax.dynamic_index_in_dim(prompt_length, group, 0, keepdims=False)
         scores = jnp.where(prompt_positions < limit, scores, -jnp.inf)
         window_own = lax.dynamic_slice_in_dim(own_scores, start, GSIZE, 0)
@@ -155,9 +158,11 @@
         prompt_weights = jnp.exp(scores - highest[..., None]).astype(jnp.bfloat16)
         own_weights = jnp.exp(window_own - highest[..., None]).astype(jnp.bfloat16)
         window_values = lax.dynamic_slice_in_dim(new_values, start, GSIZE, 0)
-        summed = jnp.einsum(
-            "rhij,jhd->rihd", prompt_weights, group_values, preferred_element_type=jnp.float32
-        )
+        summed = jnp.dot(
+            jnp.transpose(prompt_weights, (0, 2, 1, 3)).reshape(GSIZE * SB, longest),
+            group_values.reshape(longest, local_width),
+            preferred_element_type=jnp.float32,
+        ).reshape(GSIZE, SB, heads_here, HD)
         summed = summed + jnp.einsum(
             "rhij,rjhd->rihd", own_weights, window_values, preferred_element_type=jnp.float32
         )

time: 353 us -> 358 us (1.014)
  matrix products: 34.8 us -> 38.5 us
    dot_general x3, matrix products: 0.79 us -> 5.49 us  [group_step(): jnp.einsum('rhij,rjhd->rihd', own_weights, window_values, preferred_eleme...]
where the time goes in v9:
time: 358 us; the launch traced here: 357 us
  blocking collectives  95.4 us (27%)
  waiting for transfers between devices  89.1 us (25%)
  starting transfers between devices  53 us (15%)
  local copies, waits for them, and re-layouts  51.6 us (14%)
  matrix products  38.5 us (11%)
  other arithmetic  26.2 us (7%)
    all_to_all x1, blocking collectives, per_device(): arrived = lax.all_to_all(outgoing, ('dp', 'expert'), 0, 0, tiled=True)  95.4 us
    all_to_all x1, waiting for transfers between devices, per_device(): lax.all_to_all(produced.reshape(devices, capacity * sub, lanes), ('dp', '...  75.4 us
    ppermute x32, starting transfers between devices, ring_shift(): return lax.ppermute(block, 'expert', pairs)  47.1 us
    ppermute x32, waiting for transfers between devices, ring_shift(): return lax.ppermute(block, 'expert', pairs)  13.6 us
    dot_general x1, matrix products, expert_block(): jnp.dot(hidden, down_weight[0], preferred_element_type=jnp.float32)  11.9 us
    another operation x1, local copies, waits for them, and re-layouts, per_device(): produced.reshape(devices, capacity * sub, lanes)  10.5 us
    gather x1, local copies, waits for them, and re-layouts, per_device(): returned.reshape(experts, hidden_split, capacity, sub, lanes)  9.03 us
  transfers between devices with their start and end apart: 33, of which 9 were waited for; matrix products, arithmetic and copies ran while one was open for 6% of the time, Pallas kernels for 0%

profile of v9, /device:TPU:1, one launch (start us, length us, event | category | flops | bytes accessed | tf_op | source)
XLA Modules:
  0.0 357.1 jit_solution(7087261115091199222)
XLA Ops:
  24.3 2.7 collective-permute-start.3
  28.1 2.7 collective-permute-start.12
  31.7 2.7 collective-permute-start.4
  35.1 5.1 %collective-permute-done.13 = bf16[4,32,2048]{2,1,0:T(8,128)(2,1)S(1)} collective-permute-done((bf16[4,32,2048]{2,1,0:T(8,128)(2,1)S(1)}, bf16[4,32,2048]{2,1,0:T(8,128)(2,1)S(1)}, u32[]{:S(2)}, u32[]{:S(2)}) %collective-permute-start.13) | collective-permute-done | bytes 524320 | tf_op jit(solution)/shard_map/ppermute | solution.py:45
  42.6 2.7 collective-permute-start.15
  49.5 2.9 collective-permute-start.7
  64.1 29.6 %while.14 = (s32[]{:T(128)}, bf16[32,32,1,128]{3,1,0,2:T(8,128)(2,1)}, s32[32]{0:T(128)S(1)}, s32[3]{0:T(128)S(1)}, bf16[32,32,1,128]{3,1,0,2:T(8,128)(2,1)S(1)}...) while((s32[]{:T(128)}, ...), condition=%wide.region_7.8_spmd.clone, body=%wide.region_1.7_spmd.clone.sunk | while | flops 555074688 | bytes 16176579 | solution.py:178
  98.5 2.7 collective-permute-start.18
  101.4 3.2 collective-permute-start.26
  105.2 2.7 collective-permute-start.19
  108.8 2.9 collective-permute-start.27
  111.8 4.6 %collective-permute-done.17 = bf16[4,32,2048]{2,1,0:T(8,128)(2,1)S(1)} collective-permute-done((bf16[4,32,2048]{2,1,0:T(8,128)(2,1)S(1)}, bf16[4,32,2048]{2,1,0:T(8,128)(2,1)S(1)}, u32[]{:S(2)}, u32[]{:S(2)}) %collective-permute-start.17) | collective-permute-done | bytes 524320 | tf_op jit(solution)/shard_map/ppermute | solution.py:45
  116.7 3.5 collective-permute-start.22
  120.7 2.7 collective-permute-start.30
  126.8 2.7 collective-permute-start.31
  132.3 5.8 %gather_fusion.4 = bf16[1536,16,128]{2,1,0:T(8,128)(2,1)} fusion(bf16[65,16,128]{2,1,0:T(8,128)(2,1)S(1)} %concatenate.75, s32[2048]{0:T(1024)S(1)} %pad_clamp_fusion), kind=kCustom, calls=%fused_computation.4 | custom fusion | bytes 12589056 | tf_op jit(solution)/shard_map/gather | solution.py:217
  138.1 95.4 %all_to_all.10 = bf16[128,192,128]{2,1,0:T(8,128)(2,1)S(1)} all-to-all(bf16[128,192,128]{2,1,0:T(8,128)(2,1)} %bitcast.234), channel_id=1, replica_groups=mesh['dp'=8,'expert'=16] {'dp','expert'}, dimensions={0} | all-to-all | bytes 12582912 | tf_op jit(solution)/shard_map/all_to_all | solution.py:218
  233.5 5.1 %fusion.28 = f32[1536,512]{1,0:T(8,128)} fusion(bf16[16,128,512]{2,1,0:T(8,128)(2,1)S(1)} %bitcast.273, bf16[1536,16,128]{2,1,0:T(8,128)(2,1)S(1)} %bitcast.235), kind=kOutput, calls=%fused_computation.48 | convolution fusion | flops 3221225472 | bytes 11534336 | tf_op jit(solution)/shard_map/dot_general | solution.py:29
  238.6 11.9 %convolution_convert_fusion = bf16[1536,2048]{1,0:T(8,128)(2,1)} fusion(bf16[1,512,2048]{2,1,0:T(8,128)(2,1)} %param.35, bf16[16,128,512]{2,1,0:T(8,128)(2,1)S(1)} %bitcast.232, bf16[1536,16,128]{2,1,0:T(8,128)(2,1)} %bitcast.236, f32[1536,512]{1,0:T(8,128)} %fusion.28), kind=kOutput, calls=%fused_computation.42 | convolution fusion | flops 6450315264 | bytes 19922944 | tf_op jit(solution)/shard_map/dot_general | solution.py:32
  250.5 10.5 %reshape_reshape.3 = bf16[128,192,128]{2,1,0:T(8,128)(2,1)} reshape(bf16[1536,2048]{1,0:T(8,128)(2,1)} %convolution_convert_fusion) | data formatting | bytes 12582912 | tf_op jit(solution)/shard_map/reshape;reshape | solution.py:223
  261.0 5.9 %all-to-all-start.1 = ((bf16[128,192,128]{2,1,0:T(8,128)(2,1)}), bf16[128,192,128]{2,1,0:T(8,128)(2,1)}, u32[]{:S(2)}, u32[]{:S(2)}) async-start(bf16[128,192,128]{2,1,0:T(8,128)(2,1)} %reshape_reshape.3), calls=%async_computation.1 | async-start | bytes 12582912 | tf_op jit(solution)/shard_map/all_to_all | solution.py:222
  267.0 75.4 %all-to-all-done.1 = bf16[128,192,128]{2,1,0:T(8,128)(2,1)} async-done(((bf16[128,192,128]{2,1,0:T(8,128)(2,1)}), bf16[128,192,128]{2,1,0:T(8,128)(2,1)}, u32[]{:S(2)}, u32[]{:S(2)}) %all-to-all-start.1) | async-done | bytes 6291488 | tf_op jit(solution)/shard_map/all_to_all | solution.py:222
  342.4 9.0 %gather_fusion.5 = bf16[512,2,16,128]{3,2,1,0:T(8,128)(2,1)} fusion(bf16[64,2,12,16,128]{4,3,2,1,0:T(8,128)(2,1)} %bitcast.70, s32[512]{0:T(512)S(1)} %bitcast.233), kind=kCustom, calls=%fused_computation.5 | custom fusion | bytes 8392704 | tf_op jit(solution)/shard_map/gather | solution.py:225
  351.5 4.0 %convert_reduce_fusion.2 = f32[512,16,128]{2,1,0:T(8,128)S(1)} fusion(bf16[512,2,16,128]{3,2,1,0:T(8,128)(2,1)} %gather_fusion.5), kind=kLoop, calls=%fused_computation.41 | loop fusion | flops 3145728 | bytes 8388608 | tf_op jit(solution)/shard_map/reduce_sum | solution.py:226
  (225 shorter events, 86.8 us)
Async XLA Ops:
  3.8 16.8 %collective-permute-start.9 = (bf16[32,2048]{1,0:T(8,128)(2,1)}, bf16[32,2048]{1,0:T(8,128)(2,1)S(1)}, u32[]{:S(2)}, u32[]{:S(2)}) collective-permute-start(bf16[32,2048]{1,0:T(8,128)(2,1)} %get-tuple-element.251), channel_id=1, source_target_pairs={{0,1},{1,2},{2,3},{3,0},{4,5},{5,6},{6,7},{7,4},{8,9},{9,10},{10,1... | collective-permute-start | bytes 393224 | tf_op jit(solution)/shard_map/ppermute | solution.py:45
  5.9 14.8 %collective-permute-start.8 = (bf16[32,2048]{1,0:T(8,128)(2,1)}, bf16[32,2048]{1,0:T(8,128)(2,1)}, u32[]{:S(2)}, u32[]{:S(2)}) collective-permute-start(bf16[32,2048]{1,0:T(8,128)(2,1)} %get-tuple-element.251), channel_id=1, source_target_pairs={{0,3},{1,0},{2,1},{3,2},{4,7},{5,4},{6,5},{7,6},{8,11},{9,8},{10,9... | collective-permute-start | bytes 393224 | tf_op jit(solution)/shard_map/ppermute | solution.py:45
  7.3 16.9 %collective-permute-start.1 = (bf16[32,2048]{1,0:T(8,128)(2,1)}, bf16[32,2048]{1,0:T(8,128)(2,1)S(1)}, u32[]{:S(2)}, u32[]{:S(2)}) collective-permute-start(bf16[32,2048]{1,0:T(8,128)(2,1)} %get-tuple-element.252), channel_id=1, source_target_pairs={{0,4},{1,5},{2,6},{3,7},{4,8},{5,9},{6,10},{7,11},{8,12},{9,13},{1... | collective-permute-start | bytes 393224 | tf_op jit(solution)/shard_map/ppermute | solution.py:45
  8.5 15.7 %collective-permute-start = (bf16[32,2048]{1,0:T(8,128)(2,1)}, bf16[32,2048]{1,0:T(8,128)(2,1)S(1)}, u32[]{:S(2)}, u32[]{:S(2)}) collective-permute-start(bf16[32,2048]{1,0:T(8,128)(2,1)} %get-tuple-element.252), channel_id=1, source_target_pairs={{0,12},{1,13},{2,14},{3,15},{4,0},{5,1},{6,2},{7,3},{8,4},{9,5},{1... | collective-permute-start | bytes 393224 | tf_op jit(solution)/shard_map/ppermute | solution.py:45
  24.2 6.6 %collective-permute-start.2 = (bf16[16,2048]{1,0:T(8,128)(2,1)S(1)}, bf16[16,2048]{1,0:T(8,128)(2,1)S(1)}, u32[]{:S(2)}, u32[]{:S(2)}) collective-permute-start(bf16[16,2048]{1,0:T(8,128)(2,1)S(1)} %slice.311), channel_id=1, source_target_pairs={{0,4},{1,5},{2,6},{3,7},{4,8},{5,9},{6,10},{7,11},{8,12},{9,13},{1... | collective-permute-start | bytes 196616 | tf_op jit(solution)/shard_map/ppermute | solution.py:45
  24.3 6.5 %collective-permute-start.3 = (bf16[16,2048]{1,0:T(8,128)(2,1)S(1)}, bf16[16,2048]{1,0:T(8,128)(2,1)S(1)}, u32[]{:S(2)}, u32[]{:S(2)}) collective-permute-start(bf16[16,2048]{1,0:T(8,128)(2,1)S(1)} %slice.312), channel_id=1, source_target_pairs={{0,12},{1,13},{2,14},{3,15},{4,0},{5,1},{6,2},{7,3},{8,4},{9,5},{1... | collective-permute-start | bytes 196616 | tf_op jit(solution)/shard_map/ppermute | solution.py:45
  28.1 12.1 %collective-permute-start.13 = (bf16[4,32,2048]{2,1,0:T(8,128)(2,1)S(1)}, bf16[4,32,2048]{2,1,0:T(8,128)(2,1)S(1)}, u32[]{:S(2)}, u32[]{:S(2)}) collective-permute-start(bf16[4,32,2048]{2,1,0:T(8,128)(2,1)S(1)} %get-tuple-element.246), channel_id=1, source_target_pairs={{0,4},{1,5},{2,6},{3,7},{4,8},{5,9},{6,10},{7,11},{8,12},{9,13},{1... | collective-permute-start | bytes 1572872 | tf_op jit(solution)/shard_map/ppermute | solution.py:45
  28.1 13.0 %collective-permute-start.12 = (bf16[4,32,2048]{2,1,0:T(8,128)(2,1)S(1)}, bf16[4,32,2048]{2,1,0:T(8,128)(2,1)S(1)}, u32[]{:S(2)}, u32[]{:S(2)}) collective-permute-start(bf16[4,32,2048]{2,1,0:T(8,128)(2,1)S(1)} %get-tuple-element.246), channel_id=1, source_target_pairs={{0,12},{1,13},{2,14},{3,15},{4,0},{5,1},{6,2},{7,3},{8,4},{9,5},{1... | collective-permute-start | bytes 1572872 | tf_op jit(solution)/shard_map/ppermute | solution.py:45
  31.7 15.6 %collective-permute-start.5 = (bf16[4,32,2048]{2,1,0:T(8,128)(2,1)}, bf16[4,32,2048]{2,1,0:T(8,128)(2,1)}, u32[]{:S(2)}, u32[]{:S(2)}) collective-permute-start(bf16[4,32,2048]{2,1,0:T(8,128)(2,1)} %get-tuple-element.244), channel_id=1, source_target_pairs={{0,1},{1,2},{2,3},{3,0},{4,5},{5,6},{6,7},{7,4},{8,9},{9,10},{10,1... | collective-permute-start | bytes 1572872 | tf_op jit(solution)/shard_map/ppermute | solution.py:45
  31.7 16.8 %collective-permute-start.4 = (bf16[4,32,2048]{2,1,0:T(8,128)(2,1)}, bf16[4,32,2048]{2,1,0:T(8,128)(2,1)}, u32[]{:S(2)}, u32[]{:S(2)}) collective-permute-start(bf16[4,32,2048]{2,1,0:T(8,128)(2,1)} %get-tuple-element.244), channel_id=1, source_target_pairs={{0,3},{1,0},{2,1},{3,2},{4,7},{5,4},{6,5},{7,6},{8,11},{9,8},{10,9... | collective-permute-start | bytes 1572872 | tf_op jit(solution)/shard_map/ppermute | solution.py:45
  41.0 11.4 %collective-permute-start.14 = (bf16[4,16,2048]{2,1,0:T(8,128)(2,1)S(1)}, bf16[4,16,2048]{2,1,0:T(8,128)(2,1)}, u32[]{:S(2)}, u32[]{:S(2)}) collective-permute-start(bf16[4,16,2048]{2,1,0:T(8,128)(2,1)S(1)} %slice.318), channel_id=1, source_target_pairs={{0,4},{1,5},{2,6},{3,7},{4,8},{5,9},{6,10},{7,11},{8,12},{9,13},{1... | collective-permute-start | bytes 786440 | tf_op jit(solution)/shard_map/ppermute | solution.py:45
  42.6 9.8 %collective-permute-start.15 = (bf16[4,16,2048]{2,1,0:T(8,128)(2,1)}, bf16[4,16,2048]{2,1,0:T(8,128)(2,1)}, u32[]{:S(2)}, u32[]{:S(2)}) collective-permute-start(bf16[4,16,2048]{2,1,0:T(8,128)(2,1)} %slice.319), channel_id=1, source_target_pairs={{0,12},{1,13},{2,14},{3,15},{4,0},{5,1},{6,2},{7,3},{8,4},{9,5},{1... | collective-permute-start | bytes 786440 | tf_op jit(solution)/shard_map/ppermute | solution.py:45
  48.4 6.6 %collective-permute-start.6 = (bf16[4,16,2048]{2,1,0:T(8,128)(2,1)S(1)}, bf16[4,16,2048]{2,1,0:T(8,128)(2,1)S(1)}, u32[]{:S(2)}, u32[]{:S(2)}) collective-permute-start(bf16[4,16,2048]{2,1,0:T(8,128)(2,1)S(1)} %slice.313), channel_id=1, source_target_pairs={{0,1},{1,2},{2,3},{3,0},{4,5},{5,6},{6,7},{7,4},{8,9},{9,10},{10,1... | collective-permute-start | bytes 786440 | tf_op jit(solution)/shard_map/ppermute | solution.py:45
  98.3 6.5 %collective-permute-start.16 = (bf16[4,16,2048]{2,1,0:T(8,128)(2,1)S(1)}, bf16[4,16,2048]{2,1,0:T(8,128)(2,1)S(1)}, u32[]{:S(2)}, u32[]{:S(2)}) collective-permute-start(bf16[4,16,2048]{2,1,0:T(8,128)(2,1)S(1)} %get-tuple-element.235), channel_id=1, source_target_pairs={{0,4},{1,5},{2,6},{3,7},{4,8},{5,9},{6,10},{7,11},{8,12},{9,13},{1... | collective-permute-start | bytes 786440 | tf_op jit(solution)/shard_map/ppermute | solution.py:45
  98.5 6.6 %collective-permute-start.18 = (bf16[4,16,2048]{2,1,0:T(8,128)(2,1)S(1)}, bf16[4,16,2048]{2,1,0:T(8,128)(2,1)S(1)}, u32[]{:S(2)}, u32[]{:S(2)}) collective-permute-start(bf16[4,16,2048]{2,1,0:T(8,128)(2,1)S(1)} %get-tuple-element.236), channel_id=1, source_target_pairs={{0,12},{1,13},{2,14},{3,15},{4,0},{5,1},{6,2},{7,3},{8,4},{9,5},{1... | collective-permute-start | bytes 786440 | tf_op jit(solution)/shard_map/ppermute | solution.py:45
  101.3 7.2 %collective-permute-start.24 = (bf16[4,16,2048]{2,1,0:T(8,128)(2,1)S(1)}, bf16[4,16,2048]{2,1,0:T(8,128)(2,1)S(1)}, u32[]{:S(2)}, u32[]{:S(2)}) collective-permute-start(bf16[4,16,2048]{2,1,0:T(8,128)(2,1)S(1)} %get-tuple-element.241), channel_id=1, source_target_pairs={{0,1},{1,2},{2,3},{3,0},{4,5},{5,6},{6,7},{7,4},{8,9},{9,10},{10,1... | collective-permute-start | bytes 786440 | tf_op jit(solution)/shard_map/ppermute | solution.py:45
  101.4 7.3 %collective-permute-start.26 = (bf16[4,16,2048]{2,1,0:T(8,128)(2,1)S(1)}, bf16[4,16,2048]{2,1,0:T(8,128)(2,1)S(1)}, u32[]{:S(2)}, u32[]{:S(2)}) collective-permute-start(bf16[4,16,2048]{2,1,0:T(8,128)(2,1)S(1)} %get-tuple-element.242), channel_id=1, source_target_pairs={{0,3},{1,0},{2,1},{3,2},{4,7},{5,4},{6,5},{7,6},{8,11},{9,8},{10,9... | collective-permute-start | bytes 786440 | tf_op jit(solution)/shard_map/ppermute | solution.py:45
  105.0 11.4 %collective-permute-start.17 = (bf16[4,32,2048]{2,1,0:T(8,128)(2,1)S(1)}, bf16[4,32,2048]{2,1,0:T(8,128)(2,1)S(1)}, u32[]{:S(2)}, u32[]{:S(2)}) collective-permute-start(bf16[4,32,2048]{2,1,0:T(8,128)(2,1)S(1)} %pad_maximum_fusion.5), channel_id=1, source_target_pairs={{0,4},{1,5},{2,6},{3,7},{4,8},{5,9},{6,10},{7,11},{8,12},{9,13},{1... | collective-permute-start | bytes 1572872 | tf_op jit(solution)/shard_map/ppermute | solution.py:45
  105.2 11.2 %collective-permute-start.19 = (bf16[4,32,2048]{2,1,0:T(8,128)(2,1)S(1)}, bf16[4,32,2048]{2,1,0:T(8,128)(2,1)S(1)}, u32[]{:S(2)}, u32[]{:S(2)}) collective-permute-start(bf16[4,32,2048]{2,1,0:T(8,128)(2,1)S(1)} %pad_maximum_fusion.6), channel_id=1, source_target_pairs={{0,12},{1,13},{2,14},{3,15},{4,0},{5,1},{6,2},{7,3},{8,4},{9,5},{1... | collective-permute-start | bytes 1572872 | tf_op jit(solution)/shard_map/ppermute | solution.py:45
  108.6 11.7 %collective-permute-start.25 = (bf16[4,32,2048]{2,1,0:T(8,128)(2,1)S(1)}, bf16[4,32,2048]{2,1,0:T(8,128)(2,1)S(1)}, u32[]{:S(2)}, u32[]{:S(2)}) collective-permute-start(bf16[4,32,2048]{2,1,0:T(8,128)(2,1)S(1)} %pad_maximum_fusion.7), channel_id=1, source_target_pairs={{0,1},{1,2},{2,3},{3,0},{4,5},{5,6},{6,7},{7,4},{8,9},{9,10},{10,1... | collective-permute-start | bytes 1572872 | tf_op jit(solution)/shard_map/ppermute | solution.py:45
  108.8 11.5 %collective-permute-start.27 = (bf16[4,32,2048]{2,1,0:T(8,128)(2,1)S(1)}, bf16[4,32,2048]{2,1,0:T(8,128)(2,1)S(1)}, u32[]{:S(2)}, u32[]{:S(2)}) collective-permute-start(bf16[4,32,2048]{2,1,0:T(8,128)(2,1)S(1)} %pad_maximum_fusion.8), channel_id=1, source_target_pairs={{0,3},{1,0},{2,1},{3,2},{4,7},{5,4},{6,5},{7,6},{8,11},{9,8},{10,9... | collective-permute-start | bytes 1572872 | tf_op jit(solution)/shard_map/ppermute | solution.py:45
  116.7 6.8 %collective-permute-start.20 = (bf16[16,2048]{1,0:T(8,128)(2,1)S(1)}, bf16[16,2048]{1,0:T(8,128)(2,1)S(1)}, u32[]{:S(2)}, u32[]{:S(2)}) collective-permute-start(bf16[16,2048]{1,0:T(8,128)(2,1)S(1)} %get-tuple-element.231), channel_id=1, source_target_pairs={{0,1},{1,2},{2,3},{3,0},{4,5},{5,6},{6,7},{7,4},{8,9},{9,10},{10,1... | collective-permute-start | bytes 196616 | tf_op jit(solution)/shard_map/ppermute | solution.py:45
  116.7 6.7 %collective-permute-start.22 = (bf16[16,2048]{1,0:T(8,128)(2,1)S(1)}, bf16[16,2048]{1,0:T(8,128)(2,1)S(1)}, u32[]{:S(2)}, u32[]{:S(2)}) collective-permute-start(bf16[16,2048]{1,0:T(8,128)(2,1)S(1)} %get-tuple-element.232), channel_id=1, source_target_pairs={{0,3},{1,0},{2,1},{3,2},{4,7},{5,4},{6,5},{7,6},{8,11},{9,8},{10,9... | collective-permute-start | bytes 196616 | tf_op jit(solution)/shard_map/ppermute | solution.py:45
  261.0 81.4 %all-to-all-start.1 = ((bf16[128,192,128]{2,1,0:T(8,128)(2,1)}), bf16[128,192,128]{2,1,0:T(8,128)(2,1)}, u32[]{:S(2)}, u32[]{:S(2)}) async-start(bf16[128,192,128]{2,1,0:T(8,128)(2,1)} %reshape_reshape.3), calls=%async_computation.1 | async-start | bytes 12582912 | tf_op jit(solution)/shard_map/all_to_all | solution.py:222
  (28 other events, 513.4 us)

commit v10 on v5

--- a/solution.py
+++ b/solution.py
@@ -45,11 +45,14 @@
     return lax.ppermute(block, "expert", pairs)
 
 
-def ring_gather(block, side, along_x):
+def ring_gather(block, side, along_x, split=True):
     assert side == 4
     from_left = ring_shift(block, side, along_x, 1)
     from_right = ring_shift(block, side, along_x, -1)
     cut = block.shape[-2] // 2
+    if not split:
+        far = ring_shift(from_left, side, along_x, 1)
+        return jnp.stack([block, from_right, far, from_left])
     far = jnp.concatenate(
         [
             ring_shift(from_left[..., :cut, :], side, along_x, 1),
@@ -60,9 +63,15 @@
     return jnp.stack([block, from_right, far, from_left])
 
 
-def ring_reduce(relative, side, along_x):
+def ring_reduce(relative, side, along_x, split=True):
     assert side == 4
     cut = relative.shape[-2] // 2
+    if not split:
+        came_left = ring_shift(relative[2].astype(jnp.bfloat16), side, along_x, 1)
+        rightward = relative[1] + came_left.astype(jnp.float32)
+        from_left = ring_shift(rightward.astype(jnp.bfloat16), side, along_x, 1)
+        from_right = ring_shift(relative[3].astype(jnp.bfloat16), side, along_x, -1)
+        return relative[0] + from_left.astype(jnp.float32) + from_right.astype(jnp.float32)
     far = relative[2].astype(jnp.bfloat16)
     came_left = ring_shift(far[..., :cut, :], side, along_x, 1).astype(jnp.float32)
     came_right = ring_shift(far[..., cut:, :], side, along_x, -1).astype(jnp.float32)
@@ -102,8 +111,8 @@
     expert_groups = lax.axis_size("expert")
     side = math.isqrt(expert_groups)
     half = tok_rows // 2
-    first = ring_gather(normed[:half], side, True)
-    second = ring_gather(normed[half:], side, False)
+    first = ring_gather(normed[:half], side, True, False)
+    second = ring_gather(normed[half:], side, False, False)
     first = ring_gather(first, side, False)
     second = ring_gather(second, side, True)
     joined = jnp.concatenate([query_weight, key_weight, value_weight], axis=1)
@@ -181,8 +190,8 @@
     second = jnp.dot(second, output_weight, preferred_element_type=jnp.float32)
     first = ring_reduce(first.reshape(side, side, half, width), side, True)
     second = ring_reduce(second.reshape(side, side, half, width), side, False)
-    first = ring_reduce(first, side, False)
-    second = ring_reduce(second, side, True)
+    first = ring_reduce(first, side, False, False)
+    second = ring_reduce(second, side, True, False)
     attention_update = jnp.concatenate([first, second], axis=0).astype(jnp.bfloat16)
     expert_input = rms_scale(
         residual_in.astype(jnp.float32) + attention_update.astype(jnp.float32), expert_gain

time: 353 us -> 346 us (0.980)
  starting transfers between devices: 53 us -> 42.6 us
  waiting for transfers between devices: 89.1 us -> 97.6 us
    ppermute x32 -> x28, starting transfers between devices: 47.1 us -> 37 us  [ring_shift(): return lax.ppermute(block, 'expert', pairs)]
    ppermute x32 -> x28, waiting for transfers between devices: 13.7 us -> 22.2 us  [ring_shift(): return lax.ppermute(block, 'expert', pairs)]
  transfers between devices with their start and end apart: 33 -> 29, of which waited for: 9 -> 12; matrix products, arithmetic and copies ran while one was open for 6% -> 6% of each run, Pallas kernels for 0% -> 0%
where the time goes in v10:
time: 346 us; the launch traced here: 345 us
  waiting for transfers between devices  97.6 us (28%)
  blocking collectives  92.8 us (27%)
  local copies, waits for them, and re-layouts  48.7 us (14%)
  starting transfers between devices  42.6 us (12%)
  matrix products  34.8 us (10%)
  other arithmetic  25 us (7%)
    all_to_all x1, blocking collectives, per_device(): arrived = lax.all_to_all(outgoing, ('dp', 'expert'), 0, 0, tiled=True)  92.8 us
    all_to_all x1, waiting for transfers between devices, per_device(): lax.all_to_all(produced.reshape(devices, capacity * sub, lanes), ('dp', '...  75.4 us
    ppermute x28, starting transfers between devices, ring_shift(): return lax.ppermute(block, 'expert', pairs)  37 us
    ppermute x28, waiting for transfers between devices, ring_shift(): return lax.ppermute(block, 'expert', pairs)  22.2 us
    dot_general x1, matrix products, expert_block(): jnp.dot(hidden, down_weight[0], preferred_element_type=jnp.float32)  11.9 us
    another operation x1, local copies, waits for them, and re-layouts, per_device(): produced.reshape(devices, capacity * sub, lanes)  10.5 us
    gather x1, local copies, waits for them, and re-layouts, per_device(): returned.reshape(experts, hidden_split, capacity, sub, lanes)  8.99 us
  transfers between devices with their start and end apart: 29, of which 12 were waited for; matrix products, arithmetic and copies ran while one was open for 6% of the time, Pallas kernels for 0%

profile of v10, /device:TPU:1, one launch (start us, length us, event | category | flops | bytes accessed | tf_op | source)
XLA Modules:
  0.0 345.0 jit_solution(12028494854441166201)
XLA Ops:
  15.3 2.4 scatter_custom_fusion
  19.7 4.4 %collective-permute-done.9 = bf16[32,2048]{1,0:T(8,128)(2,1)S(1)} collective-permute-done((bf16[32,2048]{1,0:T(8,128)(2,1)S(1)}, bf16[32,2048]{1,0:T(8,128)(2,1)S(1)}, u32[]{:S(2)}, u32[]{:S(2)}) %collective-permute-start.9) | collective-permute-done | bytes 131104 | tf_op jit(solution)/shard_map/ppermute | solution.py:45
  25.1 2.7 collective-permute-start.10
  28.7 2.7 collective-permute-start.3
  32.1 5.0 %collective-permute-done.11 = bf16[4,32,2048]{2,1,0:T(8,128)(2,1)S(1)} collective-permute-done((bf16[4,32,2048]{2,1,0:T(8,128)(2,1)S(1)}, bf16[4,32,2048]{2,1,0:T(8,128)(2,1)S(1)}, u32[]{:S(2)}, u32[]{:S(2)}) %collective-permute-start.11) | collective-permute-done | bytes 524320 | tf_op jit(solution)/shard_map/ppermute | solution.py:45
  39.5 2.7 collective-permute-start.13
  59.6 24.7 %while.14 = (s32[]{:T(128)}, bf16[32,32,1,128]{3,1,0,2:T(8,128)(2,1)S(1)}, s32[32]{0:T(128)S(1)}, bf16[3,2048,128]{2,1,0:T(8,128)(2,1)}, s32[3]{0:T(128)S(1)}, /...) while((s32[]{:T(128)}, ...), condition=%wide.region_7.8_spmd.clone, body=%wide.region_1.7_spmd.clone.sunk | while | flops 555074688 | bytes 15133611 | solution.py:182
  89.8 2.7 collective-permute-start.16
  93.5 2.5 collective-permute-start.23
  96.5 2.7 collective-permute-start.17
  100.3 2.8 collective-permute-start.24
  103.1 4.7 %collective-permute-done.15 = bf16[4,32,2048]{2,1,0:T(8,128)(2,1)S(1)} collective-permute-done((bf16[4,32,2048]{2,1,0:T(8,128)(2,1)S(1)}, bf16[4,32,2048]{2,1,0:T(8,128)(2,1)S(1)}, u32[]{:S(2)}, u32[]{:S(2)}) %collective-permute-start.15) | collective-permute-done | bytes 524320 | tf_op jit(solution)/shard_map/ppermute | solution.py:45
  108.1 3.5 %collective-permute-start.20 = (bf16[32,2048]{1,0:T(8,128)(2,1)S(1)}, bf16[32,2048]{1,0:T(8,128)(2,1)S(1)}, u32[]{:S(2)}, u32[]{:S(2)}) collective-permute-start(bf16[32,2048]{1,0:T(8,128)(2,1)S(1)} %get-tuple-element.228), channel_id=1, source_target_pairs={{0,3},{1,0},{2,1},{3,2},{4,7},{5,4},{6,5},{7,6},{8,11},{9,8},{10,9... | collective-permute-start | bytes 393224 | tf_op jit(solution)/shard_map/ppermute | solution.py:45
  112.1 2.7 collective-permute-start.27
  117.5 4.4 %collective-permute-done.19 = bf16[32,2048]{1,0:T(8,128)(2,1)S(1)} collective-permute-done((bf16[32,2048]{1,0:T(8,128)(2,1)S(1)}, bf16[32,2048]{1,0:T(8,128)(2,1)S(1)}, u32[]{:S(2)}, u32[]{:S(2)}) %collective-permute-start.19) | collective-permute-done | bytes 131104 | tf_op jit(solution)/shard_map/ppermute | solution.py:45
  123.1 5.7 %gather_fusion.4 = bf16[1536,16,128]{2,1,0:T(8,128)(2,1)} fusion(bf16[65,16,128]{2,1,0:T(8,128)(2,1)S(1)} %concatenate.47, s32[2048]{0:T(1024)S(1)} %pad_clamp_fusion), kind=kCustom, calls=%fused_computation.4 | custom fusion | bytes 12589056 | tf_op jit(solution)/shard_map/gather | solution.py:221
  128.8 92.8 %all_to_all.10 = bf16[128,192,128]{2,1,0:T(8,128)(2,1)S(1)} all-to-all(bf16[128,192,128]{2,1,0:T(8,128)(2,1)} %bitcast.266), channel_id=1, replica_groups=mesh['dp'=8,'expert'=16] {'dp','expert'}, dimensions={0} | all-to-all | bytes 12582912 | tf_op jit(solution)/shard_map/all_to_all | solution.py:222
  221.6 5.1 %fusion.45 = f32[1536,512]{1,0:T(8,128)} fusion(bf16[16,128,512]{2,1,0:T(8,128)(2,1)S(1)} %bitcast.308, bf16[1536,16,128]{2,1,0:T(8,128)(2,1)S(1)} %bitcast.267), kind=kOutput, calls=%fused_computation.52 | convolution fusion | flops 3221225472 | bytes 11534336 | tf_op jit(solution)/shard_map/dot_general | solution.py:29
  226.7 11.9 %convolution_convert_fusion = bf16[1536,2048]{1,0:T(8,128)(2,1)} fusion(bf16[1,512,2048]{2,1,0:T(8,128)(2,1)} %param.35, bf16[16,128,512]{2,1,0:T(8,128)(2,1)S(1)} %bitcast.264, bf16[1536,16,128]{2,1,0:T(8,128)(2,1)} %bitcast.268, f32[1536,512]{1,0:T(8,128)} %fusion.45), kind=kOutput, calls=%fused_computation.46 | convolution fusion | flops 6450315264 | bytes 19922944 | tf_op jit(solution)/shard_map/dot_general | solution.py:32
  238.6 10.5 %reshape_reshape.3 = bf16[128,192,128]{2,1,0:T(8,128)(2,1)} reshape(bf16[1536,2048]{1,0:T(8,128)(2,1)} %convolution_convert_fusion) | data formatting | bytes 12582912 | tf_op jit(solution)/shard_map/reshape;reshape | solution.py:227
  249.1 5.7 %all-to-all-start.1 = ((bf16[128,192,128]{2,1,0:T(8,128)(2,1)}), bf16[128,192,128]{2,1,0:T(8,128)(2,1)}, u32[]{:S(2)}, u32[]{:S(2)}) async-start(bf16[128,192,128]{2,1,0:T(8,128)(2,1)} %reshape_reshape.3), calls=%async_computation.1 | async-start | bytes 12582912 | tf_op jit(solution)/shard_map/all_to_all | solution.py:226
  254.9 75.4 %all-to-all-done.1 = bf16[128,192,128]{2,1,0:T(8,128)(2,1)} async-done(((bf16[128,192,128]{2,1,0:T(8,128)(2,1)}), bf16[128,192,128]{2,1,0:T(8,128)(2,1)}, u32[]{:S(2)}, u32[]{:S(2)}) %all-to-all-start.1) | async-done | bytes 6291488 | tf_op jit(solution)/shard_map/all_to_all | solution.py:226
  330.3 9.0 %gather_fusion.5 = bf16[512,2,16,128]{3,2,1,0:T(8,128)(2,1)} fusion(bf16[64,2,12,16,128]{4,3,2,1,0:T(8,128)(2,1)} %bitcast.64, s32[512]{0:T(512)S(1)} %bitcast.265), kind=kCustom, calls=%fused_computation.5 | custom fusion | bytes 8392704 | tf_op jit(solution)/shard_map/gather | solution.py:229
  339.3 4.0 %convert_reduce_fusion.2 = f32[512,16,128]{2,1,0:T(8,128)S(1)} fusion(bf16[512,2,16,128]{3,2,1,0:T(8,128)(2,1)} %gather_fusion.5), kind=kLoop, calls=%fused_computation.45 | loop fusion | flops 3145728 | bytes 8388608 | tf_op jit(solution)/shard_map/reduce_sum | solution.py:230
  (205 shorter events, 75.5 us)
Async XLA Ops:
  3.8 15.2 %collective-permute-start.8 = (bf16[32,2048]{1,0:T(8,128)(2,1)}, bf16[32,2048]{1,0:T(8,128)(2,1)S(1)}, u32[]{:S(2)}, u32[]{:S(2)}) collective-permute-start(bf16[32,2048]{1,0:T(8,128)(2,1)} %get-tuple-element.243), channel_id=1, source_target_pairs={{0,1},{1,2},{2,3},{3,0},{4,5},{5,6},{6,7},{7,4},{8,9},{9,10},{10,1... | collective-permute-start | bytes 393224 | tf_op jit(solution)/shard_map/ppermute | solution.py:45
  5.9 13.8 %collective-permute-start.7 = (bf16[32,2048]{1,0:T(8,128)(2,1)}, bf16[32,2048]{1,0:T(8,128)(2,1)}, u32[]{:S(2)}, u32[]{:S(2)}) collective-permute-start(bf16[32,2048]{1,0:T(8,128)(2,1)} %get-tuple-element.243), channel_id=1, source_target_pairs={{0,3},{1,0},{2,1},{3,2},{4,7},{5,4},{6,5},{7,6},{8,11},{9,8},{10,9... | collective-permute-start | bytes 393224 | tf_op jit(solution)/shard_map/ppermute | solution.py:45
  7.3 12.3 %collective-permute-start.1 = (bf16[32,2048]{1,0:T(8,128)(2,1)}, bf16[32,2048]{1,0:T(8,128)(2,1)S(1)}, u32[]{:S(2)}, u32[]{:S(2)}) collective-permute-start(bf16[32,2048]{1,0:T(8,128)(2,1)} %get-tuple-element.244), channel_id=1, source_target_pairs={{0,4},{1,5},{2,6},{3,7},{4,8},{5,9},{6,10},{7,11},{8,12},{9,13},{1... | collective-permute-start | bytes 393224 | tf_op jit(solution)/shard_map/ppermute | solution.py:45
  8.5 19.2 %collective-permute-start = (bf16[32,2048]{1,0:T(8,128)(2,1)}, bf16[32,2048]{1,0:T(8,128)(2,1)S(1)}, u32[]{:S(2)}, u32[]{:S(2)}) collective-permute-start(bf16[32,2048]{1,0:T(8,128)(2,1)} %get-tuple-element.244), channel_id=1, source_target_pairs={{0,12},{1,13},{2,14},{3,15},{4,0},{5,1},{6,2},{7,3},{8,4},{9,5},{1... | collective-permute-start | bytes 393224 | tf_op jit(solution)/shard_map/ppermute | solution.py:45
  19.7 8.1 %collective-permute-start.2 = (bf16[32,2048]{1,0:T(8,128)(2,1)S(1)}, bf16[32,2048]{1,0:T(8,128)(2,1)S(1)}, u32[]{:S(2)}, u32[]{:S(2)}) collective-permute-start(bf16[32,2048]{1,0:T(8,128)(2,1)S(1)} %collective-permute-done.1), channel_id=1, source_target_pairs={{0,4},{1,5},{2,6},{3,7},{4,8},{5,9},{6,10},{7,11},{8,12},{9,13},{1... | collective-permute-start | bytes 393224 | tf_op jit(solution)/shard_map/ppermute | solution.py:45
  25.0 12.1 %collective-permute-start.11 = (bf16[4,32,2048]{2,1,0:T(8,128)(2,1)S(1)}, bf16[4,32,2048]{2,1,0:T(8,128)(2,1)S(1)}, u32[]{:S(2)}, u32[]{:S(2)}) collective-permute-start(bf16[4,32,2048]{2,1,0:T(8,128)(2,1)S(1)} %get-tuple-element.238), channel_id=1, source_target_pairs={{0,4},{1,5},{2,6},{3,7},{4,8},{5,9},{6,10},{7,11},{8,12},{9,13},{1... | collective-permute-start | bytes 1572872 | tf_op jit(solution)/shard_map/ppermute | solution.py:45
  25.1 12.9 %collective-permute-start.10 = (bf16[4,32,2048]{2,1,0:T(8,128)(2,1)S(1)}, bf16[4,32,2048]{2,1,0:T(8,128)(2,1)S(1)}, u32[]{:S(2)}, u32[]{:S(2)}) collective-permute-start(bf16[4,32,2048]{2,1,0:T(8,128)(2,1)S(1)} %get-tuple-element.238), channel_id=1, source_target_pairs={{0,12},{1,13},{2,14},{3,15},{4,0},{5,1},{6,2},{7,3},{8,4},{9,5},{1... | collective-permute-start | bytes 1572872 | tf_op jit(solution)/shard_map/ppermute | solution.py:45
  28.7 15.6 %collective-permute-start.4 = (bf16[4,32,2048]{2,1,0:T(8,128)(2,1)}, bf16[4,32,2048]{2,1,0:T(8,128)(2,1)}, u32[]{:S(2)}, u32[]{:S(2)}) collective-permute-start(bf16[4,32,2048]{2,1,0:T(8,128)(2,1)} %get-tuple-element.236), channel_id=1, source_target_pairs={{0,1},{1,2},{2,3},{3,0},{4,5},{5,6},{6,7},{7,4},{8,9},{9,10},{10,1... | collective-permute-start | bytes 1572872 | tf_op jit(solution)/shard_map/ppermute | solution.py:45
  28.7 17.2 %collective-permute-start.3 = (bf16[4,32,2048]{2,1,0:T(8,128)(2,1)}, bf16[4,32,2048]{2,1,0:T(8,128)(2,1)}, u32[]{:S(2)}, u32[]{:S(2)}) collective-permute-start(bf16[4,32,2048]{2,1,0:T(8,128)(2,1)} %get-tuple-element.236), channel_id=1, source_target_pairs={{0,3},{1,0},{2,1},{3,2},{4,7},{5,4},{6,5},{7,6},{8,11},{9,8},{10,9... | collective-permute-start | bytes 1572872 | tf_op jit(solution)/shard_map/ppermute | solution.py:45
  37.9 11.4 %collective-permute-start.12 = (bf16[4,16,2048]{2,1,0:T(8,128)(2,1)S(1)}, bf16[4,16,2048]{2,1,0:T(8,128)(2,1)}, u32[]{:S(2)}, u32[]{:S(2)}) collective-permute-start(bf16[4,16,2048]{2,1,0:T(8,128)(2,1)S(1)} %slice.202), channel_id=1, source_target_pairs={{0,4},{1,5},{2,6},{3,7},{4,8},{5,9},{6,10},{7,11},{8,12},{9,13},{1... | collective-permute-start | bytes 786440 | tf_op jit(solution)/shard_map/ppermute | solution.py:45
  39.5 9.8 %collective-permute-start.13 = (bf16[4,16,2048]{2,1,0:T(8,128)(2,1)}, bf16[4,16,2048]{2,1,0:T(8,128)(2,1)}, u32[]{:S(2)}, u32[]{:S(2)}) collective-permute-start(bf16[4,16,2048]{2,1,0:T(8,128)(2,1)} %slice.203), channel_id=1, source_target_pairs={{0,12},{1,13},{2,14},{3,15},{4,0},{5,1},{6,2},{7,3},{8,4},{9,5},{1... | collective-permute-start | bytes 786440 | tf_op jit(solution)/shard_map/ppermute | solution.py:45
  45.3 6.6 %collective-permute-start.5 = (bf16[4,16,2048]{2,1,0:T(8,128)(2,1)S(1)}, bf16[4,16,2048]{2,1,0:T(8,128)(2,1)S(1)}, u32[]{:S(2)}, u32[]{:S(2)}) collective-permute-start(bf16[4,16,2048]{2,1,0:T(8,128)(2,1)S(1)} %slice.199), channel_id=1, source_target_pairs={{0,1},{1,2},{2,3},{3,0},{4,5},{5,6},{6,7},{7,4},{8,9},{9,10},{10,1... | collective-permute-start | bytes 786440 | tf_op jit(solution)/shard_map/ppermute | solution.py:45
  89.8 6.6 %collective-permute-start.16 = (bf16[4,16,2048]{2,1,0:T(8,128)(2,1)S(1)}, bf16[4,16,2048]{2,1,0:T(8,128)(2,1)S(1)}, u32[]{:S(2)}, u32[]{:S(2)}) collective-permute-start(bf16[4,16,2048]{2,1,0:T(8,128)(2,1)S(1)} %get-tuple-element.230), channel_id=1, source_target_pairs={{0,12},{1,13},{2,14},{3,15},{4,0},{5,1},{6,2},{7,3},{8,4},{9,5},{1... | collective-permute-start | bytes 786440 | tf_op jit(solution)/shard_map/ppermute | solution.py:45
  92.6 7.2 %collective-permute-start.21 = (bf16[4,16,2048]{2,1,0:T(8,128)(2,1)S(1)}, bf16[4,16,2048]{2,1,0:T(8,128)(2,1)S(1)}, u32[]{:S(2)}, u32[]{:S(2)}) collective-permute-start(bf16[4,16,2048]{2,1,0:T(8,128)(2,1)S(1)} %get-tuple-element.233), channel_id=1, source_target_pairs={{0,1},{1,2},{2,3},{3,0},{4,5},{5,6},{6,7},{7,4},{8,9},{9,10},{10,1... | collective-permute-start | bytes 786440 | tf_op jit(solution)/shard_map/ppermute | solution.py:45
  93.5 6.7 %collective-permute-start.23 = (bf16[4,16,2048]{2,1,0:T(8,128)(2,1)S(1)}, bf16[4,16,2048]{2,1,0:T(8,128)(2,1)S(1)}, u32[]{:S(2)}, u32[]{:S(2)}) collective-permute-start(bf16[4,16,2048]{2,1,0:T(8,128)(2,1)S(1)} %get-tuple-element.234), channel_id=1, source_target_pairs={{0,3},{1,0},{2,1},{3,2},{4,7},{5,4},{6,5},{7,6},{8,11},{9,8},{10,9... | collective-permute-start | bytes 786440 | tf_op jit(solution)/shard_map/ppermute | solution.py:45
  96.3 11.5 %collective-permute-start.15 = (bf16[4,32,2048]{2,1,0:T(8,128)(2,1)S(1)}, bf16[4,32,2048]{2,1,0:T(8,128)(2,1)S(1)}, u32[]{:S(2)}, u32[]{:S(2)}) collective-permute-start(bf16[4,32,2048]{2,1,0:T(8,128)(2,1)S(1)} %pad_maximum_fusion.5), channel_id=1, source_target_pairs={{0,4},{1,5},{2,6},{3,7},{4,8},{5,9},{6,10},{7,11},{8,12},{9,13},{1... | collective-permute-start | bytes 1572872 | tf_op jit(solution)/shard_map/ppermute | solution.py:45
  96.5 11.3 %collective-permute-start.17 = (bf16[4,32,2048]{2,1,0:T(8,128)(2,1)S(1)}, bf16[4,32,2048]{2,1,0:T(8,128)(2,1)S(1)}, u32[]{:S(2)}, u32[]{:S(2)}) collective-permute-start(bf16[4,32,2048]{2,1,0:T(8,128)(2,1)S(1)} %pad_maximum_fusion.6), channel_id=1, source_target_pairs={{0,12},{1,13},{2,14},{3,15},{4,0},{5,1},{6,2},{7,3},{8,4},{9,5},{1... | collective-permute-start | bytes 1572872 | tf_op jit(solution)/shard_map/ppermute | solution.py:45
  100.0 11.8 %collective-permute-start.22 = (bf16[4,32,2048]{2,1,0:T(8,128)(2,1)S(1)}, bf16[4,32,2048]{2,1,0:T(8,128)(2,1)S(1)}, u32[]{:S(2)}, u32[]{:S(2)}) collective-permute-start(bf16[4,32,2048]{2,1,0:T(8,128)(2,1)S(1)} %pad_maximum_fusion.7), channel_id=1, source_target_pairs={{0,1},{1,2},{2,3},{3,0},{4,5},{5,6},{6,7},{7,4},{8,9},{9,10},{10,1... | collective-permute-start | bytes 1572872 | tf_op jit(solution)/shard_map/ppermute | solution.py:45
  100.3 11.5 %collective-permute-start.24 = (bf16[4,32,2048]{2,1,0:T(8,128)(2,1)S(1)}, bf16[4,32,2048]{2,1,0:T(8,128)(2,1)S(1)}, u32[]{:S(2)}, u32[]{:S(2)}) collective-permute-start(bf16[4,32,2048]{2,1,0:T(8,128)(2,1)S(1)} %pad_maximum_fusion.8), channel_id=1, source_target_pairs={{0,3},{1,0},{2,1},{3,2},{4,7},{5,4},{6,5},{7,6},{8,11},{9,8},{10,9... | collective-permute-start | bytes 1572872 | tf_op jit(solution)/shard_map/ppermute | solution.py:45
  108.0 6.8 %collective-permute-start.18 = (bf16[32,2048]{1,0:T(8,128)(2,1)S(1)}, bf16[32,2048]{1,0:T(8,128)(2,1)S(1)}, u32[]{:S(2)}, u32[]{:S(2)}) collective-permute-start(bf16[32,2048]{1,0:T(8,128)(2,1)S(1)} %get-tuple-element.227), channel_id=1, source_target_pairs={{0,1},{1,2},{2,3},{3,0},{4,5},{5,6},{6,7},{7,4},{8,9},{9,10},{10,1... | collective-permute-start | bytes 393224 | tf_op jit(solution)/shard_map/ppermute | solution.py:45
  108.1 9.4 %collective-permute-start.20 = (bf16[32,2048]{1,0:T(8,128)(2,1)S(1)}, bf16[32,2048]{1,0:T(8,128)(2,1)S(1)}, u32[]{:S(2)}, u32[]{:S(2)}) collective-permute-start(bf16[32,2048]{1,0:T(8,128)(2,1)S(1)} %get-tuple-element.228), channel_id=1, source_target_pairs={{0,3},{1,0},{2,1},{3,2},{4,7},{5,4},{6,5},{7,6},{8,11},{9,8},{10,9... | collective-permute-start | bytes 393224 | tf_op jit(solution)/shard_map/ppermute | solution.py:45
  112.1 9.9 %collective-permute-start.27 = (bf16[32,2048]{1,0:T(8,128)(2,1)S(1)}, bf16[32,2048]{1,0:T(8,128)(2,1)S(1)}, u32[]{:S(2)}, u32[]{:S(2)}) collective-permute-start(bf16[32,2048]{1,0:T(8,128)(2,1)S(1)} %get-tuple-element.232), channel_id=1, source_target_pairs={{0,12},{1,13},{2,14},{3,15},{4,0},{5,1},{6,2},{7,3},{8,4},{9,5},{1... | collective-permute-start | bytes 393224 | tf_op jit(solution)/shard_map/ppermute | solution.py:45
  114.9 7.0 %collective-permute-start.19 = (bf16[32,2048]{1,0:T(8,128)(2,1)S(1)}, bf16[32,2048]{1,0:T(8,128)(2,1)S(1)}, u32[]{:S(2)}, u32[]{:S(2)}) collective-permute-start(bf16[32,2048]{1,0:T(8,128)(2,1)S(1)} %fusion.76), channel_id=1, source_target_pairs={{0,1},{1,2},{2,3},{3,0},{4,5},{5,6},{6,7},{7,4},{8,9},{9,10},{10,1... | collective-permute-start | bytes 393224 | tf_op jit(solution)/shard_map/ppermute | solution.py:45
  249.1 81.2 %all-to-all-start.1 = ((bf16[128,192,128]{2,1,0:T(8,128)(2,1)}), bf16[128,192,128]{2,1,0:T(8,128)(2,1)}, u32[]{:S(2)}, u32[]{:S(2)}) async-start(bf16[128,192,128]{2,1,0:T(8,128)(2,1)} %reshape_reshape.3), calls=%async_computation.1 | async-start | bytes 12582912 | tf_op jit(solution)/shard_map/all_to_all | solution.py:226
  (23 other events, 469.8 us)

commit v11 on v10

--- a/solution.py
+++ b/solution.py
@@ -45,7 +45,7 @@
     return lax.ppermute(block, "expert", pairs)
 
 
-def ring_gather(block, side, along_x, split=True):
+def ring_gather(block, side, along_x, split=True, stacked=True):
     assert side == 4
     from_left = ring_shift(block, side, along_x, 1)
     from_right = ring_shift(block, side, along_x, -1)
@@ -60,6 +60,8 @@
         ],
         axis=-2,
     )
+    if not stacked:
+        return [block, from_right, far, from_left]
     return jnp.stack([block, from_right, far, from_left])
 
 
@@ -113,13 +115,20 @@
     half = tok_rows // 2
     first = ring_gather(normed[:half], side, True, False)
     second = ring_gather(normed[half:], side, False, False)
-    first = ring_gather(first, side, False)
-    second = ring_gather(second, side, True)
     joined = jnp.concatenate([query_weight, key_weight, value_weight], axis=1)
-    first = jnp.dot(first.reshape(-1, width), joined, preferred_element_type=jnp.float32)
-    second = jnp.dot(second.reshape(-1, width), joined, preferred_element_type=jnp.float32)
-    first = jnp.swapaxes(first.astype(jnp.bfloat16).reshape(side, side, half, -1), 0, 1)
-    second = second.astype(jnp.bfloat16).reshape(side, side, half, -1)
+
+    def project(pieces):
+        return jnp.stack(
+            [
+                jnp.dot(piece.reshape(-1, width), joined, preferred_element_type=jnp.float32)
+                .astype(jnp.bfloat16)
+                .reshape(side, half, -1)
+                for piece in pieces
+            ]
+        )
+
+    first = jnp.swapaxes(project(ring_gather(first, side, False, True, False)), 0, 1)
+    second = project(ring_gather(second, side, True, True, False))
     relative = jnp.concatenate([first, second], axis=2)
     place = lax.axis_index("expert")
     offsets = jnp.arange(side, dtype=jnp.int32)

time: 346 us -> 343 us (level)
  local copies, waits for them, and re-layouts: 48.7 us -> 44 us
where the time goes in v11:
time: 343 us; the launch traced here: 342 us
  waiting for transfers between devices  99.6 us (29%)
  blocking collectives  92.5 us (27%)
  local copies, waits for them, and re-layouts  44 us (13%)
  starting transfers between devices  40.7 us (12%)
  matrix products  37.3 us (11%)
  other arithmetic  24.4 us (7%)
    all_to_all x1, blocking collectives, per_device(): arrived = lax.all_to_all(outgoing, ('dp', 'expert'), 0, 0, tiled=True)  92.5 us
    all_to_all x1, waiting for transfers between devices, per_device(): lax.all_to_all(produced.reshape(devices, capacity * sub, lanes), ('dp', '...  75.4 us
    ppermute x28, starting transfers between devices, ring_shift(): return lax.ppermute(block, 'expert', pairs)  35 us
    ppermute x28, waiting for transfers between devices, ring_shift(): return lax.ppermute(block, 'expert', pairs)  24.2 us
    dot_general x1, matrix products, expert_block(): jnp.dot(hidden, down_weight[0], preferred_element_type=jnp.float32)  11.9 us
    another operation x1, local copies, waits for them, and re-layouts, per_device(): produced.reshape(devices, capacity * sub, lanes)  10.4 us
    gather x1, local copies, waits for them, and re-layouts, per_device(): returned.reshape(experts, hidden_split, capacity, sub, lanes)  8.99 us
  transfers between devices with their start and end apart: 29, of which 12 were waited for; matrix products, arithmetic and copies ran while one was open for 6% of the time, Pallas kernels for 0%

profile of v11, /device:TPU:1, one launch (start us, length us, event | category | flops | bytes accessed | tf_op | source)
XLA Modules:
  0.0 341.9 jit_solution(10962943340795583952)
XLA Ops:
  18.3 2.6 scatter_custom_fusion
  23.8 4.6 %collective-permute-done.2 = bf16[32,2048]{1,0:T(8,128)(2,1)S(1)} collective-permute-done((bf16[32,2048]{1,0:T(8,128)(2,1)}, bf16[32,2048]{1,0:T(8,128)(2,1)S(1)}, u32[]{:S(2)}, u32[]{:S(2)}) %collective-permute-start.2) | collective-permute-done | bytes 131104 | tf_op jit(solution)/shard_map/ppermute | solution.py:45
  29.6 2.7 collective-permute-start.3
  33.4 2.7 collective-permute-start.10
  38.4 3.1 collective-permute-done.4
  41.6 2.7 collective-permute-start.6
  45.8 2.9 collective-permute-start.13
  56.8 24.7 %while.14 = (s32[]{:T(128)}, bf16[32,32,1,128]{3,1,0,2:T(8,128)(2,1)S(1)}, s32[32]{0:T(128)S(1)}, bf16[3,2048,128]{2,1,0:T(8,128)(2,1)}, s32[3]{0:T(128)S(1)}, /...) while((s32[]{:T(128)}, ...), condition=%wide.region_7.8_spmd.clone, body=%wide.region_1.7_spmd.clone.sunk | while | flops 555074688 | bytes 15133611 | solution.py:191
  87.2 3.1 collective-permute-start.16
  90.5 2.7 collective-permute-start.23
  94.3 2.7 collective-permute-start.17
  97.3 2.8 collective-permute-start.24
  100.2 5.5 %collective-permute-done.15 = bf16[4,32,2048]{2,1,0:T(8,128)(2,1)S(1)} collective-permute-done((bf16[4,32,2048]{2,1,0:T(8,128)(2,1)S(1)}, bf16[4,32,2048]{2,1,0:T(8,128)(2,1)S(1)}, u32[]{:S(2)}, u32[]{:S(2)}) %collective-permute-start.15) | collective-permute-done | bytes 524320 | tf_op jit(solution)/shard_map/ppermute | solution.py:45
  106.0 2.7 collective-permute-start.20
  115.0 4.0 %collective-permute-done.19 = bf16[32,2048]{1,0:T(8,128)(2,1)S(1)} collective-permute-done((bf16[32,2048]{1,0:T(8,128)(2,1)S(1)}, bf16[32,2048]{1,0:T(8,128)(2,1)S(1)}, u32[]{:S(2)}, u32[]{:S(2)}) %collective-permute-start.19) | collective-permute-done | bytes 131104 | tf_op jit(solution)/shard_map/ppermute | solution.py:45
  120.5 5.7 %gather_fusion.4 = bf16[1536,16,128]{2,1,0:T(8,128)(2,1)} fusion(bf16[65,16,128]{2,1,0:T(8,128)(2,1)S(1)} %concatenate.47, s32[2048]{0:T(1024)S(1)} %pad_clamp_fusion), kind=kCustom, calls=%fused_computation.4 | custom fusion | bytes 12589056 | tf_op jit(solution)/shard_map/gather | solution.py:230
  126.2 92.5 %all_to_all.10 = bf16[128,192,128]{2,1,0:T(8,128)(2,1)S(1)} all-to-all(bf16[128,192,128]{2,1,0:T(8,128)(2,1)} %bitcast.286), channel_id=1, replica_groups=mesh['dp'=8,'expert'=16] {'dp','expert'}, dimensions={0} | all-to-all | bytes 12582912 | tf_op jit(solution)/shard_map/all_to_all | solution.py:231
  218.6 5.1 %fusion.45 = f32[1536,512]{1,0:T(8,128)} fusion(bf16[16,128,512]{2,1,0:T(8,128)(2,1)S(1)} %bitcast.335, bf16[1536,16,128]{2,1,0:T(8,128)(2,1)S(1)} %bitcast.287), kind=kOutput, calls=%fused_computation.52 | convolution fusion | flops 3221225472 | bytes 11534336 | tf_op jit(solution)/shard_map/dot_general | solution.py:29
  223.7 11.9 %convolution_convert_fusion = bf16[1536,2048]{1,0:T(8,128)(2,1)} fusion(bf16[1,512,2048]{2,1,0:T(8,128)(2,1)} %param.35, bf16[16,128,512]{2,1,0:T(8,128)(2,1)S(1)} %bitcast.284, bf16[1536,16,128]{2,1,0:T(8,128)(2,1)} %bitcast.288, f32[1536,512]{1,0:T(8,128)} %fusion.45), kind=kOutput, calls=%fused_computation.46 | convolution fusion | flops 6450315264 | bytes 19922944 | tf_op jit(solution)/shard_map/dot_general | solution.py:32
  235.7 10.4 %reshape_reshape.3 = bf16[128,192,128]{2,1,0:T(8,128)(2,1)} reshape(bf16[1536,2048]{1,0:T(8,128)(2,1)} %convolution_convert_fusion) | data formatting | bytes 12582912 | tf_op jit(solution)/shard_map/reshape;reshape | solution.py:236
  246.1 5.7 %all-to-all-start.1 = ((bf16[128,192,128]{2,1,0:T(8,128)(2,1)}), bf16[128,192,128]{2,1,0:T(8,128)(2,1)}, u32[]{:S(2)}, u32[]{:S(2)}) async-start(bf16[128,192,128]{2,1,0:T(8,128)(2,1)} %reshape_reshape.3), calls=%async_computation.1 | async-start | bytes 12582912 | tf_op jit(solution)/shard_map/all_to_all | solution.py:235
  251.9 75.4 %all-to-all-done.1 = bf16[128,192,128]{2,1,0:T(8,128)(2,1)} async-done(((bf16[128,192,128]{2,1,0:T(8,128)(2,1)}), bf16[128,192,128]{2,1,0:T(8,128)(2,1)}, u32[]{:S(2)}, u32[]{:S(2)}) %all-to-all-start.1) | async-done | bytes 6291488 | tf_op jit(solution)/shard_map/all_to_all | solution.py:235
  327.3 9.0 %gather_fusion.5 = bf16[512,2,16,128]{3,2,1,0:T(8,128)(2,1)} fusion(bf16[64,2,12,16,128]{4,3,2,1,0:T(8,128)(2,1)} %bitcast.72, s32[512]{0:T(512)S(1)} %bitcast.285), kind=kCustom, calls=%fused_computation.5 | custom fusion | bytes 8392704 | tf_op jit(solution)/shard_map/gather | solution.py:238
  336.3 4.0 %convert_reduce_fusion.2 = f32[512,16,128]{2,1,0:T(8,128)S(1)} fusion(bf16[512,2,16,128]{3,2,1,0:T(8,128)(2,1)} %gather_fusion.5), kind=kLoop, calls=%fused_computation.45 | loop fusion | flops 3145728 | bytes 8388608 | tf_op jit(solution)/shard_map/reduce_sum | solution.py:239
  (200 shorter events, 73.9 us)
Async XLA Ops:
  3.8 19.3 %collective-permute-start.1 = (bf16[32,2048]{1,0:T(8,128)(2,1)}, bf16[32,2048]{1,0:T(8,128)(2,1)}, u32[]{:S(2)}, u32[]{:S(2)}) collective-permute-start(bf16[32,2048]{1,0:T(8,128)(2,1)} %get-tuple-element.240), channel_id=1, source_target_pairs={{0,4},{1,5},{2,6},{3,7},{4,8},{5,9},{6,10},{7,11},{8,12},{9,13},{1... | collective-permute-start | bytes 393224 | tf_op jit(solution)/shard_map/ppermute | solution.py:45
  5.8 18.0 %collective-permute-start = (bf16[32,2048]{1,0:T(8,128)(2,1)}, bf16[32,2048]{1,0:T(8,128)(2,1)}, u32[]{:S(2)}, u32[]{:S(2)}) collective-permute-start(bf16[32,2048]{1,0:T(8,128)(2,1)} %get-tuple-element.240), channel_id=1, source_target_pairs={{0,12},{1,13},{2,14},{3,15},{4,0},{5,1},{6,2},{7,3},{8,4},{9,5},{1... | collective-permute-start | bytes 393224 | tf_op jit(solution)/shard_map/ppermute | solution.py:45
  7.1 16.7 %collective-permute-start.8 = (bf16[32,2048]{1,0:T(8,128)(2,1)}, bf16[32,2048]{1,0:T(8,128)(2,1)}, u32[]{:S(2)}, u32[]{:S(2)}) collective-permute-start(bf16[32,2048]{1,0:T(8,128)(2,1)} %get-tuple-element.239), channel_id=1, source_target_pairs={{0,1},{1,2},{2,3},{3,0},{4,5},{5,6},{6,7},{7,4},{8,9},{9,10},{10,1... | collective-permute-start | bytes 393224 | tf_op jit(solution)/shard_map/ppermute | solution.py:45
  8.6 23.7 %collective-permute-start.7 = (bf16[32,2048]{1,0:T(8,128)(2,1)}, bf16[32,2048]{1,0:T(8,128)(2,1)}, u32[]{:S(2)}, u32[]{:S(2)}) collective-permute-start(bf16[32,2048]{1,0:T(8,128)(2,1)} %get-tuple-element.239), channel_id=1, source_target_pairs={{0,3},{1,0},{2,1},{3,2},{4,7},{5,4},{6,5},{7,6},{8,11},{9,8},{10,9... | collective-permute-start | bytes 393224 | tf_op jit(solution)/shard_map/ppermute | solution.py:45
  23.8 8.5 %collective-permute-start.9 = (bf16[32,2048]{1,0:T(8,128)(2,1)}, bf16[32,2048]{1,0:T(8,128)(2,1)S(1)}, u32[]{:S(2)}, u32[]{:S(2)}) collective-permute-start(bf16[32,2048]{1,0:T(8,128)(2,1)} %collective-permute-done.8), channel_id=1, source_target_pairs={{0,1},{1,2},{2,3},{3,0},{4,5},{5,6},{6,7},{7,4},{8,9},{9,10},{10,1... | collective-permute-start | bytes 393224 | tf_op jit(solution)/shard_map/ppermute | solution.py:45
  29.5 12.0 %collective-permute-start.4 = (bf16[4,32,2048]{2,1,0:T(8,128)(2,1)S(1)}, bf16[4,32,2048]{2,1,0:T(8,128)(2,1)S(1)}, u32[]{:S(2)}, u32[]{:S(2)}) collective-permute-start(bf16[4,32,2048]{2,1,0:T(8,128)(2,1)S(1)} %pad_maximum_fusion), channel_id=1, source_target_pairs={{0,1},{1,2},{2,3},{3,0},{4,5},{5,6},{6,7},{7,4},{8,9},{9,10},{10,1... | collective-permute-start | bytes 1572872 | tf_op jit(solution)/shard_map/ppermute | solution.py:45
  29.6 12.0 %collective-permute-start.3 = (bf16[4,32,2048]{2,1,0:T(8,128)(2,1)S(1)}, bf16[4,32,2048]{2,1,0:T(8,128)(2,1)S(1)}, u32[]{:S(2)}, u32[]{:S(2)}) collective-permute-start(bf16[4,32,2048]{2,1,0:T(8,128)(2,1)S(1)} %pad_maximum_fusion), channel_id=1, source_target_pairs={{0,3},{1,0},{2,1},{3,2},{4,7},{5,4},{6,5},{7,6},{8,11},{9,8},{10,9... | collective-permute-start | bytes 1572872 | tf_op jit(solution)/shard_map/ppermute | solution.py:45
  33.3 11.4 %collective-permute-start.11 = (bf16[4,32,2048]{2,1,0:T(8,128)(2,1)S(1)}, bf16[4,32,2048]{2,1,0:T(8,128)(2,1)S(1)}, u32[]{:S(2)}, u32[]{:S(2)}) collective-permute-start(bf16[4,32,2048]{2,1,0:T(8,128)(2,1)S(1)} %pad_maximum_fusion.2), channel_id=1, source_target_pairs={{0,4},{1,5},{2,6},{3,7},{4,8},{5,9},{6,10},{7,11},{8,12},{9,13},{1... | collective-permute-start | bytes 1572872 | tf_op jit(solution)/shard_map/ppermute | solution.py:45
  33.4 12.4 %collective-permute-start.10 = (bf16[4,32,2048]{2,1,0:T(8,128)(2,1)S(1)}, bf16[4,32,2048]{2,1,0:T(8,128)(2,1)S(1)}, u32[]{:S(2)}, u32[]{:S(2)}) collective-permute-start(bf16[4,32,2048]{2,1,0:T(8,128)(2,1)S(1)} %pad_maximum_fusion.2), channel_id=1, source_target_pairs={{0,12},{1,13},{2,14},{3,15},{4,0},{5,1},{6,2},{7,3},{8,4},{9,5},{1... | collective-permute-start | bytes 1572872 | tf_op jit(solution)/shard_map/ppermute | solution.py:45
  41.5 8.1 %collective-permute-start.5 = (bf16[4,16,2048]{2,1,0:T(8,128)(2,1)S(1)}, bf16[4,16,2048]{2,1,0:T(8,128)(2,1)S(1)}, u32[]{:S(2)}, u32[]{:S(2)}) collective-permute-start(bf16[4,16,2048]{2,1,0:T(8,128)(2,1)S(1)} %slice.199), channel_id=1, source_target_pairs={{0,1},{1,2},{2,3},{3,0},{4,5},{5,6},{6,7},{7,4},{8,9},{9,10},{10,1... | collective-permute-start | bytes 786440 | tf_op jit(solution)/shard_map/ppermute | solution.py:45
  41.6 8.0 %collective-permute-start.6 = (bf16[4,16,2048]{2,1,0:T(8,128)(2,1)S(1)}, bf16[4,16,2048]{2,1,0:T(8,128)(2,1)S(1)}, u32[]{:S(2)}, u32[]{:S(2)}) collective-permute-start(bf16[4,16,2048]{2,1,0:T(8,128)(2,1)S(1)} %slice.200), channel_id=1, source_target_pairs={{0,3},{1,0},{2,1},{3,2},{4,7},{5,4},{6,5},{7,6},{8,11},{9,8},{10,9... | collective-permute-start | bytes 786440 | tf_op jit(solution)/shard_map/ppermute | solution.py:45
  44.8 6.8 %collective-permute-start.12 = (bf16[4,16,2048]{2,1,0:T(8,128)(2,1)S(1)}, bf16[4,16,2048]{2,1,0:T(8,128)(2,1)S(1)}, u32[]{:S(2)}, u32[]{:S(2)}) collective-permute-start(bf16[4,16,2048]{2,1,0:T(8,128)(2,1)S(1)} %slice.202), channel_id=1, source_target_pairs={{0,4},{1,5},{2,6},{3,7},{4,8},{5,9},{6,10},{7,11},{8,12},{9,13},{1... | collective-permute-start | bytes 786440 | tf_op jit(solution)/shard_map/ppermute | solution.py:45
  87.0 6.9 %collective-permute-start.14 = (bf16[4,16,2048]{2,1,0:T(8,128)(2,1)S(1)}, bf16[4,16,2048]{2,1,0:T(8,128)(2,1)S(1)}, u32[]{:S(2)}, u32[]{:S(2)}) collective-permute-start(bf16[4,16,2048]{2,1,0:T(8,128)(2,1)S(1)} %get-tuple-element.229), channel_id=1, source_target_pairs={{0,4},{1,5},{2,6},{3,7},{4,8},{5,9},{6,10},{7,11},{8,12},{9,13},{1... | collective-permute-start | bytes 786440 | tf_op jit(solution)/shard_map/ppermute | solution.py:45
  87.2 7.0 %collective-permute-start.16 = (bf16[4,16,2048]{2,1,0:T(8,128)(2,1)S(1)}, bf16[4,16,2048]{2,1,0:T(8,128)(2,1)S(1)}, u32[]{:S(2)}, u32[]{:S(2)}) collective-permute-start(bf16[4,16,2048]{2,1,0:T(8,128)(2,1)S(1)} %get-tuple-element.230), channel_id=1, source_target_pairs={{0,12},{1,13},{2,14},{3,15},{4,0},{5,1},{6,2},{7,3},{8,4},{9,5},{1... | collective-permute-start | bytes 786440 | tf_op jit(solution)/shard_map/ppermute | solution.py:45
  90.4 6.6 %collective-permute-start.21 = (bf16[4,16,2048]{2,1,0:T(8,128)(2,1)S(1)}, bf16[4,16,2048]{2,1,0:T(8,128)(2,1)S(1)}, u32[]{:S(2)}, u32[]{:S(2)}) collective-permute-start(bf16[4,16,2048]{2,1,0:T(8,128)(2,1)S(1)} %get-tuple-element.233), channel_id=1, source_target_pairs={{0,1},{1,2},{2,3},{3,0},{4,5},{5,6},{6,7},{7,4},{8,9},{9,10},{10,1... | collective-permute-start | bytes 786440 | tf_op jit(solution)/shard_map/ppermute | solution.py:45
  90.5 6.7 %collective-permute-start.23 = (bf16[4,16,2048]{2,1,0:T(8,128)(2,1)S(1)}, bf16[4,16,2048]{2,1,0:T(8,128)(2,1)S(1)}, u32[]{:S(2)}, u32[]{:S(2)}) collective-permute-start(bf16[4,16,2048]{2,1,0:T(8,128)(2,1)S(1)} %get-tuple-element.234), channel_id=1, source_target_pairs={{0,3},{1,0},{2,1},{3,2},{4,7},{5,4},{6,5},{7,6},{8,11},{9,8},{10,9... | collective-permute-start | bytes 786440 | tf_op jit(solution)/shard_map/ppermute | solution.py:45
  94.1 11.6 %collective-permute-start.15 = (bf16[4,32,2048]{2,1,0:T(8,128)(2,1)S(1)}, bf16[4,32,2048]{2,1,0:T(8,128)(2,1)S(1)}, u32[]{:S(2)}, u32[]{:S(2)}) collective-permute-start(bf16[4,32,2048]{2,1,0:T(8,128)(2,1)S(1)} %pad_maximum_fusion.4), channel_id=1, source_target_pairs={{0,4},{1,5},{2,6},{3,7},{4,8},{5,9},{6,10},{7,11},{8,12},{9,13},{1... | collective-permute-start | bytes 1572872 | tf_op jit(solution)/shard_map/ppermute | solution.py:45
  94.3 11.4 %collective-permute-start.17 = (bf16[4,32,2048]{2,1,0:T(8,128)(2,1)S(1)}, bf16[4,32,2048]{2,1,0:T(8,128)(2,1)S(1)}, u32[]{:S(2)}, u32[]{:S(2)}) collective-permute-start(bf16[4,32,2048]{2,1,0:T(8,128)(2,1)S(1)} %pad_maximum_fusion.5), channel_id=1, source_target_pairs={{0,12},{1,13},{2,14},{3,15},{4,0},{5,1},{6,2},{7,3},{8,4},{9,5},{1... | collective-permute-start | bytes 1572872 | tf_op jit(solution)/shard_map/ppermute | solution.py:45
  97.1 12.1 %collective-permute-start.22 = (bf16[4,32,2048]{2,1,0:T(8,128)(2,1)S(1)}, bf16[4,32,2048]{2,1,0:T(8,128)(2,1)S(1)}, u32[]{:S(2)}, u32[]{:S(2)}) collective-permute-start(bf16[4,32,2048]{2,1,0:T(8,128)(2,1)S(1)} %pad_maximum_fusion.6), channel_id=1, source_target_pairs={{0,1},{1,2},{2,3},{3,0},{4,5},{5,6},{6,7},{7,4},{8,9},{9,10},{10,1... | collective-permute-start | bytes 1572872 | tf_op jit(solution)/shard_map/ppermute | solution.py:45
  97.3 11.9 %collective-permute-start.24 = (bf16[4,32,2048]{2,1,0:T(8,128)(2,1)S(1)}, bf16[4,32,2048]{2,1,0:T(8,128)(2,1)S(1)}, u32[]{:S(2)}, u32[]{:S(2)}) collective-permute-start(bf16[4,32,2048]{2,1,0:T(8,128)(2,1)S(1)} %pad_maximum_fusion.7), channel_id=1, source_target_pairs={{0,3},{1,0},{2,1},{3,2},{4,7},{5,4},{6,5},{7,6},{8,11},{9,8},{10,9... | collective-permute-start | bytes 1572872 | tf_op jit(solution)/shard_map/ppermute | solution.py:45
  106.0 8.9 %collective-permute-start.20 = (bf16[32,2048]{1,0:T(8,128)(2,1)S(1)}, bf16[32,2048]{1,0:T(8,128)(2,1)S(1)}, u32[]{:S(2)}, u32[]{:S(2)}) collective-permute-start(bf16[32,2048]{1,0:T(8,128)(2,1)S(1)} %get-tuple-element.228), channel_id=1, source_target_pairs={{0,3},{1,0},{2,1},{3,2},{4,7},{5,4},{6,5},{7,6},{8,11},{9,8},{10,9... | collective-permute-start | bytes 393224 | tf_op jit(solution)/shard_map/ppermute | solution.py:45
  109.7 9.4 %collective-permute-start.27 = (bf16[32,2048]{1,0:T(8,128)(2,1)S(1)}, bf16[32,2048]{1,0:T(8,128)(2,1)S(1)}, u32[]{:S(2)}, u32[]{:S(2)}) collective-permute-start(bf16[32,2048]{1,0:T(8,128)(2,1)S(1)} %get-tuple-element.232), channel_id=1, source_target_pairs={{0,12},{1,13},{2,14},{3,15},{4,0},{5,1},{6,2},{7,3},{8,4},{9,5},{1... | collective-permute-start | bytes 393224 | tf_op jit(solution)/shard_map/ppermute | solution.py:45
  112.2 6.7 %collective-permute-start.19 = (bf16[32,2048]{1,0:T(8,128)(2,1)S(1)}, bf16[32,2048]{1,0:T(8,128)(2,1)S(1)}, u32[]{:S(2)}, u32[]{:S(2)}) collective-permute-start(bf16[32,2048]{1,0:T(8,128)(2,1)S(1)} %fusion.76), channel_id=1, source_target_pairs={{0,1},{1,2},{2,3},{3,0},{4,5},{5,6},{6,7},{7,4},{8,9},{9,10},{10,1... | collective-permute-start | bytes 393224 | tf_op jit(solution)/shard_map/ppermute | solution.py:45
  246.1 81.2 %all-to-all-start.1 = ((bf16[128,192,128]{2,1,0:T(8,128)(2,1)}), bf16[128,192,128]{2,1,0:T(8,128)(2,1)}, u32[]{:S(2)}, u32[]{:S(2)}) async-start(bf16[128,192,128]{2,1,0:T(8,128)(2,1)} %reshape_reshape.3), calls=%async_computation.1 | async-start | bytes 12582912 | tf_op jit(solution)/shard_map/all_to_all | solution.py:235
  (18 other events, 445.3 us)
